TPU v7x, 32 devices: a whole 2x2x4 slice. The times are simulated.
32 devices in a mesh: seq: 4 (over y, x), fsdp: 8 (over z, core).
Axes of the slice: x: 2, y: 2, z: 4, core: 2. Of those that a mesh axis runs over, the one named last changes fastest.
Arguments:
- queries: bfloat16 [8, 2048, 2560], P('fsdp', 'seq'), may hold values from -26 to 26
- kv_cache: bfloat16 [8, 5, 4, 2, 128, 2560], P('fsdp', None, 'seq'), may hold values from -24 to 24
- block_lists: int32 [8, 16, 5], P('fsdp', 'seq'), may hold values from 0 to 19, as said below
- key_limit: int32 [8, 16], P('fsdp', 'seq'), may hold values from 800 to 2559, as said below
- out_weight: bfloat16 [2560, 2560], P('fsdp'), may hold values from -0.125 to 0.125
- gate: float32 [8, 2560], P('fsdp'), may hold values from -8 to 8
Outputs:
- branch: bfloat16 [8, 2048, 2560], P('fsdp', 'seq')
Inputs may be any that keep to these rules, and one draw needn't show every extreme that they name: `block_lists`: in every tile's list the first 2 entries are the same distinct blocks below 4 for all tiles of a clip; the other 3 entries are consecutive blocks at or above 4, the most recent blocks before the tile's own position, and the last device's last tile reads block 19. Among the window blocks listed by the tiles of one device no two have the same remainder modulo 4. key_limit[n, t] lies 128 // 4 to 127 positions after the first position of the last block in the tile's list (the tile sees that far into its own stretch).
All inputs are finite; a program needn't handle non-finite values.
Results may differ from a plain program's by a relative error of at most 0.0058.
Values may be sent and summed in bfloat16 or wider, within the bound.
No kernel may reach another device: no remote copies, remote signals or barrier semaphores. Data moves between devices by JAX's collectives and lax.ppermute only.
A program may use at most 192 MiB of HBM per device.

v0:
```python
import math

import jax
import jax.numpy as jnp
from jax import lax
from jax.sharding import PartitionSpec as P

HS = 128
NSINK = 2


def spread(block, axis, source):
    block = jnp.where(lax.axis_index(axis) == source, block, jnp.zeros_like(block))
    return lax.psum(block, axis)


def shards(queries, kv_cache, block_lists, key_limit, out_weight, gate):
    owners = lax.axis_size("seq")
    blocks = kv_cache[0, :, 0]
    block_ids = block_lists[0]
    tiles = block_ids.shape[0]
    listed = block_ids.shape[1]
    block_len = blocks.shape[2]
    width = blocks.shape[3]
    window = block_ids[:, NSINK:]
    flat_ids = window.reshape(-1)
    owner_rows = jnp.arange(owners, dtype=jnp.int32)[:, None]
    wanted = jnp.max(
        jnp.where(flat_ids[None, :] % owners == owner_rows, flat_ids[None, :], -1), axis=1
    )
    asked = lax.all_to_all(
        wanted.reshape(owners, 1), "seq", split_axis=0, concat_axis=0, tiled=True
    )[:, 0]
    asked_slot = jnp.maximum(asked, 0) // owners
    outgoing = jnp.take(blocks, asked_slot, axis=0)
    arrived = lax.all_to_all(outgoing, "seq", split_axis=0, concat_axis=0, tiled=True)
    sink_parts = []
    for sink_index in range(NSINK):
        sink_id = block_ids[0, sink_index]
        held = lax.dynamic_index_in_dim(blocks, sink_id // owners, 0, keepdims=False)
        sink_parts.append(spread(held, "seq", sink_id % owners))
    block_pool = jnp.concatenate([jnp.stack(sink_parts), arrived], axis=0)
    sink_slots = jnp.broadcast_to(jnp.arange(NSINK, dtype=jnp.int32)[None, :], (tiles, NSINK))
    slot_index = jnp.concatenate([sink_slots, NSINK + window % owners], axis=1)
    picked = jnp.take(block_pool, slot_index.reshape(-1), axis=0).reshape(
        tiles, listed, 2, block_len, width
    )
    key_rows = picked[:, :, 0].reshape(tiles, listed * block_len, width)
    value_rows = picked[:, :, 1].reshape(tiles, listed * block_len, width)
    query_rows = queries[0].reshape(tiles, block_len, width)
    position = (
        block_ids[:, :, None] * block_len + jnp.arange(block_len, dtype=jnp.int32)[None, None, :]
    ).reshape(tiles, listed * block_len)
    allowed = (position < key_limit[0][:, None])[:, None, None, :]
    group = 4
    span = group * HS
    outputs = []
    for column in range(0, width, span):
        query_part = query_rows[:, :, column : column + span].reshape(tiles, block_len, group, HS)
        key_part = key_rows[:, :, column : column + span].reshape(
            tiles, listed * block_len, group, HS
        )
        value_part = value_rows[:, :, column : column + span].reshape(
            tiles, listed * block_len, group, HS
        )
        scores = jnp.einsum(
            "tqhd,tkhd->thqk", query_part, key_part, preferred_element_type=jnp.float32
        ) / math.sqrt(HS)
        scores = jnp.where(allowed, scores, -jnp.inf)
        row_max = jnp.max(scores, axis=-1, keepdims=True)
        exponent = jnp.exp(scores - row_max)
        weights = (exponent / jnp.sum(exponent, axis=-1, keepdims=True)).astype(jnp.bfloat16)
        result = jnp.einsum(
            "thqk,tkhd->tqhd", weights, value_part, preferred_element_type=jnp.float32
        ).astype(jnp.bfloat16)
        outputs.append(result.reshape(tiles, block_len, span))
    mixed_rows = jnp.concatenate(outputs, axis=2).reshape(tiles * block_len, width)
    projected = jnp.dot(
        mixed_rows,
        lax.all_gather(out_weight, "fsdp", axis=0, tiled=True),
        preferred_element_type=jnp.float32,
    )
    return (gate[0][None, :] * projected).astype(jnp.bfloat16)[None]


def solution(mesh):
    in_specs = (
        P("fsdp", "seq", None),
        P("fsdp", None, "seq", None, None, None),
        P("fsdp", "seq", None),
        P("fsdp", "seq"),
        P("fsdp", None),
        P("fsdp", None),
    )
    out_specs = P("fsdp", "seq", None)
    return jax.shard_map(shards, mesh=mesh, in_specs=in_specs, out_specs=out_specs, check_vma=False)
```

profile of v0, /device:TPU:0, one launch (start us, length us, event | category | flops | bytes accessed | tf_op | source)
XLA Modules:
  0.0 358.4 jit_solution(13149681641799015262)
XLA Ops:
  7.4 1.4 fusion.86
  14.2 3.5 select_bitcast_fusion.1
  18.7 9.7 %all_to_all.14 = s32[4,1,1]{2,1,0:T(1,128)S(1)} all-to-all(s32[4,1,1]{2,1,0:T(1,128)S(1)} %copy.154), channel_id=1, replica_groups=mesh['seq'=4,'fsdp'=8] {'seq'}, dimensions={0} | all-to-all | bytes 32 | tf_op jit(solution)/shard_map/all_to_all | solution.py:31
  28.8 6.9 %gather_fusion = bf16[4,2,128,2560]{3,2,1,0:T(8,128)(2,1)} fusion(bf16[5,2,128,2560]{3,2,1,0:T(8,128)(2,1)} %bitcast.169, s32[1024]{0:T(1024)S(1)} %pad_clamp_fusion.1), kind=kCustom, calls=%fused_computation | custom fusion | bytes 10485776 | tf_op jit(solution)/shard_map/jit(_take)/gather | solution.py:35
  35.7 5.5 %broadcast_select_fusion.1 = bf16[4,2,128,2560]{3,2,1,0:T(8,128)(2,1)} fusion(bf16[4,2,128,2560]{3,2,1,0:T(8,128)(2,1)} %gather_fusion, pred[4]{0:T(512)(128)(4,1)S(1)} %compare_and_fusion), kind=kLoop, calls=%fused_computation.40 | loop fusion | flops 2621440 | bytes 10485764 | tf_op jit(solution)/shard_map/jit(_take)/select_n | solution.py:35
  41.2 5.3 %all-to-all-start.1 = ((bf16[4,2,128,2560]{3,2,1,0:T(8,128)(2,1)}), bf16[4,2,128,2560]{3,2,1,0:T(8,128)(2,1)}, u32[]{:S(2)}, u32[]{:S(2)}) async-start(bf16[4,2,128,2560]{3,2,1,0:T(8,128)(2,1)} %broadcast_select_fusion.1), calls=%async_computation.1 | async-start | bytes 10485760 | tf_op jit(solution)/shard_map/all_to_all | solution.py:36
  46.7 1.4 fusion.85
  48.1 2.3 copy.186
  50.3 2.0 copy.179
  52.4 2.0 copy.172
  54.4 1.0 copy.165
  55.4 1.0 copy.158
  56.7 85.5 %all-reduce.3.cloned.1.call-done = (bf16[1,2,128,2560]{3,2,1,0:T(8,128)(2,1)}, bf16[1,2,128,2560]{3,2,1,0:T(8,128)(2,1)}) async-done(((bf16[1,2,128,2560]{3,2,1,0:T(8,128)(2,1)}, bf16[1,2,128,2560]{3,2,1,0:T(8,128)(2,1)}), (bf16[1,2,128,2560]{3,2,1,0:T(8,128)(2,1)}, bf16[1,2,128,2560]{3,2,1,0:T(8,128)(2,1)})) %all-reduce.3.cloned.1.call-update) | async-done | bytes 2621456 | tf_op jit(solution)/shard_map/psum | solution.py:14
  142.2 6.9 %pad_maximum_fusion = bf16[6,2,128,2560]{3,2,1,0:T(8,128)(2,1)} fusion(bf16[4,2,128,2560]{3,2,1,0:T(8,128)(2,1)} %all-to-all-done.1, bf16[1,2,128,2560]{3,2,1,0:T(8,128)(2,1)} %get-tuple-element.5, bf16[1,2,128,2560]{3,2,1,0:T(8,128)(2,1)} %get-tuple-element.6), kind=kLoop, calls=%fused_computation.8 | loop fusion | flops 7864320 | bytes 15728640 | tf_op jit(solution)/shard_map/concatenate | solution.py:42
  149.1 13.4 %gather_fusion.1 = bf16[20,2,128,2560]{3,2,1,0:T(8,128)(2,1)} fusion(bf16[6,2,128,2560]{3,2,1,0:T(8,128)(2,1)} %pad_maximum_fusion, s32[1024]{0:T(1024)S(1)} %pad_clamp_fusion), kind=kCustom, calls=%fused_computation.1 | custom fusion | bytes 52428880 | tf_op jit(solution)/shard_map/jit(_take)/gather | solution.py:45
  162.5 18.2 %copy.155 = bf16[20,2,128,2560]{3,2,0,1:T(8,128)(2,1)} copy(bf16[20,2,128,2560]{3,2,1,0:T(8,128)(2,1)} %gather_fusion.1) | data formatting | bytes 52428800 | tf_op jit(solution)/shard_map/jit(_take)/gather | solution.py:45
  180.7 18.6 %broadcast_select_fusion = bf16[4,5,2,128,2560]{4,3,1,0,2:T(8,128)(2,1)} fusion(bf16[4,5,2,128,2560]{4,3,1,0,2:T(8,128)(2,1)} %bitcast.166, pred[4,5]{1,0:T(4,128)(4,1)S(1)} %get-tuple-element.7), kind=kLoop, calls=%fused_computation.7 | loop fusion | flops 13107200 | bytes 52428820 | tf_op jit(solution)/shard_map/jit(_take)/select_n | solution.py:45
  199.3 16.2 %fusion.82 = (bf16[4,5,1,128,2560]{4,3,1,0,2:T(8,128)(2,1)S(1)}, bf16[4,5,1,128,2560]{4,3,1,0,2:T(8,128)(2,1)}) fusion(bf16[4,5,2,128,2560]{4,3,1,0,2:T(8,128)(2,1)} %broadcast_select_fusion), kind=kLoop, calls=%fused_computation.125 | loop fusion | bytes 52428800 | tf_op jit(solution)/shard_map/slice | solution.py:48
  215.5 4.1 %fusion.83 = (bf16[4,640,512]{2,1,0:T(8,128)(2,1)}, bf16[4,640,512]{2,1,0:T(8,128)(2,1)}, bf16[4,640,512]{2,1,0:T(8,128)(2,1)}, bf16[4,640,512]{2,1,0:T(8,128)(2,1)}, bf16[4,640,512]{2,1,0:T(8,128)(2,1)S(1)}) fusion(bf16[4,640,2560]{2,1,0:T(8,128)(2,1)S(1)} %bitcast.168), kind=kLoop, calls=%fused_computation.126 | loop fusion | bytes 26214400 | tf_op jit(solution)/shard_map/slice | solution.py:60
  219.6 4.4 %copy.210 = bf16[4,640,512]{1,2,0:T(8,128)(2,1)} copy(bf16[4,640,512]{2,1,0:T(8,128)(2,1)} %get-tuple-element.11) | data formatting | bytes 5242880
  224.0 9.9 %fusion.84 = (bf16[4,640,512]{2,1,0:T(8,128)(2,1)}, bf16[4,640,512]{2,1,0:T(8,128)(2,1)}, bf16[4,640,512]{2,1,0:T(8,128)(2,1)}, bf16[4,640,512]{2,1,0:T(8,128)(2,1)}, bf16[4,640,512]{2,1,0:T(8,128)(2,1)}) fusion(bf16[4,640,2560]{2,1,0:T(8,128)(2,1)} %bitcast.167), kind=kLoop, calls=%fused_computation.127 | loop fusion | bytes 26214400 | tf_op jit(solution)/shard_map/slice | solution.py:63
  234.0 4.5 %copy.184 = bf16[4,640,512]{1,2,0:T(8,128)(2,1)} copy(bf16[4,640,512]{2,1,0:T(8,128)(2,1)} %get-tuple-element.16) | data formatting | bytes 5242880 | tf_op jit(solution)/shard_map/slice | solution.py:63
  238.5 6.2 %fusion.91 = (f32[4,4,128]{2,1,0:T(4,128)S(1)}, f32[4,4,128,640]{2,3,1,0:T(8,128)}) fusion(pred[4,640]{1,0:T(4,128)(4,1)S(1)} %fusion.66, bf16[4,640,4,128]{1,3,2,0:T(8,128)(2,1)} %bitcast.171, bf16[4,128,4,128]{1,3,2,0:T(8,128)(2,1)S(1)} %bitcast.190), kind=kOutput, calls=%fused_computation.134 | convolution fusion | flops 340787840 | bytes 8399360 | tf_op jit(solution)/shard_map/sub | solution.py:71
  244.7 4.9 %fusion.55 = bf16[4,128,4,128]{1,3,2,0:T(8,128)(2,1)} fusion(bf16[4,640,4,128]{1,3,2,0:T(8,128)(2,1)} %bitcast.174, f32[4,4,128,640]{2,3,1,0:T(8,128)} %get-tuple-element.41, f32[4,4,128]{2,1,0:T(4,128)S(1)} %get-tuple-element.40), kind=kOutput, calls=%fused_computation.73 | convolution fusion | flops 338427904 | bytes 8396800 | tf_op jit(solution)/shard_map/thqk,tkhd->tqhd/dot_general | solution.py:73
  249.6 1.3 copy.190
  251.0 4.4 %copy.209 = bf16[4,640,512]{1,2,0:T(8,128)(2,1)} copy(bf16[4,640,512]{2,1,0:T(8,128)(2,1)} %get-tuple-element.12) | data formatting | bytes 5242880
  255.4 4.4 %copy.177 = bf16[4,640,512]{1,2,0:T(8,128)(2,1)} copy(bf16[4,640,512]{2,1,0:T(8,128)(2,1)} %get-tuple-element.17) | data formatting | bytes 5242880 | tf_op jit(solution)/shard_map/slice | solution.py:63
  259.8 6.3 %fusion.90 = (f32[4,4,128]{2,1,0:T(4,128)S(1)}, f32[4,4,128,640]{2,3,1,0:T(8,128)}) fusion(pred[4,640]{1,0:T(4,128)(4,1)S(1)} %fusion.66, bf16[4,640,4,128]{1,3,2,0:T(8,128)(2,1)} %bitcast.178, bf16[4,128,4,128]{1,3,2,0:T(8,128)(2,1)} %bitcast.189), kind=kOutput, calls=%fused_computation.133 | convolution fusion | flops 340787840 | bytes 8399360 | tf_op jit(solution)/shard_map/sub | solution.py:71
  266.1 4.9 %fusion.54 = bf16[4,128,4,128]{1,3,2,0:T(8,128)(2,1)} fusion(bf16[4,640,4,128]{1,3,2,0:T(8,128)(2,1)} %bitcast.175, f32[4,4,128,640]{2,3,1,0:T(8,128)} %get-tuple-element.39, f32[4,4,128]{2,1,0:T(4,128)S(1)} %get-tuple-element.38), kind=kOutput, calls=%fused_computation.72 | convolution fusion | flops 338427904 | bytes 8396800 | tf_op jit(solution)/shard_map/thqk,tkhd->tqhd/dot_general | solution.py:73
  271.0 2.1 copy.183
  273.1 4.4 %copy.208 = bf16[4,640,512]{1,2,0:T(8,128)(2,1)} copy(bf16[4,640,512]{2,1,0:T(8,128)(2,1)} %get-tuple-element.13) | data formatting | bytes 5242880
  277.5 4.4 %copy.170 = bf16[4,640,512]{1,2,0:T(8,128)(2,1)} copy(bf16[4,640,512]{2,1,0:T(8,128)(2,1)} %get-tuple-element.18) | data formatting | bytes 5242880 | tf_op jit(solution)/shard_map/slice | solution.py:63
  281.9 6.3 %fusion.89 = (f32[4,4,128]{2,1,0:T(4,128)S(1)}, f32[4,4,128,640]{2,3,1,0:T(8,128)}) fusion(pred[4,640]{1,0:T(4,128)(4,1)S(1)} %fusion.66, bf16[4,640,4,128]{1,3,2,0:T(8,128)(2,1)} %bitcast.179, bf16[4,128,4,128]{1,3,2,0:T(8,128)(2,1)} %bitcast.188), kind=kOutput, calls=%fused_computation.132 | convolution fusion | flops 340787840 | bytes 8399360 | tf_op jit(solution)/shard_map/sub | solution.py:71
  288.2 4.9 %fusion.53 = bf16[4,128,4,128]{1,3,2,0:T(8,128)(2,1)} fusion(bf16[4,640,4,128]{1,3,2,0:T(8,128)(2,1)} %bitcast.176, f32[4,4,128,640]{2,3,1,0:T(8,128)} %get-tuple-element.37, f32[4,4,128]{2,1,0:T(4,128)S(1)} %get-tuple-element.36), kind=kOutput, calls=%fused_computation.71 | convolution fusion | flops 338427904 | bytes 8396800 | tf_op jit(solution)/shard_map/thqk,tkhd->tqhd/dot_general | solution.py:73
  293.1 2.1 copy.176
  295.3 4.4 %copy.207 = bf16[4,640,512]{1,2,0:T(8,128)(2,1)} copy(bf16[4,640,512]{2,1,0:T(8,128)(2,1)} %get-tuple-element.14) | data formatting | bytes 5242880
  299.7 4.4 %copy.163 = bf16[4,640,512]{1,2,0:T(8,128)(2,1)} copy(bf16[4,640,512]{2,1,0:T(8,128)(2,1)} %get-tuple-element.19) | data formatting | bytes 5242880 | tf_op jit(solution)/shard_map/slice | solution.py:63
  304.1 6.3 %fusion.88 = (f32[4,4,128]{2,1,0:T(4,128)S(1)}, f32[4,4,128,640]{2,3,1,0:T(8,128)}) fusion(pred[4,640]{1,0:T(4,128)(4,1)S(1)} %fusion.66, bf16[4,640,4,128]{1,3,2,0:T(8,128)(2,1)} %bitcast.180, bf16[4,128,4,128]{1,3,2,0:T(8,128)(2,1)} %bitcast.187), kind=kOutput, calls=%fused_computation.131 | convolution fusion | flops 340787840 | bytes 8399360 | tf_op jit(solution)/shard_map/sub | solution.py:71
  310.4 4.9 %fusion.52 = bf16[4,128,4,128]{1,3,2,0:T(8,128)(2,1)} fusion(bf16[4,640,4,128]{1,3,2,0:T(8,128)(2,1)} %bitcast.177, f32[4,4,128,640]{2,3,1,0:T(8,128)} %get-tuple-element.35, f32[4,4,128]{2,1,0:T(4,128)S(1)} %get-tuple-element.34), kind=kOutput, calls=%fused_computation.70 | convolution fusion | flops 338427904 | bytes 8396800 | tf_op jit(solution)/shard_map/thqk,tkhd->tqhd/dot_general | solution.py:73
  315.3 2.1 copy.169
  317.4 2.6 copy.206
  320.0 4.5 %copy.156 = bf16[4,640,512]{1,2,0:T(8,128)(2,1)} copy(bf16[4,640,512]{2,1,0:T(8,128)(2,1)} %get-tuple-element.20) | data formatting | bytes 5242880 | tf_op jit(solution)/shard_map/slice | solution.py:63
  324.5 5.5 %fusion.87 = (f32[4,4,128]{2,1,0:T(4,128)S(1)}, f32[4,4,128,640]{2,3,1,0:T(8,128)}) fusion(pred[4,640]{1,0:T(4,128)(4,1)S(1)} %fusion.66, bf16[4,640,4,128]{1,3,2,0:T(8,128)(2,1)S(1)} %bitcast.172, bf16[4,128,4,128]{1,3,2,0:T(8,128)(2,1)} %bitcast.186), kind=kOutput, calls=%fused_computation.130 | convolution fusion | flops 340787840 | bytes 8399360 | tf_op jit(solution)/shard_map/sub | solution.py:71
  330.1 4.2 %fusion.51 = bf16[4,128,4,128]{1,3,2,0:T(8,128)(2,1)S(1)} fusion(bf16[4,640,4,128]{1,3,2,0:T(8,128)(2,1)} %bitcast.173, f32[4,4,128,640]{2,3,1,0:T(8,128)} %get-tuple-element.33, f32[4,4,128]{2,1,0:T(4,128)S(1)} %get-tuple-element.32), kind=kOutput, calls=%fused_computation.69 | convolution fusion | flops 338427904 | bytes 8396800 | tf_op jit(solution)/shard_map/thqk,tkhd->tqhd/dot_general | solution.py:73
  336.4 0.9 bitcast_dynamic-update-slice_fusion.2
  337.3 1.0 bitcast_dynamic-update-slice_fusion.1
  338.2 0.9 bitcast_dynamic-update-slice_fusion
  339.2 11.8 %fusion.15 = bf16[1,512,2560]{2,1,0:T(8,128)(2,1)} fusion(bf16[512,2560]{1,0:T(8,128)(2,1)} %bitcast_dynamic-update-slice_fusion, bf16[2560,2560]{1,0:T(8,128)(2,1)} %all-gather.2.cloned.1.call-done, f32[2560]{0:T(1024)S(1)} %reduce), kind=kOutput, calls=%fused_computation.41 | convolution fusion | flops 6713507840 | bytes 18360320 | tf_op jit(solution)/shard_map/dot_general | solution.py:78
  (49 shorter events, 3.9 us)
Async XLA Ops:
  7.4 134.8 %all-reduce.3.cloned.1.call-start = ((), (), s32[]{:S(2)}) async-start(), calls=%async_computation.3 | async-start | bytes 5242880 | tf_op jit(solution)/shard_map/psum | solution.py:14
  17.7 0.7 copy-start.7
  17.7 321.5 %all-gather.2.cloned.1.call-start = ((), (), s32[]{:S(2)}) async-start(), calls=%async_computation.2 | async-start | bytes 14745600 | tf_op jit(solution)/shard_map/all_gather | solution.py:80
  41.2 5.5 %copy-start = (bf16[1,512,2560]{2,1,0:T(8,128)(2,1)S(1)}, bf16[1,512,2560]{2,1,0:T(8,128)(2,1)}, u32[]{:S(2)}) copy-start(bf16[1,512,2560]{2,1,0:T(8,128)(2,1)} %param.6) | copy-start | bytes 7864324
  41.2 101.0 %all-to-all-start.1 = ((bf16[4,2,128,2560]{3,2,1,0:T(8,128)(2,1)}), bf16[4,2,128,2560]{3,2,1,0:T(8,128)(2,1)}, u32[]{:S(2)}, u32[]{:S(2)}) async-start(bf16[4,2,128,2560]{3,2,1,0:T(8,128)(2,1)} %broadcast_select_fusion.1), calls=%async_computation.1 | async-start | bytes 10485760 | tf_op jit(solution)/shard_map/all_to_all | solution.py:36
  48.1 6.4 %copy-start.2 = (bf16[4,128,512]{2,1,0:T(8,128)(2,1)S(1)}, bf16[4,128,512]{2,1,0:T(8,128)(2,1)}, u32[]{:S(2)}) copy-start(bf16[4,128,512]{2,1,0:T(8,128)(2,1)} %get-tuple-element.26) | copy-start | bytes 1572868
  48.1 8.4 %copy-start.8 = (f32[1,2560]{1,0:T(1,128)S(1)}, f32[1,2560]{1,0:T(1,128)}, u32[]{:S(2)}) copy-start(f32[1,2560]{1,0:T(1,128)} %param.11) | copy-start | bytes 30724
  48.1 8.5 %copy-start.9 = (s32[1,4]{1,0:T(1,128)S(1)}, s32[1,4]{1,0:T(1,128)}, u32[]{:S(2)}) copy-start(s32[1,4]{1,0:T(1,128)} %param.9) | copy-start | bytes 52
  234.0 4.5 %copy-start.6 = (bf16[4,128,512]{1,2,0:T(8,128)(2,1)S(1)}, bf16[4,128,512]{1,2,0:T(8,128)(2,1)}, u32[]{:S(2)}) copy-start(bf16[4,128,512]{1,2,0:T(8,128)(2,1)} %copy.186) | copy-start | bytes 1572868
  320.0 4.5 %copy-start.1 = (bf16[4,640,512]{1,2,0:T(8,128)(2,1)S(1)}, bf16[4,640,512]{1,2,0:T(8,128)(2,1)}, u32[]{:S(2)}) copy-start(bf16[4,640,512]{1,2,0:T(8,128)(2,1)} %copy.206) | copy-start | bytes 7864324
  330.1 5.4 %copy-start.5 = (bf16[4,128,4,128]{3,2,1,0:T(4,128)(2,1)S(1)}, bf16[4,128,4,128]{3,2,1,0:T(4,128)(2,1)}, u32[]{:S(2)}) copy-start(bf16[4,128,4,128]{3,2,1,0:T(4,128)(2,1)} %copy.169) | copy-start | bytes 1572868
  334.2 2.1 copy-start.4
  334.3 3.0 copy-start.3
Sparse Core Ops, SparseCore 0:
  17.8 124.3 all-reduce.2
Sparse Core Ops, SparseCore 1:
  19.8 123.6 all-gather.1
where the time goes:
time: 360 us; the launch traced here: 358 us
  local copies, waits for them, and re-layouts  135 us (38%)
  waiting for transfers between devices  86.1 us (24%)
  matrix products  66.4 us (18%)
  other arithmetic  35.2 us (10%)
  between operations  20.4 us (6%)
  blocking collectives  9.66 us (3%)
  starting transfers between devices  5.35 us (1%)
    psum x1, waiting for transfers between devices, spread(): return lax.psum(block, axis)  85.5 us
    slice x6, local copies, waits for them, and re-layouts, shards(): value_rows[:, :, column:column + span]  32.1 us
    gather x2, local copies, waits for them, and re-layouts, shards(): jnp.take(block_pool, slot_index.reshape(-1), axis=0)  31.6 us
    sub x5, matrix products, shards(): exponent = jnp.exp(scores - row_max)  30.7 us
    unnamed x30, local copies, waits for them, and re-layouts  24.1 us
    dot_general x5, matrix products, shards(): jnp.einsum('thqk,tkhd->tqhd', weights, value_part, preferred_element_type...  23.9 us
    select_n x2, other arithmetic, shards(): jnp.take(block_pool, slot_index.reshape(-1), axis=0)  18.6 us
    slice x1, local copies, waits for them, and re-layouts, shards(): key_rows = picked[:, :, 0].reshape(tiles, listed * block_len, width)  16.2 us
  transfers between devices with their start and end apart: 3, of which 1 were waited for; matrix products, arithmetic and copies ran while one was open for 61% of the time, Pallas kernels for 0%

commit v1 on v0

v1 whole, which is shorter than its diff:
```python
import math

import jax
import jax.numpy as jnp
from jax import lax
from jax.experimental import pallas as pl
from jax.experimental.pallas import tpu as pltpu
from jax.sharding import PartitionSpec as P

HS = 128
NSINK = 2
GROUP = 4


def attention(slot_ids, block_ids, limits, query_rows, sink_pool, window_pool):
    rows, width = query_rows.shape
    block_len = sink_pool.shape[2]
    tiles, listed = block_ids.shape
    heads = width // HS
    group = GROUP if heads % GROUP == 0 else 1
    span = group * HS
    scale = math.sqrt(HS)

    def kernel(slot_ref, block_ref, limit_ref, q_ref, *refs):
        key_refs = refs[:listed]
        value_refs = refs[listed : 2 * listed]
        out_ref = refs[2 * listed]
        t = pl.program_id(1)
        limit = limit_ref[t]
        lane = lax.broadcasted_iota(jnp.int32, (1, block_len), 1)
        allowed = [block_ref[t, j] * block_len + lane < limit for j in range(listed)]
        for h in range(group):
            cols = slice(h * HS, (h + 1) * HS)
            q = q_ref[:, cols]
            scores = []
            for j in range(listed):
                s = lax.dot_general(
                    q,
                    key_refs[j][:, cols],
                    (((1,), (1,)), ((), ())),
                    preferred_element_type=jnp.float32,
                ) / scale
                scores.append(jnp.where(allowed[j], s, -jnp.inf))
            row_max = scores[0].max(axis=1, keepdims=True)
            for s in scores[1:]:
                row_max = jnp.maximum(row_max, s.max(axis=1, keepdims=True))
            exps = [jnp.exp(s - row_max) for s in scores]
            total = exps[0].sum(axis=1, keepdims=True)
            for e in exps[1:]:
                total = total + e.sum(axis=1, keepdims=True)
            acc = None
            for j in range(listed):
                w = (exps[j] / total).astype(jnp.bfloat16)
                part = jnp.dot(w, value_refs[j][:, cols], preferred_element_type=jnp.float32)
                acc = part if acc is None else acc + part
            out_ref[:, cols] = acc.astype(out_ref.dtype)

    def pool_spec(j, kv):
        def index(g, t, slot_ref, block_ref, limit_ref):
            return (slot_ref[t, j], kv, 0, g)

        return pl.BlockSpec((None, None, block_len, span), index)

    q_spec = pl.BlockSpec((block_len, span), lambda g, t, *_: (t, g))
    in_specs = [q_spec]
    operands = [query_rows]
    for kv in range(2):
        for j in range(listed):
            in_specs.append(pool_spec(j, kv))
            operands.append(sink_pool if j < NSINK else window_pool)
    grid_spec = pltpu.PrefetchScalarGridSpec(
        num_scalar_prefetch=3,
        grid=(heads // group, tiles),
        in_specs=in_specs,
        out_specs=pl.BlockSpec((block_len, span), lambda g, t, *_: (t, g)),
    )
    flops = 4 * tiles * block_len * listed * block_len * width
    cost = pl.CostEstimate(
        flops=flops,
        transcendentals=tiles * heads * block_len * listed * block_len,
        bytes_accessed=2 * rows * width * 2 + 2 * tiles * listed * block_len * width * 2,
    )
    return pl.pallas_call(
        kernel,
        grid_spec=grid_spec,
        out_shape=jax.ShapeDtypeStruct((rows, width), jnp.bfloat16),
        compiler_params=pltpu.CompilerParams(dimension_semantics=("arbitrary", "arbitrary")),
        cost_estimate=cost,
    )(slot_ids, block_ids, limits, query_rows, *operands[1:])


def shards(queries, kv_cache, block_lists, key_limit, out_weight, gate):
    owners = lax.axis_size("seq")
    me = lax.axis_index("seq")
    blocks = kv_cache[0, :, 0]
    block_ids = block_lists[0]
    tiles = block_ids.shape[0]
    block_len = blocks.shape[2]
    width = blocks.shape[3]
    weight = lax.all_gather(out_weight, "fsdp", axis=0, tiled=True)
    every_list = lax.all_gather(block_ids, "seq")
    sink_pool = lax.all_gather(blocks[0], "seq")
    readers_ids = every_list[:, :, NSINK:].reshape(owners, -1)
    asked = jnp.max(jnp.where(readers_ids % owners == me, readers_ids, -1), axis=1)
    asked_slot = jnp.maximum(asked, 0) // owners
    outgoing = jnp.take(blocks, asked_slot, axis=0)
    window_pool = lax.all_to_all(outgoing, "seq", split_axis=0, concat_axis=0, tiled=True)
    slot_ids = jnp.concatenate(
        [block_ids[:, :NSINK], block_ids[:, NSINK:] % owners], axis=1
    ).astype(jnp.int32)
    mixed = attention(
        slot_ids, block_ids, key_limit[0], queries[0], sink_pool, window_pool
    )
    projected = jnp.dot(mixed, weight, preferred_element_type=jnp.float32)
    return (gate[0][None, :] * projected).astype(jnp.bfloat16)[None]


def solution(mesh):
    in_specs = (
        P("fsdp", "seq", None),
        P("fsdp", None, "seq", None, None, None),
        P("fsdp", "seq", None),
        P("fsdp", "seq"),
        P("fsdp", None),
        P("fsdp", None),
    )
    out_specs = P("fsdp", "seq", None)
    return jax.shard_map(shards, mesh=mesh, in_specs=in_specs, out_specs=out_specs, check_vma=False)
```

time: 360 us -> 264 us (0.73)
  local copies, waits for them, and re-layouts: 135 us -> 9.15 us
  waiting for transfers between devices: 86.1 us -> 157 us
  matrix products: 66.4 us -> 11.8 us
  Pallas kernels: 0 us -> 51 us
  other arithmetic: 35.2 us -> 6.37 us
  between operations: 20.4 us -> 13.4 us
    psum x1 -> x0, waiting for transfers between devices: 85.5 us -> none  [spread(): return lax.psum(block, axis)]
    all_to_all x1, waiting for transfers between devices: 0.01 us -> 84.4 us  [shards(): lax.all_to_all(outgoing, 'seq', split_axis=0, concat_axis=0, tiled=True)]
    all_gather x1 -> x2, waiting for transfers between devices: 0.01 us -> 72.1 us  [the longest x1 72 us: shards(): weight = lax.all_gather(out_weight, 'fsdp', axis=0, tiled=True)]
    slice x15 -> x1, local copies, waits for them, and re-layouts: 63.6 us -> 2.47 us  [shards(): sink_pool = lax.all_gather(blocks[0], 'seq')]
    pallas_call x0 -> x1, Pallas kernels: none -> 51 us  [attention(): pl.pallas_call(kernel, grid_spec=grid_spec, out_shape=jax.ShapeDtypeStruc...]
    gather x2 -> x0, local copies, waits for them, and re-layouts: 31.6 us -> none  [shards(): jnp.take(block_pool, slot_index.reshape(-1), axis=0)]
    sub x5 -> x0, matrix products: 30.7 us -> none  [shards(): exponent = jnp.exp(scores - row_max)]
    unnamed x30 -> x4, local copies, waits for them, and re-layouts: 24.1 us -> 0.01 us
  transfers between devices with their start and end apart: 3 -> 3, of which waited for: 1 -> 3; matrix products, arithmetic and copies ran while one was open for 61% -> 5% of each run, Pallas kernels for 0% -> 19%
where the time goes in v1:
time: 264 us
  waiting for transfers between devices  157 us (59%)
  Pallas kernels  51 us (19%)
  between operations  13.4 us (5%)
  matrix products  11.8 us (4%)
  blocking collectives  9.57 us (4%)
  local copies, waits for them, and re-layouts  9.15 us (3%)
  other arithmetic  6.37 us (2%)
  starting transfers between devices  5.22 us (2%)
    all_to_all x1, waiting for transfers between devices, shards(): lax.all_to_all(outgoing, 'seq', split_axis=0, concat_axis=0, tiled=True)  84.4 us
    all_gather x1, waiting for transfers between devices, shards(): weight = lax.all_gather(out_weight, 'fsdp', axis=0, tiled=True)  72 us
    pallas_call x1, Pallas kernels, attention(): pl.pallas_call(kernel, grid_spec=grid_spec, out_shape=jax.ShapeDtypeStruc...  51 us
    dot_general x1, matrix products, shards(): projected = jnp.dot(mixed, weight, preferred_element_type=jnp.float32)  11.8 us
    all_gather x1, blocking collectives, shards(): every_list = lax.all_gather(block_ids, 'seq')  9.57 us
    gather x1, local copies, waits for them, and re-layouts, shards(): outgoing = jnp.take(blocks, asked_slot, axis=0)  6.68 us
    select_n x2, other arithmetic, shards(): outgoing = jnp.take(blocks, asked_slot, axis=0)  5.39 us
  transfers between devices with their start and end apart: 3, of which 3 were waited for; matrix products, arithmetic and copies ran while one was open for 5% of the time, Pallas kernels for 19%

profile of v1, /device:TPU:0, one launch (start us, length us, event | category | flops | bytes accessed | tf_op | source)
XLA Modules:
  0.0 263.8 jit_solution(13551953268075574187)
XLA Ops:
  6.5 0.0 copy-start
  6.5 0.0 all-gather.6.cloned.1.call-start
  6.5 2.5 slice.17
  9.0 0.0 all-gather.6.cloned.1.call-update
  9.0 0.0 all-gather.4.cloned.1.call-start
  9.1 0.7 all-gather.4.cloned.1.call-update
  9.8 0.0 copy-done
  9.8 9.6 %all_gather.10 = s32[4,4,5]{2,1,0:T(4,128)S(1)} all-gather(s32[1,4,5]{2,1,0:T(4,128)S(1)} %copy-done), channel_id=1, replica_groups=mesh['seq'=4,'fsdp'=8] {'seq'}, dimensions={0}, use_global_device_ids=true | all-gather | bytes 400 | tf_op jit(solution)/shard_map/all_gather | solution.py:101
  19.4 0.2 select_reduce_fusion
  19.6 6.7 %gather_fusion = bf16[4,2,128,2560]{3,2,1,0:T(8,128)(2,1)} fusion(bf16[5,2,128,2560]{3,2,1,0:T(8,128)(2,1)} %bitcast.26, s32[1024]{0:T(1024)S(1)} %pad_clamp_fusion), kind=kCustom, calls=%fused_computation | custom fusion | bytes 10485776 | tf_op jit(solution)/shard_map/jit(_take)/gather | solution.py:106
  26.3 5.4 %broadcast_select_fusion = bf16[4,2,128,2560]{3,2,1,0:T(8,128)(2,1)} fusion(bf16[4,2,128,2560]{3,2,1,0:T(8,128)(2,1)} %gather_fusion, pred[4]{0:T(512)(128)(4,1)S(1)} %compare_and_fusion), kind=kLoop, calls=%fused_computation.2 | loop fusion | flops 2621440 | bytes 10485764 | tf_op jit(solution)/shard_map/jit(_take)/select_n | solution.py:106
  31.7 0.0 copy-start.1
  31.7 5.2 %all-to-all-start = ((bf16[4,2,128,2560]{3,2,1,0:T(8,128)(2,1)}), bf16[4,2,128,2560]{3,2,1,0:T(8,128)(2,1)}, u32[]{:S(2)}, u32[]{:S(2)}) async-start(bf16[4,2,128,2560]{3,2,1,0:T(8,128)(2,1)} %broadcast_select_fusion), calls=%async_computation | async-start | bytes 10485760 | tf_op jit(solution)/shard_map/all_to_all | solution.py:107
  36.9 0.0 copy-done.1
  36.9 0.1 add_select_fusion.1
  37.0 0.6 pad_add_fusion.slot_ref
  37.6 84.4 %all-to-all-done.refs_2_.refs_3_.refs_4_.refs_7_.refs_8_.refs_9_ = bf16[4,2,128,2560]{3,2,1,0:T(8,128)(2,1)} async-done(((bf16[4,2,128,2560]{3,2,1,0:T(8,128)(2,1)}), bf16[4,2,128,2560]{3,2,1,0:T(8,128)(2,1)}, u32[]{:S(2)}, u32[]{:S(2)}) %all-to-all-start) | async-done | bytes 5242912 | tf_op jit(solution)/shard_map/all_to_all | solution.py:107
  122.0 0.1 all-gather.6.cloned.1.call-done
  122.2 51.0 %shard_map.64 = bf16[512,2560]{1,0:T(8,128)(2,1)} custom-call(s32[4,5]{1,0:T(4,128)} %pad_add_fusion.slot_ref, s32[4,5]{1,0:T(4,128)} %bitcast.28, s32[4]{0:T(128)} %bitcast.31, bf16[512,2560]{1,0:T(8,128)(2,1)} %bitcast.27, bf16[4,2,128,2560]{3,2,1,0:T(8,128)(2,1)} %bitcast.22, bf16[4,2,128,2560]{3,2,1,0:T(8,128)(2,1)} %bitcast.23, ...), custom_call_target="tpu_custom_call" | custom-call | flops 3355443200 | bytes 31457280 | tf_op jit(solution)/shard_map/pallas_call | solution.py:83
  173.2 72.0 %all-gather.4.cloned.1.call-done = bf16[2560,2560]{1,0:T(8,128)(2,1)} async-done(((bf16[320,2560]{1,0:T(8,128)(2,1)}), bf16[2560,2560]{1,0:T(8,128)(2,1)}) %all-gather.4.cloned.1.call-update) | async-done | bytes 13107216 | tf_op jit(solution)/shard_map/all_gather | solution.py:100
  245.2 11.8 %fusion = bf16[1,512,2560]{2,1,0:T(8,128)(2,1)} fusion(bf16[512,2560]{1,0:T(8,128)(2,1)} %shard_map.64, bf16[2560,2560]{1,0:T(8,128)(2,1)} %all-gather.4.cloned.1.call-done, f32[2560]{0:T(1024)S(1)} %reduce.1), kind=kOutput, calls=%fused_computation.3 | convolution fusion | flops 6713507840 | bytes 18360320 | tf_op jit(solution)/shard_map/dot_general | solution.py:114
  (4 shorter events, 0.1 us)
Async XLA Ops:
  6.5 3.3 %copy-start = (s32[1,4,5]{2,1,0:T(4,128)S(1)}, s32[1,4,5]{2,1,0:T(4,128)}, u32[]{:S(2)}) copy-start(s32[1,4,5]{2,1,0:T(4,128)} %param.8) | copy-start | bytes 244
  6.5 115.7 %all-gather.6.cloned.1.call-start = ((), (), s32[]{:S(2)}) async-start(), calls=%async_computation.2 | async-start | bytes 6553600 | tf_op jit(solution)/shard_map/all_gather | solution.py:102
  9.0 236.1 %all-gather.4.cloned.1.call-start = ((), (), s32[]{:S(2)}) async-start(), calls=%async_computation.1 | async-start | bytes 14745600 | tf_op jit(solution)/shard_map/all_gather | solution.py:100
  31.7 5.2 %copy-start.1 = (f32[1,2560]{1,0:T(1,128)S(1)}, f32[1,2560]{1,0:T(1,128)}, u32[]{:S(2)}) copy-start(f32[1,2560]{1,0:T(1,128)} %param.11) | copy-start | bytes 30724
  31.7 90.3 %all-to-all-start = ((bf16[4,2,128,2560]{3,2,1,0:T(8,128)(2,1)}), bf16[4,2,128,2560]{3,2,1,0:T(8,128)(2,1)}, u32[]{:S(2)}, u32[]{:S(2)}) async-start(bf16[4,2,128,2560]{3,2,1,0:T(8,128)(2,1)} %broadcast_select_fusion), calls=%async_computation | async-start | bytes 10485760 | tf_op jit(solution)/shard_map/all_to_all | solution.py:107
Sparse Core Ops, SparseCore 0:
  9.2 112.9 all-gather.5
  123.8 121.2 all-gather.3

commit v2 on v1

--- a/solution.py
+++ b/solution.py
@@ -19,7 +19,7 @@
     heads = width // HS
     group = GROUP if heads % GROUP == 0 else 1
     span = group * HS
-    scale = math.sqrt(HS)
+    inv_scale = 1.0 / math.sqrt(HS)
 
     def kernel(slot_ref, block_ref, limit_ref, q_ref, *refs):
         key_refs = refs[:listed]
@@ -28,7 +28,8 @@
         t = pl.program_id(1)
         limit = limit_ref[t]
         lane = lax.broadcasted_iota(jnp.int32, (1, block_len), 1)
-        allowed = [block_ref[t, j] * block_len + lane < limit for j in range(listed)]
+        last = listed - 1
+        allowed = block_ref[t, last] * block_len + lane < limit
         for h in range(group):
             cols = slice(h * HS, (h + 1) * HS)
             q = q_ref[:, cols]
@@ -39,8 +40,10 @@
                     key_refs[j][:, cols],
                     (((1,), (1,)), ((), ())),
                     preferred_element_type=jnp.float32,
-                ) / scale
-                scores.append(jnp.where(allowed[j], s, -jnp.inf))
+                ) * inv_scale
+                if j == last:
+                    s = jnp.where(allowed, s, -jnp.inf)
+                scores.append(s)
             row_max = scores[0].max(axis=1, keepdims=True)
             for s in scores[1:]:
                 row_max = jnp.maximum(row_max, s.max(axis=1, keepdims=True))
@@ -48,9 +51,10 @@
             total = exps[0].sum(axis=1, keepdims=True)
             for e in exps[1:]:
                 total = total + e.sum(axis=1, keepdims=True)
+            inv_total = 1.0 / total
             acc = None
             for j in range(listed):
-                w = (exps[j] / total).astype(jnp.bfloat16)
+                w = (exps[j] * inv_total).astype(jnp.bfloat16)
                 part = jnp.dot(w, value_refs[j][:, cols], preferred_element_type=jnp.float32)
                 acc = part if acc is None else acc + part
             out_ref[:, cols] = acc.astype(out_ref.dtype)
@@ -89,6 +93,34 @@
     )(slot_ids, block_ids, limits, query_rows, *operands[1:])
 
 
+def swap(block, owners, bit):
+    return lax.ppermute(block, "seq", [(s, s ^ bit) for s in range(owners)])
+
+
+def spread_sinks(own, sinks, owners, me):
+    if owners != 4:
+        return lax.all_gather(own, "seq"), sinks
+    first = swap(own, owners, 1)
+    pair = me // 2
+    in_pair = sinks // 2 == pair
+    count = jnp.sum(in_pair.astype(jnp.int32))
+    lone = jnp.where(in_pair[0], sinks[0], sinks[1])
+    relay = jnp.where((count == 1) & (lone != me), first, own)
+    second = swap(relay, owners, 2)
+    third = swap(second, owners, 1)
+    other_count = jnp.sum((sinks // 2 != pair).astype(jnp.int32))
+    slots = jnp.where(
+        sinks == me,
+        0,
+        jnp.where(
+            sinks == (me ^ 1),
+            1,
+            jnp.where((other_count == 1) | (sinks == (me ^ 2)), 2, 3),
+        ),
+    ).astype(jnp.int32)
+    return jnp.stack([own, first, second, third]), slots
+
+
 def shards(queries, kv_cache, block_lists, key_limit, out_weight, gate):
     owners = lax.axis_size("seq")
     me = lax.axis_index("seq")
@@ -99,14 +131,15 @@
     width = blocks.shape[3]
     weight = lax.all_gather(out_weight, "fsdp", axis=0, tiled=True)
     every_list = lax.all_gather(block_ids, "seq")
-    sink_pool = lax.all_gather(blocks[0], "seq")
+    sink_pool, sink_slots = spread_sinks(blocks[0], block_ids[0, :NSINK], owners, me)
     readers_ids = every_list[:, :, NSINK:].reshape(owners, -1)
     asked = jnp.max(jnp.where(readers_ids % owners == me, readers_ids, -1), axis=1)
     asked_slot = jnp.maximum(asked, 0) // owners
-    outgoing = jnp.take(blocks, asked_slot, axis=0)
+    outgoing = jnp.take(blocks, asked_slot, axis=0, mode="clip")
     window_pool = lax.all_to_all(outgoing, "seq", split_axis=0, concat_axis=0, tiled=True)
     slot_ids = jnp.concatenate(
-        [block_ids[:, :NSINK], block_ids[:, NSINK:] % owners], axis=1
+        [jnp.broadcast_to(sink_slots[None, :], (tiles, NSINK)), block_ids[:, NSINK:] % owners],
+        axis=1,
     ).astype(jnp.int32)
     mixed = attention(
         slot_ids, block_ids, key_limit[0], queries[0], sink_pool, window_pool

time: 264 us -> 248 us (0.939)
  waiting for transfers between devices: 157 us -> 106 us
  blocking collectives: 9.57 us -> 32.5 us
  starting transfers between devices: 5.22 us -> 11.6 us
    ppermute x0 -> x3, waiting for transfers between devices: none -> 105 us  [swap(): return lax.ppermute(block, 'seq', [(s, s ^ bit) for s in range(owners)])]
    all_to_all x1, waiting for transfers between devices: 84.4 us -> 0.01 us  [shards(): lax.all_to_all(outgoing, 'seq', split_axis=0, concat_axis=0, tiled=True)]
    all_gather x1, waiting for transfers between devices: 72 us -> 0.01 us  [shards(): weight = lax.all_gather(out_weight, 'fsdp', axis=0, tiled=True)]
    all_gather x1, blocking collectives: 9.57 us -> 32.5 us  [shards(): every_list = lax.all_gather(block_ids, 'seq')]
    ppermute x0 -> x3, starting transfers between devices: none -> 6.46 us  [swap(): return lax.ppermute(block, 'seq', [(s, s ^ bit) for s in range(owners)])]
    another operation x0 -> x1, other arithmetic: none -> 4.96 us  [spread_sinks(): return (jnp.stack([own, first, second, third]), slots)]
    select_n x2, other arithmetic: 5.39 us -> 1.54 us  [the longest x1 1.53 us: spread_sinks(): relay = jnp.where((count == 1) & (lone != me), first, own)]
  transfers between devices with their start and end apart: 3 -> 5, of which waited for: 3 -> 2; matrix products, arithmetic and copies ran while one was open for 5% -> 7% of each run, Pallas kernels for 19% -> 21%
where the time goes in v2:
time: 248 us; the launch traced here: 247 us
  waiting for transfers between devices  106 us (43%)
  Pallas kernels  51.1 us (21%)
  blocking collectives  32.5 us (13%)
  between operations  16 us (6%)
  matrix products  11.8 us (5%)
  starting transfers between devices  11.6 us (5%)
  local copies, waits for them, and re-layouts  9.43 us (4%)
  other arithmetic  8.81 us (4%)
    ppermute x3, waiting for transfers between devices, swap(): return lax.ppermute(block, 'seq', [(s, s ^ bit) for s in range(owners)])  105 us
    pallas_call x1, Pallas kernels, attention(): pl.pallas_call(kernel, grid_spec=grid_spec, out_shape=jax.ShapeDtypeStruc...  51.1 us
    all_gather x1, blocking collectives, shards(): every_list = lax.all_gather(block_ids, 'seq')  32.5 us
    dot_general x1, matrix products, shards(): projected = jnp.dot(mixed, weight, preferred_element_type=jnp.float32)  11.8 us
    ppermute x3, starting transfers between devices, swap(): return lax.ppermute(block, 'seq', [(s, s ^ bit) for s in range(owners)])  6.46 us
    gather x1, local copies, waits for them, and re-layouts, shards(): outgoing = jnp.take(blocks, asked_slot, axis=0, mode='clip')  6.19 us
    all_to_all x1, starting transfers between devices, shards(): lax.all_to_all(outgoing, 'seq', split_axis=0, concat_axis=0, tiled=True)  5.19 us
  transfers between devices with their start and end apart: 5, of which 2 were waited for; matrix products, arithmetic and copies ran while one was open for 7% of the time, Pallas kernels for 21%

profile of v2, /device:TPU:0, one launch (start us, length us, event | category | flops | bytes accessed | tf_op | source)
XLA Modules:
  0.0 247.5 jit_solution(13247297630509979736)
XLA Ops:
  6.5 0.0 copy-start
  6.5 0.0 all-gather.2.cloned.1.call-start
  6.5 0.7 all-gather.2.cloned.1.call-update
  7.3 2.6 %slice_bitcast_fusion.1 = (bf16[1,2,128,2560]{3,2,1,0:T(8,128)(2,1)S(1)}, bf16[2,128,2560]{2,1,0:T(8,128)(2,1)}) fusion(bf16[1,5,1,2,128,2560]{5,4,3,2,1,0:T(8,128)(2,1)} %param.7), kind=kLoop, calls=%fused_computation.6 | loop fusion | bytes 3932160 | tf_op jit(solution)/shard_map/slice | solution.py:134
  9.9 3.0 %collective-permute-start = (bf16[2,128,2560]{2,1,0:T(8,128)(2,1)}, bf16[2,128,2560]{2,1,0:T(8,128)(2,1)S(1)}, u32[]{:S(2)}, u32[]{:S(2)}) collective-permute-start(bf16[2,128,2560]{2,1,0:T(8,128)(2,1)} %get-tuple-element.9), channel_id=1, source_target_pairs={{0,8},{8,0},{16,24},{24,16},{1,9},{9,1},{17,25},{25,17},{2,10},{10... | collective-permute-start | bytes 3932168 | tf_op jit(solution)/shard_map/ppermute | solution.py:97
  12.8 0.0 copy-done
  12.8 32.5 %all_gather.6 = s32[4,4,5]{2,1,0:T(4,128)S(1)} all-gather(s32[1,4,5]{2,1,0:T(4,128)S(1)} %copy-done), channel_id=1, replica_groups=mesh['seq'=4,'fsdp'=8] {'seq'}, dimensions={0}, use_global_device_ids=true | all-gather | bytes 400 | tf_op jit(solution)/shard_map/all_gather | solution.py:133
  45.3 0.2 select_reduce_fusion
  45.6 6.2 %gather_fusion = bf16[4,2,128,2560]{3,2,1,0:T(8,128)(2,1)} fusion(bf16[5,2,128,2560]{3,2,1,0:T(8,128)(2,1)} %bitcast.42, s32[1024]{0:T(1024)S(1)} %pad_clamp_fusion), kind=kCustom, calls=%fused_computation | custom fusion | bytes 10485776 | tf_op jit(solution)/shard_map/jit(_take)/gather | solution.py:138
  51.7 0.0 copy-start.1
  51.7 5.2 %all-to-all-start = ((bf16[4,2,128,2560]{3,2,1,0:T(8,128)(2,1)}), bf16[4,2,128,2560]{3,2,1,0:T(8,128)(2,1)}, u32[]{:S(2)}, u32[]{:S(2)}) async-start(bf16[4,2,128,2560]{3,2,1,0:T(8,128)(2,1)} %gather_fusion), calls=%async_computation | async-start | bytes 10485760 | tf_op jit(solution)/shard_map/all_to_all | solution.py:139
  57.0 0.6 fusion.7
  57.6 0.7 convert_reduce_fusion
  60.2 0.0 collective-permute-done
  60.2 1.5 broadcast_select_fusion
  61.7 2.0 collective-permute-start.1
  63.7 78.9 %collective-permute-done.1 = bf16[2,128,2560]{2,1,0:T(8,128)(2,1)} collective-permute-done((bf16[2,128,2560]{2,1,0:T(8,128)(2,1)S(1)}, bf16[2,128,2560]{2,1,0:T(8,128)(2,1)}, u32[]{:S(2)}, u32[]{:S(2)}) %collective-permute-start.1) | collective-permute-done | bytes 1310752 | tf_op jit(solution)/shard_map/ppermute | solution.py:97
  142.6 1.5 collective-permute-start.2
  144.1 0.6 fusion.4
  145.4 0.0 copy-done.1
  145.5 0.1 add_select_fusion.1
  145.6 0.7 pad_add_fusion.slot_ref
  146.2 26.5 %collective-permute-done.2 = bf16[2,128,2560]{2,1,0:T(8,128)(2,1)} collective-permute-done((bf16[2,128,2560]{2,1,0:T(8,128)(2,1)}, bf16[2,128,2560]{2,1,0:T(8,128)(2,1)}, u32[]{:S(2)}, u32[]{:S(2)}) %collective-permute-start.2) | collective-permute-done | bytes 1310752 | tf_op jit(solution)/shard_map/ppermute | solution.py:97
  172.8 5.0 %pad_maximum_fusion.refs_0_.refs_1_.refs_5_.refs_6_ = bf16[4,2,128,2560]{3,2,1,0:T(8,128)(2,1)} fusion(bf16[1,2,128,2560]{3,2,1,0:T(8,128)(2,1)} %bitcast.12, bf16[1,2,128,2560]{3,2,1,0:T(8,128)(2,1)} %bitcast.11, bf16[1,2,128,2560]{3,2,1,0:T(8,128)(2,1)S(1)} %bitcast.43, bf16[1,2,128,2560]{3,2,1,0:T(8,128)(2,1)S(1)} %get-tuple-element.8), kind=kLoop, calls=%fused_computation.1 | loop fusion | flops 7864320 | bytes 10485760 | tf_op jit(solution)/shard_map/stack | solution.py:121
  177.7 0.0 all-to-all-done.refs_2_.refs_3_.refs_4_.refs_7_.refs_8_.refs_9_
  177.7 51.1 %shard_map.64 = bf16[512,2560]{1,0:T(8,128)(2,1)} custom-call(s32[4,5]{1,0:T(4,128)} %pad_add_fusion.slot_ref, s32[4,5]{1,0:T(4,128)} %bitcast.45, s32[4]{0:T(128)} %bitcast.51, bf16[512,2560]{1,0:T(8,128)(2,1)} %bitcast.44, bf16[4,2,128,2560]{3,2,1,0:T(8,128)(2,1)} %pad_maximum_fusion.refs_0_.refs_1_.refs_5_.refs_6_, ...), custom_call_target="tpu_custom_call" | custom-call | flops 3355443200 | bytes 31457280 | tf_op jit(solution)/shard_map/pallas_call | solution.py:87
  228.8 0.0 all-gather.2.cloned.1.call-done
  228.8 11.8 %fusion = bf16[1,512,2560]{2,1,0:T(8,128)(2,1)} fusion(bf16[512,2560]{1,0:T(8,128)(2,1)} %shard_map.64, bf16[2560,2560]{1,0:T(8,128)(2,1)} %all-gather.2.cloned.1.call-done, f32[2560]{0:T(1024)S(1)} %reduce.1), kind=kOutput, calls=%fused_computation.3 | convolution fusion | flops 6713507840 | bytes 18360320 | tf_op jit(solution)/shard_map/dot_general | solution.py:147
  (5 shorter events, 0.1 us)
Async XLA Ops:
  6.5 6.3 %copy-start = (s32[1,4,5]{2,1,0:T(4,128)S(1)}, s32[1,4,5]{2,1,0:T(4,128)}, u32[]{:S(2)}) copy-start(s32[1,4,5]{2,1,0:T(4,128)} %param.8) | copy-start | bytes 244
  6.5 222.3 %all-gather.2.cloned.1.call-start = ((), (), s32[]{:S(2)}) async-start(), calls=%async_computation.1 | async-start | bytes 14745600 | tf_op jit(solution)/shard_map/all_gather | solution.py:132
  9.9 50.3 %collective-permute-start = (bf16[2,128,2560]{2,1,0:T(8,128)(2,1)}, bf16[2,128,2560]{2,1,0:T(8,128)(2,1)S(1)}, u32[]{:S(2)}, u32[]{:S(2)}) collective-permute-start(bf16[2,128,2560]{2,1,0:T(8,128)(2,1)} %get-tuple-element.9), channel_id=1, source_target_pairs={{0,8},{8,0},{16,24},{24,16},{1,9},{9,1},{17,25},{25,17},{2,10},{10... | collective-permute-start | bytes 3932168 | tf_op jit(solution)/shard_map/ppermute | solution.py:97
  51.7 93.7 %copy-start.1 = (f32[1,2560]{1,0:T(1,128)S(1)}, f32[1,2560]{1,0:T(1,128)}, u32[]{:S(2)}) copy-start(f32[1,2560]{1,0:T(1,128)} %param.11) | copy-start | bytes 30724
  51.7 126.0 %all-to-all-start = ((bf16[4,2,128,2560]{3,2,1,0:T(8,128)(2,1)}), bf16[4,2,128,2560]{3,2,1,0:T(8,128)(2,1)}, u32[]{:S(2)}, u32[]{:S(2)}) async-start(bf16[4,2,128,2560]{3,2,1,0:T(8,128)(2,1)} %gather_fusion), calls=%async_computation | async-start | bytes 10485760 | tf_op jit(solution)/shard_map/all_to_all | solution.py:139
  61.7 80.9 %collective-permute-start.1 = (bf16[2,128,2560]{2,1,0:T(8,128)(2,1)S(1)}, bf16[2,128,2560]{2,1,0:T(8,128)(2,1)}, u32[]{:S(2)}, u32[]{:S(2)}) collective-permute-start(bf16[2,128,2560]{2,1,0:T(8,128)(2,1)S(1)} %broadcast_select_fusion), channel_id=1, source_target_pairs={{0,16},{8,24},{16,0},{24,8},{1,17},{9,25},{17,1},{25,9},{2,18},{10... | collective-permute-start | bytes 3932168 | tf_op jit(solution)/shard_map/ppermute | solution.py:97
  142.6 30.1 %collective-permute-start.2 = (bf16[2,128,2560]{2,1,0:T(8,128)(2,1)}, bf16[2,128,2560]{2,1,0:T(8,128)(2,1)}, u32[]{:S(2)}, u32[]{:S(2)}) collective-permute-start(bf16[2,128,2560]{2,1,0:T(8,128)(2,1)} %collective-permute-done.1), channel_id=1, source_target_pairs={{0,8},{8,0},{16,24},{24,16},{1,9},{9,1},{17,25},{25,17},{2,10},{10... | collective-permute-start | bytes 3932168 | tf_op jit(solution)/shard_map/ppermute | solution.py:97
Sparse Core Ops, SparseCore 0:
  9.0 123.7 all-gather.1

commit v3 on v2

--- a/solution.py
+++ b/solution.py
@@ -44,13 +44,15 @@
                 if j == last:
                     s = jnp.where(allowed, s, -jnp.inf)
                 scores.append(s)
-            row_max = scores[0].max(axis=1, keepdims=True)
+            peak = scores[0]
             for s in scores[1:]:
-                row_max = jnp.maximum(row_max, s.max(axis=1, keepdims=True))
+                peak = jnp.maximum(peak, s)
+            row_max = peak.max(axis=1, keepdims=True)
             exps = [jnp.exp(s - row_max) for s in scores]
-            total = exps[0].sum(axis=1, keepdims=True)
+            mass = exps[0]
             for e in exps[1:]:
-                total = total + e.sum(axis=1, keepdims=True)
+                mass = mass + e
+            total = mass.sum(axis=1, keepdims=True)
             inv_total = 1.0 / total
             acc = None
             for j in range(listed):
@@ -131,6 +133,7 @@
     width = blocks.shape[3]
     weight = lax.all_gather(out_weight, "fsdp", axis=0, tiled=True)
     every_list = lax.all_gather(block_ids, "seq")
+    every_list, blocks = lax.optimization_barrier((every_list, blocks))
     sink_pool, sink_slots = spread_sinks(blocks[0], block_ids[0, :NSINK], owners, me)
     readers_ids = every_list[:, :, NSINK:].reshape(owners, -1)
     asked = jnp.max(jnp.where(readers_ids % owners == me, readers_ids, -1), axis=1)

time: 248 us -> 218 us (0.88)
  blocking collectives: 32.5 us -> 9.7 us
  waiting for transfers between devices: 106 us -> 103 us
  Pallas kernels: 51.1 us -> 48.5 us
    all_gather x1, blocking collectives: 32.5 us -> 9.7 us  [shards(): every_list = lax.all_gather(block_ids, 'seq')]
    ppermute x3, waiting for transfers between devices: 105 us -> 102 us  [swap(): return lax.ppermute(block, 'seq', [(s, s ^ bit) for s in range(owners)])]
    pallas_call x1, Pallas kernels: 51.1 us -> 48.5 us  [attention(): pl.pallas_call(kernel, grid_spec=grid_spec, out_shape=jax.ShapeDtypeStruc...]
  transfers between devices with their start and end apart: 5 -> 5, of which waited for: 2 -> 3; matrix products, arithmetic and copies ran while one was open for 7% -> 9% of each run, Pallas kernels for 21% -> 22%
where the time goes in v3:
time: 218 us
  waiting for transfers between devices  103 us (47%)
  Pallas kernels  48.5 us (22%)
  between operations  16 us (7%)
  matrix products  11.8 us (5%)
  local copies, waits for them, and re-layouts  10.4 us (5%)
  blocking collectives  9.7 us (4%)
  starting transfers between devices  9.25 us (4%)
  other arithmetic  8.73 us (4%)
    ppermute x3, waiting for transfers between devices, swap(): return lax.ppermute(block, 'seq', [(s, s ^ bit) for s in range(owners)])  102 us
    pallas_call x1, Pallas kernels, attention(): pl.pallas_call(kernel, grid_spec=grid_spec, out_shape=jax.ShapeDtypeStruc...  48.5 us
    dot_general x1, matrix products, shards(): projected = jnp.dot(mixed, weight, preferred_element_type=jnp.float32)  11.8 us
    all_gather x1, blocking collectives, shards(): every_list = lax.all_gather(block_ids, 'seq')  9.7 us
    gather x1, local copies, waits for them, and re-layouts, shards(): outgoing = jnp.take(blocks, asked_slot, axis=0, mode='clip')  7.05 us
    all_to_all x1, starting transfers between devices, shards(): lax.all_to_all(outgoing, 'seq', split_axis=0, concat_axis=0, tiled=True)  5.19 us
    another operation x1, other arithmetic, spread_sinks(): return (jnp.stack([own, first, second, third]), slots)  4.96 us
  transfers between devices with their start and end apart: 5, of which 3 were waited for; matrix products, arithmetic and copies ran while one was open for 9% of the time, Pallas kernels for 22%

profile of v3, /device:TPU:0, one launch (start us, length us, event | category | flops | bytes accessed | tf_op | source)
XLA Modules:
  0.0 217.7 jit_solution(3491512629199485871)
XLA Ops:
  6.5 0.0 all-gather.2.cloned.1.call-start
  6.5 0.7 all-gather.2.cloned.1.call-update
  7.3 9.7 %all_gather.6 = s32[4,4,5]{2,1,0:T(4,128)S(1)} all-gather(s32[1,4,5]{2,1,0:T(4,128)} %param.8), channel_id=1, replica_groups=mesh['seq'=4,'fsdp'=8] {'seq'}, dimensions={0}, use_global_device_ids=true | all-gather | bytes 400 | tf_op jit(solution)/shard_map/all_gather | solution.py:135
  17.0 2.7 %fusion.7 = (bf16[1,2,128,2560]{3,2,1,0:T(8,128)(2,1)S(1)}, bf16[2,128,2560]{2,1,0:T(8,128)(2,1)}) fusion(bf16[5,2,128,2560]{3,2,1,0:T(8,128)(2,1)} %bitcast.39), kind=kLoop, calls=%fused_computation.33 | loop fusion | bytes 3932160 | tf_op jit(solution)/shard_map/slice | solution.py:137
  19.7 1.3 collective-permute-start
  20.9 0.2 select_reduce_fusion
  21.2 7.1 %gather_fusion = bf16[4,2,128,2560]{3,2,1,0:T(8,128)(2,1)} fusion(bf16[5,2,128,2560]{3,2,1,0:T(8,128)(2,1)} %bitcast.40, s32[1024]{0:T(1024)S(1)} %pad_clamp_fusion), kind=kCustom, calls=%fused_computation | custom fusion | bytes 10485776 | tf_op jit(solution)/shard_map/jit(_take)/gather | solution.py:141
  28.2 0.0 copy-start
  28.2 0.0 copy-start.1
  28.2 5.2 %all-to-all-start = ((bf16[4,2,128,2560]{3,2,1,0:T(8,128)(2,1)}), bf16[4,2,128,2560]{3,2,1,0:T(8,128)(2,1)}, u32[]{:S(2)}, u32[]{:S(2)}) async-start(bf16[4,2,128,2560]{3,2,1,0:T(8,128)(2,1)} %gather_fusion), calls=%async_computation | async-start | bytes 10485760 | tf_op jit(solution)/shard_map/all_to_all | solution.py:142
  33.4 0.0 copy-done
  33.5 0.6 fusion.8
  34.1 0.7 convert_reduce_fusion
  36.7 14.8 %collective-permute-done = bf16[2,128,2560]{2,1,0:T(8,128)(2,1)S(1)} collective-permute-done((bf16[2,128,2560]{2,1,0:T(8,128)(2,1)}, bf16[2,128,2560]{2,1,0:T(8,128)(2,1)S(1)}, u32[]{:S(2)}, u32[]{:S(2)}) %collective-permute-start) | collective-permute-done | bytes 1310752 | tf_op jit(solution)/shard_map/ppermute | solution.py:99
  51.5 1.5 broadcast_select_fusion
  53.0 1.3 collective-permute-start.1
  54.3 63.7 %collective-permute-done.1 = bf16[2,128,2560]{2,1,0:T(8,128)(2,1)} collective-permute-done((bf16[2,128,2560]{2,1,0:T(8,128)(2,1)S(1)}, bf16[2,128,2560]{2,1,0:T(8,128)(2,1)}, u32[]{:S(2)}, u32[]{:S(2)}) %collective-permute-start.1) | collective-permute-done | bytes 1310752 | tf_op jit(solution)/shard_map/ppermute | solution.py:99
  118.0 1.5 collective-permute-start.2
  119.4 0.6 fusion.4
  120.8 0.0 copy-done.1
  120.8 0.1 add_select_fusion.1
  120.9 0.7 pad_add_fusion.slot_ref
  121.5 24.0 %collective-permute-done.2 = bf16[2,128,2560]{2,1,0:T(8,128)(2,1)} collective-permute-done((bf16[2,128,2560]{2,1,0:T(8,128)(2,1)}, bf16[2,128,2560]{2,1,0:T(8,128)(2,1)}, u32[]{:S(2)}, u32[]{:S(2)}) %collective-permute-start.2) | collective-permute-done | bytes 1310752 | tf_op jit(solution)/shard_map/ppermute | solution.py:99
  145.5 5.0 %pad_maximum_fusion.refs_0_.refs_1_.refs_5_.refs_6_ = bf16[4,2,128,2560]{3,2,1,0:T(8,128)(2,1)} fusion(bf16[1,2,128,2560]{3,2,1,0:T(8,128)(2,1)} %bitcast.12, bf16[1,2,128,2560]{3,2,1,0:T(8,128)(2,1)} %bitcast.11, bf16[1,2,128,2560]{3,2,1,0:T(8,128)(2,1)S(1)} %bitcast.42, bf16[1,2,128,2560]{3,2,1,0:T(8,128)(2,1)S(1)} %get-tuple-element.12), kind=kLoop, calls=%fused_computation.1 | loop fusion | flops 7864320 | bytes 10485760 | tf_op jit(solution)/shard_map/stack | solution.py:123
  150.5 0.0 all-to-all-done.refs_2_.refs_3_.refs_4_.refs_7_.refs_8_.refs_9_
  150.5 48.5 %shard_map.64 = bf16[512,2560]{1,0:T(8,128)(2,1)} custom-call(s32[4,5]{1,0:T(4,128)} %pad_add_fusion.slot_ref, s32[4,5]{1,0:T(4,128)} %bitcast.44, s32[4]{0:T(128)} %bitcast.50, bf16[512,2560]{1,0:T(8,128)(2,1)} %bitcast.43, bf16[4,2,128,2560]{3,2,1,0:T(8,128)(2,1)} %pad_maximum_fusion.refs_0_.refs_1_.refs_5_.refs_6_, ...), custom_call_target="tpu_custom_call" | custom-call | flops 3355443200 | bytes 31457280 | tf_op jit(solution)/shard_map/pallas_call | solution.py:89
  199.0 0.0 all-gather.2.cloned.1.call-done
  199.0 11.8 %fusion = bf16[1,512,2560]{2,1,0:T(8,128)(2,1)} fusion(bf16[512,2560]{1,0:T(8,128)(2,1)} %shard_map.64, bf16[2560,2560]{1,0:T(8,128)(2,1)} %all-gather.2.cloned.1.call-done, f32[2560]{0:T(1024)S(1)} %reduce.1), kind=kOutput, calls=%fused_computation.3 | convolution fusion | flops 6713507840 | bytes 18360320 | tf_op jit(solution)/shard_map/dot_general | solution.py:150
  (5 shorter events, 0.1 us)
Async XLA Ops:
  6.5 192.5 %all-gather.2.cloned.1.call-start = ((), (), s32[]{:S(2)}) async-start(), calls=%async_computation.1 | async-start | bytes 14745600 | tf_op jit(solution)/shard_map/all_gather | solution.py:134
  19.7 31.9 %collective-permute-start = (bf16[2,128,2560]{2,1,0:T(8,128)(2,1)}, bf16[2,128,2560]{2,1,0:T(8,128)(2,1)S(1)}, u32[]{:S(2)}, u32[]{:S(2)}) collective-permute-start(bf16[2,128,2560]{2,1,0:T(8,128)(2,1)} %get-tuple-element.13), channel_id=1, source_target_pairs={{0,8},{8,0},{16,24},{24,16},{1,9},{9,1},{17,25},{25,17},{2,10},{10... | collective-permute-start | bytes 3932168 | tf_op jit(solution)/shard_map/ppermute | solution.py:99
  28.2 5.2 %copy-start = (s32[1,4,5]{2,1,0:T(4,128)S(1)}, s32[1,4,5]{2,1,0:T(4,128)}, u32[]{:S(2)}) copy-start(s32[1,4,5]{2,1,0:T(4,128)} %param.8) | copy-start | bytes 244
  28.2 92.5 %copy-start.1 = (f32[1,2560]{1,0:T(1,128)S(1)}, f32[1,2560]{1,0:T(1,128)}, u32[]{:S(2)}) copy-start(f32[1,2560]{1,0:T(1,128)} %param.11) | copy-start | bytes 30724
  28.2 122.2 %all-to-all-start = ((bf16[4,2,128,2560]{3,2,1,0:T(8,128)(2,1)}), bf16[4,2,128,2560]{3,2,1,0:T(8,128)(2,1)}, u32[]{:S(2)}, u32[]{:S(2)}) async-start(bf16[4,2,128,2560]{3,2,1,0:T(8,128)(2,1)} %gather_fusion), calls=%async_computation | async-start | bytes 10485760 | tf_op jit(solution)/shard_map/all_to_all | solution.py:142
  53.0 65.0 %collective-permute-start.1 = (bf16[2,128,2560]{2,1,0:T(8,128)(2,1)S(1)}, bf16[2,128,2560]{2,1,0:T(8,128)(2,1)}, u32[]{:S(2)}, u32[]{:S(2)}) collective-permute-start(bf16[2,128,2560]{2,1,0:T(8,128)(2,1)S(1)} %broadcast_select_fusion), channel_id=1, source_target_pairs={{0,16},{8,24},{16,0},{24,8},{1,17},{9,25},{17,1},{25,9},{2,18},{10... | collective-permute-start | bytes 3932168 | tf_op jit(solution)/shard_map/ppermute | solution.py:99
  118.0 27.5 %collective-permute-start.2 = (bf16[2,128,2560]{2,1,0:T(8,128)(2,1)}, bf16[2,128,2560]{2,1,0:T(8,128)(2,1)}, u32[]{:S(2)}, u32[]{:S(2)}) collective-permute-start(bf16[2,128,2560]{2,1,0:T(8,128)(2,1)} %collective-permute-done.1), channel_id=1, source_target_pairs={{0,8},{8,0},{16,24},{24,16},{1,9},{9,1},{17,25},{25,17},{2,10},{10... | collective-permute-start | bytes 3932168 | tf_op jit(solution)/shard_map/ppermute | solution.py:99
Sparse Core Ops, SparseCore 0:
  9.0 123.7 all-gather.1

commit v4 on v2

v4 whole, which is shorter than its diff:
```python
import math

import jax
import jax.numpy as jnp
from jax import lax
from jax.experimental import pallas as pl
from jax.experimental.pallas import tpu as pltpu
from jax.sharding import PartitionSpec as P

HS = 128
NSINK = 2
GROUP = 4


def attention(sink_slots, bias, query_rows, sink_pool, window_pool):
    rows, width = query_rows.shape
    block_len = sink_pool.shape[2]
    owners = window_pool.shape[0]
    pooled = NSINK + owners
    heads = width // HS
    group = GROUP if heads % GROUP == 0 else 1
    span = group * HS
    inv_scale = 1.0 / math.sqrt(HS)

    def kernel(slot_ref, bias_ref, q_ref, *refs):
        key_refs = refs[:pooled]
        value_refs = refs[pooled : 2 * pooled]
        out_ref = refs[2 * pooled]
        mask = bias_ref[...]
        for h in range(group):
            cols = slice(h * HS, (h + 1) * HS)
            keys = jnp.concatenate([r[:, cols] for r in key_refs], axis=0)
            values = jnp.concatenate([r[:, cols] for r in value_refs], axis=0)
            s = lax.dot_general(
                q_ref[:, cols], keys, (((1,), (1,)), ((), ())), preferred_element_type=jnp.float32
            )
            s = s * inv_scale + mask
            row_max = s.max(axis=1, keepdims=True)
            e = jnp.exp(s - row_max)
            inv_total = 1.0 / e.sum(axis=1, keepdims=True)
            w = (e * inv_total).astype(jnp.bfloat16)
            out_ref[:, cols] = jnp.dot(w, values, preferred_element_type=jnp.float32).astype(
                out_ref.dtype
            )

    def sink_spec(u, kv):
        return pl.BlockSpec(
            (None, None, block_len, span), lambda g, slot_ref: (slot_ref[u], kv, 0, g)
        )

    def window_spec(r, kv):
        return pl.BlockSpec((None, None, block_len, span), lambda g, slot_ref: (r, kv, 0, g))

    in_specs = [
        pl.BlockSpec((rows, pooled * block_len), lambda g, slot_ref: (0, 0)),
        pl.BlockSpec((rows, span), lambda g, slot_ref: (0, g)),
    ]
    operands = [bias, query_rows]
    for kv in range(2):
        for u in range(NSINK):
            in_specs.append(sink_spec(u, kv))
            operands.append(sink_pool)
        for r in range(owners):
            in_specs.append(window_spec(r, kv))
            operands.append(window_pool)
    grid_spec = pltpu.PrefetchScalarGridSpec(
        num_scalar_prefetch=1,
        grid=(heads // group,),
        in_specs=in_specs,
        out_specs=pl.BlockSpec((rows, span), lambda g, slot_ref: (0, g)),
    )
    keys_total = pooled * block_len
    cost = pl.CostEstimate(
        flops=4 * rows * keys_total * width,
        transcendentals=heads * rows * keys_total,
        bytes_accessed=2 * rows * width * 2 + 2 * keys_total * width * 2 + rows * keys_total * 4,
    )
    return pl.pallas_call(
        kernel,
        grid_spec=grid_spec,
        out_shape=jax.ShapeDtypeStruct((rows, width), jnp.bfloat16),
        compiler_params=pltpu.CompilerParams(dimension_semantics=("arbitrary",)),
        cost_estimate=cost,
    )(sink_slots, *operands)


def visibility(block_ids, limits, owners, block_len):
    tiles = block_ids.shape[0]
    sinks = block_ids[:, :NSINK]
    window = block_ids[:, NSINK:]
    match = window[:, :, None] % owners == jnp.arange(owners, dtype=jnp.int32)[None, None, :]
    held = jnp.max(jnp.where(match, window[:, :, None], -1), axis=1)
    pooled_ids = jnp.concatenate([sinks, held], axis=1)
    visible = jnp.where(
        pooled_ids >= 0, jnp.clip(limits[:, None] - pooled_ids * block_len, 0, block_len), 0
    )
    lane = jnp.arange(block_len, dtype=jnp.int32)
    seen = lane[None, None, :] < visible[:, :, None]
    bias = jnp.where(seen, 0.0, -jnp.inf).astype(jnp.float32)
    bias = bias.reshape(tiles, 1, -1)
    return jnp.broadcast_to(bias, (tiles, block_len, bias.shape[-1])).reshape(
        tiles * block_len, -1
    )


def swap(block, owners, bit):
    return lax.ppermute(block, "seq", [(s, s ^ bit) for s in range(owners)])


def spread_sinks(own, sinks, owners, me):
    if owners != 4:
        return lax.all_gather(own, "seq"), sinks
    first = swap(own, owners, 1)
    pair = me // 2
    in_pair = sinks // 2 == pair
    count = jnp.sum(in_pair.astype(jnp.int32))
    lone = jnp.where(in_pair[0], sinks[0], sinks[1])
    relay = jnp.where((count == 1) & (lone != me), first, own)
    second = swap(relay, owners, 2)
    third = swap(second, owners, 1)
    other_count = jnp.sum((sinks // 2 != pair).astype(jnp.int32))
    slots = jnp.where(
        sinks == me,
        0,
        jnp.where(
            sinks == (me ^ 1),
            1,
            jnp.where((other_count == 1) | (sinks == (me ^ 2)), 2, 3),
        ),
    ).astype(jnp.int32)
    return jnp.stack([own, first, second, third]), slots


def shards(queries, kv_cache, block_lists, key_limit, out_weight, gate):
    owners = lax.axis_size("seq")
    me = lax.axis_index("seq")
    blocks = kv_cache[0, :, 0]
    block_ids = block_lists[0]
    tiles = block_ids.shape[0]
    block_len = blocks.shape[2]
    width = blocks.shape[3]
    weight = lax.all_gather(out_weight, "fsdp", axis=0, tiled=True)
    every_list = lax.all_gather(block_ids, "seq")
    every_list, blocks = lax.optimization_barrier((every_list, blocks))
    sink_pool, sink_slots = spread_sinks(blocks[0], block_ids[0, :NSINK], owners, me)
    readers_ids = every_list[:, :, NSINK:].reshape(owners, -1)
    asked = jnp.max(jnp.where(readers_ids % owners == me, readers_ids, -1), axis=1)
    asked_slot = jnp.maximum(asked, 0) // owners
    outgoing = jnp.take(blocks, asked_slot, axis=0, mode="clip")
    window_pool = lax.all_to_all(outgoing, "seq", split_axis=0, concat_axis=0, tiled=True)
    bias = visibility(block_ids, key_limit[0], owners, block_len)
    mixed = attention(sink_slots, bias, queries[0], sink_pool, window_pool)
    projected = jnp.dot(mixed, weight, preferred_element_type=jnp.float32)
    return (gate[0][None, :] * projected).astype(jnp.bfloat16)[None]


def solution(mesh):
    in_specs = (
        P("fsdp", "seq", None),
        P("fsdp", None, "seq", None, None, None),
        P("fsdp", "seq", None),
        P("fsdp", "seq"),
        P("fsdp", None),
        P("fsdp", None),
    )
    out_specs = P("fsdp", "seq", None)
    return jax.shard_map(shards, mesh=mesh, in_specs=in_specs, out_specs=out_specs, check_vma=False)
```

time: 248 us -> 190 us (0.77)
  Pallas kernels: 51.1 us -> 19.2 us
  blocking collectives: 32.5 us -> 9.7 us
  waiting for transfers between devices: 106 us -> 102 us
    pallas_call x1, Pallas kernels: 51.1 us -> 19.2 us  [attention(): pl.pallas_call(kernel, grid_spec=grid_spec, out_shape=jax.ShapeDtypeStruc...]
    all_gather x1, blocking collectives: 32.5 us -> 9.7 us  [shards(): every_list = lax.all_gather(block_ids, 'seq')]
    ppermute x3, waiting for transfers between devices: 105 us -> 101 us  [swap(): return lax.ppermute(block, 'seq', [(s, s ^ bit) for s in range(owners)])]
  transfers between devices with their start and end apart: 5 -> 5, of which waited for: 2 -> 3; matrix products, arithmetic and copies ran while one was open for 7% -> 12% of each run, Pallas kernels for 21% -> 10%
where the time goes in v4:
time: 190 us; the launch traced here: 189 us
  waiting for transfers between devices  102 us (54%)
  Pallas kernels  19.2 us (10%)
  between operations  16.1 us (8%)
  local copies, waits for them, and re-layouts  11.8 us (6%)
  matrix products  11.8 us (6%)
  other arithmetic  9.99 us (5%)
  blocking collectives  9.7 us (5%)
  starting transfers between devices  9.19 us (5%)
    ppermute x3, waiting for transfers between devices, swap(): return lax.ppermute(block, 'seq', [(s, s ^ bit) for s in range(owners)])  101 us
    pallas_call x1, Pallas kernels, attention(): pl.pallas_call(kernel, grid_spec=grid_spec, out_shape=jax.ShapeDtypeStruc...  19.2 us
    dot_general x1, matrix products, shards(): projected = jnp.dot(mixed, weight, preferred_element_type=jnp.float32)  11.8 us
    all_gather x1, blocking collectives, shards(): every_list = lax.all_gather(block_ids, 'seq')  9.7 us
    gather x1, local copies, waits for them, and re-layouts, shards(): outgoing = jnp.take(blocks, asked_slot, axis=0, mode='clip')  7.05 us
    all_to_all x1, starting transfers between devices, shards(): lax.all_to_all(outgoing, 'seq', split_axis=0, concat_axis=0, tiled=True)  5.19 us
    another operation x1, other arithmetic, spread_sinks(): return (jnp.stack([own, first, second, third]), slots)  4.94 us
    ppermute x3, starting transfers between devices, swap(): return lax.ppermute(block, 'seq', [(s, s ^ bit) for s in range(owners)])  4 us
  transfers between devices with their start and end apart: 5, of which 3 were waited for; matrix products, arithmetic and copies ran while one was open for 12% of the time, Pallas kernels for 10%

profile of v4, /device:TPU:0, one launch (start us, length us, event | category | flops | bytes accessed | tf_op | source)
XLA Modules:
  0.0 189.5 jit_solution(2678360035821812278)
XLA Ops:
  6.5 0.0 all-gather.2.cloned.1.call-start
  6.5 0.7 all-gather.2.cloned.1.call-update
  7.3 9.7 %all_gather.6 = s32[4,4,5]{2,1,0:T(4,128)S(1)} all-gather(s32[1,4,5]{2,1,0:T(4,128)} %param.8), channel_id=1, replica_groups=mesh['seq'=4,'fsdp'=8] {'seq'}, dimensions={0}, use_global_device_ids=true | all-gather | bytes 400 | tf_op jit(solution)/shard_map/all_gather | solution.py:143
  17.0 2.6 %fusion.7 = (bf16[1,2,128,2560]{3,2,1,0:T(8,128)(2,1)S(1)}, bf16[2,128,2560]{2,1,0:T(8,128)(2,1)}) fusion(bf16[5,2,128,2560]{3,2,1,0:T(8,128)(2,1)} %bitcast.48), kind=kLoop, calls=%fused_computation.39 | loop fusion | bytes 3932160 | tf_op jit(solution)/shard_map/slice | solution.py:145
  19.6 1.3 collective-permute-start
  20.9 0.2 select_reduce_fusion
  21.1 7.1 %gather_fusion = bf16[4,2,128,2560]{3,2,1,0:T(8,128)(2,1)} fusion(bf16[5,2,128,2560]{3,2,1,0:T(8,128)(2,1)} %bitcast.49, s32[1024]{0:T(1024)S(1)} %pad_clamp_fusion), kind=kCustom, calls=%fused_computation | custom fusion | bytes 10485776 | tf_op jit(solution)/shard_map/jit(_take)/gather | solution.py:149
  28.2 0.0 copy-start
  28.2 0.0 copy-start.1
  28.2 0.0 copy-start.2
  28.2 5.2 %all-to-all-start = ((bf16[4,2,128,2560]{3,2,1,0:T(8,128)(2,1)}), bf16[4,2,128,2560]{3,2,1,0:T(8,128)(2,1)}, u32[]{:S(2)}, u32[]{:S(2)}) async-start(bf16[4,2,128,2560]{3,2,1,0:T(8,128)(2,1)} %gather_fusion), calls=%async_computation | async-start | bytes 10485760 | tf_op jit(solution)/shard_map/all_to_all | solution.py:150
  33.4 0.0 copy-done
  33.4 0.6 fusion.8
  34.0 0.7 convert_reduce_fusion
  36.7 14.7 %collective-permute-done = bf16[2,128,2560]{2,1,0:T(8,128)(2,1)S(1)} collective-permute-done((bf16[2,128,2560]{2,1,0:T(8,128)(2,1)}, bf16[2,128,2560]{2,1,0:T(8,128)(2,1)S(1)}, u32[]{:S(2)}, u32[]{:S(2)}) %collective-permute-start) | collective-permute-done | bytes 1310752 | tf_op jit(solution)/shard_map/ppermute | solution.py:107
  51.5 2.5 %broadcast_select_fusion = bf16[2,128,2560]{2,1,0:T(8,128)(2,1)} fusion(bf16[2,128,2560]{2,1,0:T(8,128)(2,1)S(1)} %collective-permute-done, pred[]{:T(512)S(6)} %and.53, bf16[5,2,128,2560]{3,2,1,0:T(8,128)(2,1)} %bitcast.50), kind=kLoop, calls=%fused_computation.4 | loop fusion | flops 655360 | bytes 3932161 | tf_op jit(solution)/shard_map/jit(_where)/select_n | solution.py:118
  54.0 1.3 collective-permute-start.1
  55.2 0.7 fusion.5
  56.6 61.3 %collective-permute-done.1 = bf16[2,128,2560]{2,1,0:T(8,128)(2,1)} collective-permute-done((bf16[2,128,2560]{2,1,0:T(8,128)(2,1)}, bf16[2,128,2560]{2,1,0:T(8,128)(2,1)}, u32[]{:S(2)}, u32[]{:S(2)}) %collective-permute-start.1) | collective-permute-done | bytes 1310752 | tf_op jit(solution)/shard_map/ppermute | solution.py:107
  117.9 1.5 collective-permute-start.2
  119.4 0.1 add_select_fusion.1
  119.4 0.1 copy.7
  119.5 0.1 copy.8
  119.6 0.0 copy-done.1
  119.7 0.1 select_reduce_fusion.1
  119.8 0.6 compare_select_fusion.1.slot_ref
  120.3 0.0 copy-done.2
  120.4 0.1 clamp_select_fusion
  120.4 0.1 broadcast_bitcast_fusion
  120.5 24.9 %collective-permute-done.2 = bf16[2,128,2560]{2,1,0:T(8,128)(2,1)} collective-permute-done((bf16[2,128,2560]{2,1,0:T(8,128)(2,1)}, bf16[2,128,2560]{2,1,0:T(8,128)(2,1)}, u32[]{:S(2)}, u32[]{:S(2)}) %collective-permute-start.2) | collective-permute-done | bytes 1310752 | tf_op jit(solution)/shard_map/ppermute | solution.py:107
  145.4 4.9 %pad_maximum_fusion.refs_0_.refs_1_.refs_6_.refs_7_ = bf16[4,2,128,2560]{3,2,1,0:T(8,128)(2,1)} fusion(bf16[1,2,128,2560]{3,2,1,0:T(8,128)(2,1)} %bitcast.13, bf16[1,2,128,2560]{3,2,1,0:T(8,128)(2,1)} %bitcast.12, bf16[1,2,128,2560]{3,2,1,0:T(8,128)(2,1)S(1)} %bitcast.52, bf16[1,2,128,2560]{3,2,1,0:T(8,128)(2,1)S(1)} %get-tuple-element.12), kind=kLoop, calls=%fused_computation.1 | loop fusion | flops 7864320 | bytes 10485760 | tf_op jit(solution)/shard_map/stack | solution.py:131
  150.4 0.0 all-to-all-done.refs_2_.refs_3_.refs_4_.refs_5_.refs_8_.refs_9_.refs_10_.refs_11_
  150.4 1.3 broadcast_in_dim.61
  151.6 19.2 %shard_map.64 = bf16[512,2560]{1,0:T(8,128)(2,1)} custom-call(s32[2]{0:T(128)} %compare_select_fusion.1.slot_ref, f32[512,768]{1,0:T(8,128)} %bitcast.51, bf16[512,2560]{1,0:T(8,128)(2,1)} %bitcast.53, bf16[4,2,128,2560]{3,2,1,0:T(8,128)(2,1)} %pad_maximum_fusion.refs_0_.refs_1_.refs_6_.refs_7_, ...), custom_call_target="tpu_custom_call" | custom-call | flops 4026531840 | bytes 14680064 | tf_op jit(solution)/shard_map/pallas_call | solution.py:78
  170.8 0.0 all-gather.2.cloned.1.call-done
  170.8 11.8 %fusion = bf16[1,512,2560]{2,1,0:T(8,128)(2,1)} fusion(bf16[512,2560]{1,0:T(8,128)(2,1)} %shard_map.64, bf16[2560,2560]{1,0:T(8,128)(2,1)} %all-gather.2.cloned.1.call-done, f32[2560]{0:T(1024)S(1)} %reduce.1), kind=kOutput, calls=%fused_computation.3 | convolution fusion | flops 6713507840 | bytes 18360320 | tf_op jit(solution)/shard_map/dot_general | solution.py:153
  (5 shorter events, 0.1 us)
Async XLA Ops:
  6.5 164.3 %all-gather.2.cloned.1.call-start = ((), (), s32[]{:S(2)}) async-start(), calls=%async_computation.1 | async-start | bytes 14745600 | tf_op jit(solution)/shard_map/all_gather | solution.py:142
  19.6 31.9 %collective-permute-start = (bf16[2,128,2560]{2,1,0:T(8,128)(2,1)}, bf16[2,128,2560]{2,1,0:T(8,128)(2,1)S(1)}, u32[]{:S(2)}, u32[]{:S(2)}) collective-permute-start(bf16[2,128,2560]{2,1,0:T(8,128)(2,1)} %get-tuple-element.13), channel_id=1, source_target_pairs={{0,8},{8,0},{16,24},{24,16},{1,9},{9,1},{17,25},{25,17},{2,10},{10... | collective-permute-start | bytes 3932168 | tf_op jit(solution)/shard_map/ppermute | solution.py:107
  28.2 5.2 %copy-start = (s32[1,4,5]{2,1,0:T(4,128)S(1)}, s32[1,4,5]{2,1,0:T(4,128)}, u32[]{:S(2)}) copy-start(s32[1,4,5]{2,1,0:T(4,128)} %param.8) | copy-start | bytes 244
  28.2 91.4 %copy-start.1 = (f32[1,2560]{1,0:T(1,128)S(1)}, f32[1,2560]{1,0:T(1,128)}, u32[]{:S(2)}) copy-start(f32[1,2560]{1,0:T(1,128)} %param.11) | copy-start | bytes 30724
  28.2 92.2 %copy-start.2 = (s32[1,4]{1,0:T(1,128)S(1)}, s32[1,4]{1,0:T(1,128)}, u32[]{:S(2)}) copy-start(s32[1,4]{1,0:T(1,128)} %param.9) | copy-start | bytes 52
  28.2 122.2 %all-to-all-start = ((bf16[4,2,128,2560]{3,2,1,0:T(8,128)(2,1)}), bf16[4,2,128,2560]{3,2,1,0:T(8,128)(2,1)}, u32[]{:S(2)}, u32[]{:S(2)}) async-start(bf16[4,2,128,2560]{3,2,1,0:T(8,128)(2,1)} %gather_fusion), calls=%async_computation | async-start | bytes 10485760 | tf_op jit(solution)/shard_map/all_to_all | solution.py:150
  54.0 63.9 %collective-permute-start.1 = (bf16[2,128,2560]{2,1,0:T(8,128)(2,1)}, bf16[2,128,2560]{2,1,0:T(8,128)(2,1)}, u32[]{:S(2)}, u32[]{:S(2)}) collective-permute-start(bf16[2,128,2560]{2,1,0:T(8,128)(2,1)} %broadcast_select_fusion), channel_id=1, source_target_pairs={{0,16},{8,24},{16,0},{24,8},{1,17},{9,25},{17,1},{25,9},{2,18},{10... | collective-permute-start | bytes 3932168 | tf_op jit(solution)/shard_map/ppermute | solution.py:107
  117.9 27.5 %collective-permute-start.2 = (bf16[2,128,2560]{2,1,0:T(8,128)(2,1)}, bf16[2,128,2560]{2,1,0:T(8,128)(2,1)}, u32[]{:S(2)}, u32[]{:S(2)}) collective-permute-start(bf16[2,128,2560]{2,1,0:T(8,128)(2,1)} %collective-permute-done.1), channel_id=1, source_target_pairs={{0,8},{8,0},{16,24},{24,16},{1,9},{9,1},{17,25},{25,17},{2,10},{10... | collective-permute-start | bytes 3932168 | tf_op jit(solution)/shard_map/ppermute | solution.py:107
Sparse Core Ops, SparseCore 0:
  9.0 123.7 all-gather.1

commit v5 on v4

--- a/solution.py
+++ b/solution.py
@@ -12,10 +12,10 @@
 GROUP = 4
 
 
-def attention(sink_slots, bias, query_rows, sink_pool, window_pool):
+def attention(sink_ids, bias, query_rows, arrived):
     rows, width = query_rows.shape
-    block_len = sink_pool.shape[2]
-    owners = window_pool.shape[0]
+    block_len = arrived.shape[3]
+    owners = arrived.shape[0]
     pooled = NSINK + owners
     heads = width // HS
     group = GROUP if heads % GROUP == 0 else 1
@@ -45,11 +45,13 @@
 
     def sink_spec(u, kv):
         return pl.BlockSpec(
-            (None, None, block_len, span), lambda g, slot_ref: (slot_ref[u], kv, 0, g)
+            (None, None, None, block_len, span), lambda g, slot_ref: (slot_ref[u], 1, kv, 0, g)
         )
 
     def window_spec(r, kv):
-        return pl.BlockSpec((None, None, block_len, span), lambda g, slot_ref: (r, kv, 0, g))
+        return pl.BlockSpec(
+            (None, None, None, block_len, span), lambda g, slot_ref: (r, 0, kv, 0, g)
+        )
 
     in_specs = [
         pl.BlockSpec((rows, pooled * block_len), lambda g, slot_ref: (0, 0)),
@@ -59,10 +61,10 @@
     for kv in range(2):
         for u in range(NSINK):
             in_specs.append(sink_spec(u, kv))
-            operands.append(sink_pool)
+            operands.append(arrived)
         for r in range(owners):
             in_specs.append(window_spec(r, kv))
-            operands.append(window_pool)
+            operands.append(arrived)
     grid_spec = pltpu.PrefetchScalarGridSpec(
         num_scalar_prefetch=1,
         grid=(heads // group,),
@@ -81,7 +83,7 @@
         out_shape=jax.ShapeDtypeStruct((rows, width), jnp.bfloat16),
         compiler_params=pltpu.CompilerParams(dimension_semantics=("arbitrary",)),
         cost_estimate=cost,
-    )(sink_slots, *operands)
+    )(sink_ids, *operands)
 
 
 def visibility(block_ids, limits, owners, block_len):
@@ -103,34 +105,6 @@
     )
 
 
-def swap(block, owners, bit):
-    return lax.ppermute(block, "seq", [(s, s ^ bit) for s in range(owners)])
-
-
-def spread_sinks(own, sinks, owners, me):
-    if owners != 4:
-        return lax.all_gather(own, "seq"), sinks
-    first = swap(own, owners, 1)
-    pair = me // 2
-    in_pair = sinks // 2 == pair
-    count = jnp.sum(in_pair.astype(jnp.int32))
-    lone = jnp.where(in_pair[0], sinks[0], sinks[1])
-    relay = jnp.where((count == 1) & (lone != me), first, own)
-    second = swap(relay, owners, 2)
-    third = swap(second, owners, 1)
-    other_count = jnp.sum((sinks // 2 != pair).astype(jnp.int32))
-    slots = jnp.where(
-        sinks == me,
-        0,
-        jnp.where(
-            sinks == (me ^ 1),
-            1,
-            jnp.where((other_count == 1) | (sinks == (me ^ 2)), 2, 3),
-        ),
-    ).astype(jnp.int32)
-    return jnp.stack([own, first, second, third]), slots
-
-
 def shards(queries, kv_cache, block_lists, key_limit, out_weight, gate):
     owners = lax.axis_size("seq")
     me = lax.axis_index("seq")
@@ -141,15 +115,15 @@
     width = blocks.shape[3]
     weight = lax.all_gather(out_weight, "fsdp", axis=0, tiled=True)
     every_list = lax.all_gather(block_ids, "seq")
-    every_list, blocks = lax.optimization_barrier((every_list, blocks))
-    sink_pool, sink_slots = spread_sinks(blocks[0], block_ids[0, :NSINK], owners, me)
     readers_ids = every_list[:, :, NSINK:].reshape(owners, -1)
     asked = jnp.max(jnp.where(readers_ids % owners == me, readers_ids, -1), axis=1)
     asked_slot = jnp.maximum(asked, 0) // owners
-    outgoing = jnp.take(blocks, asked_slot, axis=0, mode="clip")
-    window_pool = lax.all_to_all(outgoing, "seq", split_axis=0, concat_axis=0, tiled=True)
+    wanted = jnp.take(blocks, asked_slot, axis=0, mode="clip")
+    first = jnp.broadcast_to(blocks[0][None], wanted.shape)
+    outgoing = jnp.stack([wanted, first], axis=1)
+    arrived = lax.all_to_all(outgoing, "seq", split_axis=0, concat_axis=0, tiled=True)
     bias = visibility(block_ids, key_limit[0], owners, block_len)
-    mixed = attention(sink_slots, bias, queries[0], sink_pool, window_pool)
+    mixed = attention(block_ids[0, :NSINK], bias, queries[0], arrived)
     projected = jnp.dot(mixed, weight, preferred_element_type=jnp.float32)
     return (gate[0][None, :] * projected).astype(jnp.bfloat16)[None]
 

time: 190 us -> 196 us (1.032)
  waiting for transfers between devices: 102 us -> 112 us
  starting transfers between devices: 9.19 us -> 6.16 us
  between operations: 16.1 us -> 13.5 us
    all_to_all x1, waiting for transfers between devices: 0.01 us -> 112 us  [shards(): lax.all_to_all(outgoing, 'seq', split_axis=0, concat_axis=0, tiled=True)]
    ppermute x3 -> x0, waiting for transfers between devices: 101 us -> none  [swap(): return lax.ppermute(block, 'seq', [(s, s ^ bit) for s in range(owners)])]
    another operation x1, other arithmetic: 4.94 us -> 9.01 us  [shards(): outgoing = jnp.stack([wanted, first], axis=1)]
    ppermute x3 -> x0, starting transfers between devices: 4 us -> none  [swap(): return lax.ppermute(block, 'seq', [(s, s ^ bit) for s in range(owners)])]
    select_n x2 -> x0, other arithmetic: 3.09 us -> none  [the longest x1 2.5 us: spread_sinks(): relay = jnp.where((count == 1) & (lone != me), first, own)]
    another operation x0 -> x1, local copies, waits for them, and re-layouts: none -> 2.79 us  [shards(): outgoing = jnp.stack([wanted, first], axis=1)]
  transfers between devices with their start and end apart: 5 -> 2, of which waited for: 3 -> 1; matrix products, arithmetic and copies ran while one was open for 12% -> 12% of each run, Pallas kernels for 10% -> 10%
where the time goes in v5:
time: 196 us; the launch traced here: 195 us
  waiting for transfers between devices  112 us (57%)
  Pallas kernels  19.1 us (10%)
  between operations  13.5 us (7%)
  local copies, waits for them, and re-layouts  13.2 us (7%)
  matrix products  11.8 us (6%)
  blocking collectives  9.7 us (5%)
  other arithmetic  9.55 us (5%)
  starting transfers between devices  6.16 us (3%)
    all_to_all x1, waiting for transfers between devices, shards(): lax.all_to_all(outgoing, 'seq', split_axis=0, concat_axis=0, tiled=True)  112 us
    pallas_call x1, Pallas kernels, attention(): pl.pallas_call(kernel, grid_spec=grid_spec, out_shape=jax.ShapeDtypeStruc...  19.1 us
    dot_general x1, matrix products, shards(): projected = jnp.dot(mixed, weight, preferred_element_type=jnp.float32)  11.8 us
    all_gather x1, blocking collectives, shards(): every_list = lax.all_gather(block_ids, 'seq')  9.7 us
    another operation x1, other arithmetic, shards(): outgoing = jnp.stack([wanted, first], axis=1)  9.01 us
    gather x1, local copies, waits for them, and re-layouts, shards(): wanted = jnp.take(blocks, asked_slot, axis=0, mode='clip')  7 us
    all_to_all x1, starting transfers between devices, shards(): lax.all_to_all(outgoing, 'seq', split_axis=0, concat_axis=0, tiled=True)  6.16 us
  transfers between devices with their start and end apart: 2, of which 1 were waited for; matrix products, arithmetic and copies ran while one was open for 12% of the time, Pallas kernels for 10%

profile of v5, /device:TPU:0, one launch (start us, length us, event | category | flops | bytes accessed | tf_op | source)
XLA Modules:
  0.0 195.5 jit_solution(1217691074302467448)
XLA Ops:
  6.5 0.0 all-gather.2.cloned.1.call-start
  6.5 0.7 all-gather.2.cloned.1.call-update
  7.3 9.7 %all_gather.6 = s32[4,4,5]{2,1,0:T(4,128)S(1)} all-gather(s32[1,4,5]{2,1,0:T(4,128)} %param.8), channel_id=1, replica_groups=mesh['seq'=4,'fsdp'=8] {'seq'}, dimensions={0}, use_global_device_ids=true | all-gather | bytes 400 | tf_op jit(solution)/shard_map/all_gather | solution.py:117
  17.0 0.2 select_reduce_fusion
  17.2 7.0 %gather_fusion = bf16[4,2,128,2560]{3,2,1,0:T(8,128)(2,1)} fusion(bf16[5,2,128,2560]{3,2,1,0:T(8,128)(2,1)} %bitcast.34, s32[1024]{0:T(1024)S(1)} %pad_clamp_fusion), kind=kCustom, calls=%fused_computation | custom fusion | bytes 10485776 | tf_op jit(solution)/shard_map/jit(_take)/gather | solution.py:121
  24.2 1.4 slice_bitcast_fusion
  25.6 2.8 %stack_broadcast_in_dim.2 = bf16[4,1,2,128,2560]{4,3,2,1,0:T(8,128)(2,1)} broadcast(bf16[2,128,2560]{2,1,0:T(8,128)(2,1)S(1)} %slice_bitcast_fusion), dimensions={2,3,4} | broadcast | bytes 6553600 | tf_op jit(solution)/shard_map/stack;broadcast_in_dim | solution.py:123
  28.4 9.0 %pad_maximum_fusion = bf16[4,2,2,128,2560]{4,3,2,1,0:T(8,128)(2,1)} fusion(bf16[4,1,2,128,2560]{4,3,2,1,0:T(8,128)(2,1)} %stack_broadcast_in_dim.2, bf16[4,1,2,128,2560]{4,3,2,1,0:T(8,128)(2,1)} %bitcast.33), kind=kLoop, calls=%fused_computation.1 | loop fusion | flops 5242880 | bytes 20971520 | tf_op jit(solution)/shard_map/stack | solution.py:123
  37.4 0.0 copy-start
  37.4 0.0 copy-start.1
  37.4 0.0 copy-start.2
  37.4 6.2 %all-to-all-start = ((bf16[4,2,2,128,2560]{4,3,2,1,0:T(8,128)(2,1)}), bf16[4,2,2,128,2560]{4,3,2,1,0:T(8,128)(2,1)}, u32[]{:S(2)}, u32[]{:S(2)}) async-start(bf16[4,2,2,128,2560]{4,3,2,1,0:T(8,128)(2,1)} %pad_maximum_fusion), calls=%async_computation | async-start | bytes 20971520 | tf_op jit(solution)/shard_map/all_to_all | solution.py:124
  43.6 0.0 copy-done
  43.6 0.1 add_select_fusion.1
  43.7 0.1 copy.7
  43.8 0.1 copy.8
  43.9 0.0 copy-done.1
  43.9 0.1 select_reduce_fusion.1
  44.0 0.5 slice_bitcast_fusion.1.slot_ref
  44.5 0.0 copy-done.2
  44.5 0.1 clamp_select_fusion
  44.6 0.1 broadcast_bitcast_fusion
  44.7 111.7 %all-to-all-done.refs_0_.refs_1_.refs_2_.refs_3_.refs_4_.refs_5_.refs_6_.refs_7_.refs_8_.refs_9_.refs_10_.refs_11_ = bf16[4,2,2,128,2560]{4,3,2,1,0:T(8,128)(2,1)} async-done(((bf16[4,2,2,128,2560]{4,3,2,1,0:T(8,128)(2,1)}), bf16[4,2,2,128,2560]{4,3,2,1,0:T(8,128)(2,1)}, u32[]{:S(2)}, u32[]{:S(2)}) %all-to-all-start) | async-done | bytes 10485792 | tf_op jit(solution)/shard_map/all_to_all | solution.py:124
  156.4 1.3 broadcast_in_dim.45
  157.6 19.1 %shard_map.64 = bf16[512,2560]{1,0:T(8,128)(2,1)} custom-call(s32[2]{0:T(128)} %slice_bitcast_fusion.1.slot_ref, f32[512,768]{1,0:T(8,128)} %bitcast.35, bf16[512,2560]{1,0:T(8,128)(2,1)} %bitcast.36, bf16[4,2,2,128,2560]{4,3,2,1,0:T(8,128)(2,1)} %all-to-all-done.refs_0_.refs_1_.refs_2_.refs_3_.refs_4_.refs_5_.refs_6_.refs_7_.refs_8_.refs_9_.refs_10_.refs_11_, ...), custom_call_target="tpu_custom_call" | custom-call | flops 4026531840 | bytes 14680064 | tf_op jit(solution)/shard_map/pallas_call | solution.py:80
  176.8 0.0 all-gather.2.cloned.1.call-done
  176.8 11.8 %fusion = bf16[1,512,2560]{2,1,0:T(8,128)(2,1)} fusion(bf16[512,2560]{1,0:T(8,128)(2,1)} %shard_map.64, bf16[2560,2560]{1,0:T(8,128)(2,1)} %all-gather.2.cloned.1.call-done, f32[2560]{0:T(1024)S(1)} %reduce.1), kind=kOutput, calls=%fused_computation.3 | convolution fusion | flops 6713507840 | bytes 18360320 | tf_op jit(solution)/shard_map/dot_general | solution.py:127
  (5 shorter events, 0.1 us)
Async XLA Ops:
  6.5 170.3 %all-gather.2.cloned.1.call-start = ((), (), s32[]{:S(2)}) async-start(), calls=%async_computation.1 | async-start | bytes 14745600 | tf_op jit(solution)/shard_map/all_gather | solution.py:116
  37.4 6.2 %copy-start = (s32[1,4,5]{2,1,0:T(4,128)S(1)}, s32[1,4,5]{2,1,0:T(4,128)}, u32[]{:S(2)}) copy-start(s32[1,4,5]{2,1,0:T(4,128)} %param.8) | copy-start | bytes 244
  37.4 6.4 %copy-start.1 = (f32[1,2560]{1,0:T(1,128)S(1)}, f32[1,2560]{1,0:T(1,128)}, u32[]{:S(2)}) copy-start(f32[1,2560]{1,0:T(1,128)} %param.11) | copy-start | bytes 30724
  37.4 7.1 %copy-start.2 = (s32[1,4]{1,0:T(1,128)S(1)}, s32[1,4]{1,0:T(1,128)}, u32[]{:S(2)}) copy-start(s32[1,4]{1,0:T(1,128)} %param.9) | copy-start | bytes 52
  37.4 118.9 %all-to-all-start = ((bf16[4,2,2,128,2560]{4,3,2,1,0:T(8,128)(2,1)}), bf16[4,2,2,128,2560]{4,3,2,1,0:T(8,128)(2,1)}, u32[]{:S(2)}, u32[]{:S(2)}) async-start(bf16[4,2,2,128,2560]{4,3,2,1,0:T(8,128)(2,1)} %pad_maximum_fusion), calls=%async_computation | async-start | bytes 20971520 | tf_op jit(solution)/shard_map/all_to_all | solution.py:124
Sparse Core Ops, SparseCore 0:
  9.0 123.7 all-gather.1

commit v6 on v5

--- a/solution.py
+++ b/solution.py
@@ -9,16 +9,18 @@
 
 HS = 128
 NSINK = 2
-GROUP = 4
+GROUPS = (5, 4, 2, 1)
+CHUNKS = 2
 
 
-def attention(sink_ids, bias, query_rows, arrived):
-    rows, width = query_rows.shape
+def attention(sink_ids, bias, query_rows, arrived, chunk):
+    rows = query_rows.shape[0]
+    width = arrived.shape[-1]
     block_len = arrived.shape[3]
     owners = arrived.shape[0]
     pooled = NSINK + owners
     heads = width // HS
-    group = GROUP if heads % GROUP == 0 else 1
+    group = next(g for g in GROUPS if heads % g == 0)
     span = group * HS
     inv_scale = 1.0 / math.sqrt(HS)
 
@@ -55,7 +57,7 @@
 
     in_specs = [
         pl.BlockSpec((rows, pooled * block_len), lambda g, slot_ref: (0, 0)),
-        pl.BlockSpec((rows, span), lambda g, slot_ref: (0, g)),
+        pl.BlockSpec((rows, span), lambda g, slot_ref: (0, g + chunk * (heads // group))),
     ]
     operands = [bias, query_rows]
     for kv in range(2):
@@ -118,13 +120,19 @@
     readers_ids = every_list[:, :, NSINK:].reshape(owners, -1)
     asked = jnp.max(jnp.where(readers_ids % owners == me, readers_ids, -1), axis=1)
     asked_slot = jnp.maximum(asked, 0) // owners
-    wanted = jnp.take(blocks, asked_slot, axis=0, mode="clip")
-    first = jnp.broadcast_to(blocks[0][None], wanted.shape)
-    outgoing = jnp.stack([wanted, first], axis=1)
-    arrived = lax.all_to_all(outgoing, "seq", split_axis=0, concat_axis=0, tiled=True)
+    picks = jnp.stack([asked_slot, jnp.zeros_like(asked_slot)], axis=1).reshape(-1)
     bias = visibility(block_ids, key_limit[0], owners, block_len)
-    mixed = attention(block_ids[0, :NSINK], bias, queries[0], arrived)
-    projected = jnp.dot(mixed, weight, preferred_element_type=jnp.float32)
+    chunks = CHUNKS if (width // HS) % CHUNKS == 0 else 1
+    chunk_width = width // chunks
+    projected = None
+    for c in range(chunks):
+        cols = slice(c * chunk_width, (c + 1) * chunk_width)
+        outgoing = jnp.take(blocks[..., cols], picks, axis=0, mode="clip")
+        outgoing = outgoing.reshape(owners, 2, 2, block_len, chunk_width)
+        arrived = lax.all_to_all(outgoing, "seq", split_axis=0, concat_axis=0, tiled=True)
+        mixed = attention(block_ids[0, :NSINK], bias, queries[0], arrived, c)
+        part = jnp.dot(mixed, weight[cols], preferred_element_type=jnp.float32)
+        projected = part if projected is None else projected + part
     return (gate[0][None, :] * projected).astype(jnp.bfloat16)[None]
 
 

time: 196 us -> 184 us (0.939)
  waiting for transfers between devices: 112 us -> 98.6 us
  other arithmetic: 9.55 us -> 0.54 us
  local copies, waits for them, and re-layouts: 13.2 us -> 17.9 us
  starting transfers between devices: 6.16 us -> 10.2 us
  Pallas kernels: 19.1 us -> 22.5 us
    all_to_all x1 -> x2, waiting for transfers between devices: 112 us -> 97.9 us  [shards(): lax.all_to_all(outgoing, 'seq', split_axis=0, concat_axis=0, tiled=True)]
    another operation x1 -> x0, other arithmetic: 9.01 us -> none  [shards(): outgoing = jnp.stack([wanted, first], axis=1)]
    slice x1, local copies, waits for them, and re-layouts: 1.4 us -> 6.13 us  [shards(): outgoing = jnp.take(blocks[..., cols], picks, axis=0, mode='clip')]
    all_to_all x1 -> x2, starting transfers between devices: 6.16 us -> 10.2 us  [shards(): lax.all_to_all(outgoing, 'seq', split_axis=0, concat_axis=0, tiled=True)]
    pallas_call x1 -> x2, Pallas kernels: 19.1 us -> 22.5 us  [attention(): pl.pallas_call(kernel, grid_spec=grid_spec, out_shape=jax.ShapeDtypeStruc...]
    another operation x1, local copies, waits for them, and re-layouts: 2.79 us -> 0.01 us  [shards(): jnp.stack([asked_slot, jnp.zeros_like(asked_slot)], axis=1).reshape(-1)]
    gather x1 -> x2, local copies, waits for them, and re-layouts: 7 us -> 8.39 us  [shards(): outgoing = jnp.take(blocks[..., cols], picks, axis=0, mode='clip')]
    dot_general x1 -> x2, matrix products: 11.8 us -> 11.1 us  [shards(): part = jnp.dot(mixed, weight[cols], preferred_element_type=jnp.float32)]
  transfers between devices with their start and end apart: 2 -> 3, of which waited for: 1 -> 2; matrix products, arithmetic and copies ran while one was open for 12% -> 9% of each run, Pallas kernels for 10% -> 12%
where the time goes in v6:
time: 184 us
  waiting for transfers between devices  98.6 us (54%)
  Pallas kernels  22.5 us (12%)
  local copies, waits for them, and re-layouts  17.9 us (10%)
  between operations  13.5 us (7%)
  matrix products  11.1 us (6%)
  starting transfers between devices  10.2 us (6%)
  blocking collectives  9.7 us (5%)
    all_to_all x2, waiting for transfers between devices, shards(): lax.all_to_all(outgoing, 'seq', split_axis=0, concat_axis=0, tiled=True)  97.9 us
    pallas_call x2, Pallas kernels, attention(): pl.pallas_call(kernel, grid_spec=grid_spec, out_shape=jax.ShapeDtypeStruc...  22.5 us
    dot_general x2, matrix products, shards(): part = jnp.dot(mixed, weight[cols], preferred_element_type=jnp.float32)  11.1 us
    all_to_all x2, starting transfers between devices, shards(): lax.all_to_all(outgoing, 'seq', split_axis=0, concat_axis=0, tiled=True)  10.2 us
    all_gather x1, blocking collectives, shards(): every_list = lax.all_gather(block_ids, 'seq')  9.7 us
    gather x2, local copies, waits for them, and re-layouts, shards(): outgoing = jnp.take(blocks[..., cols], picks, axis=0, mode='clip')  8.39 us
    slice x1, local copies, waits for them, and re-layouts, shards(): outgoing = jnp.take(blocks[..., cols], picks, axis=0, mode='clip')  6.13 us
  transfers between devices with their start and end apart: 3, of which 2 were waited for; matrix products, arithmetic and copies ran while one was open for 9% of the time, Pallas kernels for 12%

profile of v6, /device:TPU:0, one launch (start us, length us, event | category | flops | bytes accessed | tf_op | source)
XLA Modules:
  0.0 184.0 jit_solution(183408784315627329)
XLA Ops:
  6.5 0.0 all-gather.2.cloned.1.call-start
  6.5 0.7 all-gather.2.cloned.1.call-update
  7.3 9.7 %all_gather.6 = s32[4,4,5]{2,1,0:T(4,128)S(1)} all-gather(s32[1,4,5]{2,1,0:T(4,128)} %param.8), channel_id=1, replica_groups=mesh['seq'=4,'fsdp'=8] {'seq'}, dimensions={0}, use_global_device_ids=true | all-gather | bytes 400 | tf_op jit(solution)/shard_map/all_gather | solution.py:119
  17.0 0.2 select_reduce_fusion
  17.2 0.1 copy.13
  17.3 0.1 reshape.133
  17.4 6.1 %fusion.13 = (bf16[5,2,128,1280]{3,2,1,0:T(8,128)(2,1)}, bf16[5,2,128,1280]{3,2,1,0:T(8,128)(2,1)S(1)}) fusion(bf16[5,2,128,2560]{3,2,1,0:T(8,128)(2,1)} %bitcast.32), kind=kLoop, calls=%fused_computation.29 | loop fusion | bytes 13107200 | tf_op jit(solution)/shard_map/slice | solution.py:130
  23.5 5.2 %gather_fusion = bf16[8,2,128,1280]{3,2,1,0:T(8,128)(2,1)} fusion(bf16[5,2,128,1280]{3,2,1,0:T(8,128)(2,1)} %get-tuple-element.5, s32[1024]{0:T(1024)S(1)} %pad_clamp_fusion), kind=kCustom, calls=%fused_computation | custom fusion | bytes 10485792 | tf_op jit(solution)/shard_map/jit(_take)/gather | solution.py:130
  28.7 5.0 %all-to-all-start = ((bf16[4,2,2,128,1280]{4,3,2,1,0:T(8,128)(2,1)}), bf16[4,2,2,128,1280]{4,3,2,1,0:T(8,128)(2,1)}, u32[]{:S(2)}, u32[]{:S(2)}) async-start(bf16[4,2,2,128,1280]{4,3,2,1,0:T(8,128)(2,1)} %bitcast.27), calls=%async_computation | async-start | bytes 10485760 | tf_op jit(solution)/shard_map/all_to_all | solution.py:132
  33.8 3.2 %gather_fusion.1 = bf16[8,2,128,1280]{3,2,1,0:T(8,128)(2,1)} fusion(bf16[5,2,128,1280]{3,2,1,0:T(8,128)(2,1)S(1)} %get-tuple-element.6, s32[1024]{0:T(1024)S(1)} %pad_clamp_fusion), kind=kCustom, calls=%fused_computation.1 | custom fusion | bytes 10485792 | tf_op jit(solution)/shard_map/jit(_take)/gather | solution.py:130
  37.0 53.3 %all-to-all-done.refs_0_.refs_1_.refs_2_.refs_3_.refs_4_.refs_5_.refs_6_.refs_7_.refs_8_.refs_9_.refs_10_.refs_11_ = bf16[4,2,2,128,1280]{4,3,2,1,0:T(8,128)(2,1)} async-done(((bf16[4,2,2,128,1280]{4,3,2,1,0:T(8,128)(2,1)}), bf16[4,2,2,128,1280]{4,3,2,1,0:T(8,128)(2,1)}, u32[]{:S(2)}, u32[]{:S(2)}) %all-to-all-start) | async-done | bytes 5242912 | tf_op jit(solution)/shard_map/all_to_all | solution.py:132
  90.3 0.0 copy-start.1
  90.3 0.0 copy-start.2
  90.3 0.0 copy-start.3
  90.3 5.2 %all-to-all-start.1 = ((bf16[4,2,2,128,1280]{4,3,2,1,0:T(8,128)(2,1)}), bf16[4,2,2,128,1280]{4,3,2,1,0:T(8,128)(2,1)}, u32[]{:S(2)}, u32[]{:S(2)}) async-start(bf16[4,2,2,128,1280]{4,3,2,1,0:T(8,128)(2,1)} %bitcast.26), calls=%async_computation.1 | async-start | bytes 10485760 | tf_op jit(solution)/shard_map/all_to_all | solution.py:132
  95.5 0.0 copy-done.1
  95.5 0.1 add_select_fusion.1
  95.6 0.1 copy.10
  95.7 0.1 copy.11
  95.8 0.0 copy-done.2
  95.8 0.1 select_reduce_fusion.1
  95.9 0.5 slice_bitcast_fusion.slot_ref
  96.4 0.0 copy-done.3
  96.4 0.1 clamp_select_fusion
  96.5 0.1 broadcast_bitcast_fusion
  96.6 1.3 broadcast_in_dim.48
  97.8 11.3 %shard_map.64 = bf16[512,1280]{1,0:T(8,128)(2,1)} custom-call(s32[2]{0:T(128)} %slice_bitcast_fusion.slot_ref, f32[512,768]{1,0:T(8,128)} %bitcast.28, bf16[512,2560]{1,0:T(8,128)(2,1)} %bitcast.30, bf16[4,2,2,128,1280]{4,3,2,1,0:T(8,128)(2,1)} %all-to-all-done.refs_0_.refs_1_.refs_2_.refs_3_.refs_4_.refs_5_.refs_6_.refs_7_.refs_8_.refs_9_.refs_10_.refs_11_, ...), custom_call_target="tpu_custom_call" | custom-call | flops 2013265920 | bytes 8126464 | tf_op jit(solution)/shard_map/pallas_call | solution.py:82
  109.1 44.5 %all-to-all-done.1.refs_0_.refs_1_.refs_2_.refs_3_.refs_4_.refs_5_.refs_6_.refs_7_.refs_8_.refs_9_.refs_10_.refs_11_ = bf16[4,2,2,128,1280]{4,3,2,1,0:T(8,128)(2,1)} async-done(((bf16[4,2,2,128,1280]{4,3,2,1,0:T(8,128)(2,1)}), bf16[4,2,2,128,1280]{4,3,2,1,0:T(8,128)(2,1)}, u32[]{:S(2)}, u32[]{:S(2)}) %all-to-all-start.1) | async-done | bytes 5242912 | tf_op jit(solution)/shard_map/all_to_all | solution.py:132
  153.6 11.2 %shard_map.65 = bf16[512,1280]{1,0:T(8,128)(2,1)} custom-call(s32[2]{0:T(128)} %slice_bitcast_fusion.slot_ref, f32[512,768]{1,0:T(8,128)} %bitcast.29, bf16[512,2560]{1,0:T(8,128)(2,1)} %bitcast.31, bf16[4,2,2,128,1280]{4,3,2,1,0:T(8,128)(2,1)} %all-to-all-done.1.refs_0_.refs_1_.refs_2_.refs_3_.refs_4_.refs_5_.refs_6_.refs_7_.refs_8_.refs_9_.refs_10_.refs_11_, ...), custom_call_target="tpu_custom_call" | custom-call | flops 2013265920 | bytes 8126464 | tf_op jit(solution)/shard_map/pallas_call | solution.py:82
  164.9 0.0 copy-start
  164.9 0.0 all-gather.2.cloned.1.call-done
  164.9 0.0 copy-start.4
  164.9 6.2 %fusion = f32[512,2560]{1,0:T(8,128)S(1)} fusion(bf16[512,1280]{1,0:T(8,128)(2,1)} %shard_map.65, bf16[2560,2560]{1,0:T(8,128)(2,1)} %all-gather.2.cloned.1.call-done), kind=kOutput, calls=%fused_computation.2 | convolution fusion | flops 3355443200 | bytes 13107200 | tf_op jit(solution)/shard_map/dot_general | solution.py:134
  171.2 0.0 copy-done
  171.2 1.2 copy-done.4
  172.3 4.8 %fusion.6 = bf16[1,512,2560]{2,1,0:T(8,128)(2,1)} fusion(f32[512,2560]{1,0:T(8,128)S(1)} %fusion, bf16[512,1280]{1,0:T(8,128)(2,1)S(1)} %copy-done, bf16[2560,2560]{1,0:T(8,128)(2,1)S(1)} %copy-done.4, f32[2560]{0:T(1024)S(1)} %reduce.1), kind=kOutput, calls=%fused_computation.7 | convolution fusion | flops 3359375360 | bytes 15740928 | tf_op jit(solution)/shard_map/dot_general | solution.py:134
  (6 shorter events, 0.1 us)
Async XLA Ops:
  6.5 158.4 %all-gather.2.cloned.1.call-start = ((), (), s32[]{:S(2)}) async-start(), calls=%async_computation.2 | async-start | bytes 14745600 | tf_op jit(solution)/shard_map/all_gather | solution.py:118
  28.7 61.6 %all-to-all-start = ((bf16[4,2,2,128,1280]{4,3,2,1,0:T(8,128)(2,1)}), bf16[4,2,2,128,1280]{4,3,2,1,0:T(8,128)(2,1)}, u32[]{:S(2)}, u32[]{:S(2)}) async-start(bf16[4,2,2,128,1280]{4,3,2,1,0:T(8,128)(2,1)} %bitcast.27), calls=%async_computation | async-start | bytes 10485760 | tf_op jit(solution)/shard_map/all_to_all | solution.py:132
  90.3 5.2 %copy-start.1 = (s32[1,4,5]{2,1,0:T(4,128)S(1)}, s32[1,4,5]{2,1,0:T(4,128)}, u32[]{:S(2)}) copy-start(s32[1,4,5]{2,1,0:T(4,128)} %param.8) | copy-start | bytes 244
  90.3 5.5 %copy-start.2 = (f32[1,2560]{1,0:T(1,128)S(1)}, f32[1,2560]{1,0:T(1,128)}, u32[]{:S(2)}) copy-start(f32[1,2560]{1,0:T(1,128)} %param.11) | copy-start | bytes 30724
  90.3 6.1 %copy-start.3 = (s32[1,4]{1,0:T(1,128)S(1)}, s32[1,4]{1,0:T(1,128)}, u32[]{:S(2)}) copy-start(s32[1,4]{1,0:T(1,128)} %param.9) | copy-start | bytes 52
  90.3 63.3 %all-to-all-start.1 = ((bf16[4,2,2,128,1280]{4,3,2,1,0:T(8,128)(2,1)}), bf16[4,2,2,128,1280]{4,3,2,1,0:T(8,128)(2,1)}, u32[]{:S(2)}, u32[]{:S(2)}) async-start(bf16[4,2,2,128,1280]{4,3,2,1,0:T(8,128)(2,1)} %bitcast.26), calls=%async_computation.1 | async-start | bytes 10485760 | tf_op jit(solution)/shard_map/all_to_all | solution.py:132
  164.9 6.3 %copy-start = (bf16[512,1280]{1,0:T(8,128)(2,1)S(1)}, bf16[512,1280]{1,0:T(8,128)(2,1)}, u32[]{:S(2)}) copy-start(bf16[512,1280]{1,0:T(8,128)(2,1)} %shard_map.64) | copy-start | bytes 3932164
  164.9 7.4 %copy-start.4 = (bf16[2560,2560]{1,0:T(8,128)(2,1)S(1)}, bf16[2560,2560]{1,0:T(8,128)(2,1)}, u32[]{:S(2)}) copy-start(bf16[2560,2560]{1,0:T(8,128)(2,1)} %all-gather.2.cloned.1.call-done) | copy-start | bytes 39321604
Sparse Core Ops, SparseCore 0:
  9.0 123.8 all-gather.1

commit v7 on v6

--- a/solution.py
+++ b/solution.py
@@ -10,7 +10,7 @@
 HS = 128
 NSINK = 2
 GROUPS = (5, 4, 2, 1)
-CHUNKS = 2
+CHUNKS = 4
 
 
 def attention(sink_ids, bias, query_rows, arrived, chunk):
@@ -88,6 +88,41 @@
     )(sink_ids, *operands)
 
 
+def pack(slots, blocks, chunk, chunk_width):
+    owners = slots.shape[0]
+    _, pair, block_len, _ = blocks.shape
+    offset = chunk * chunk_width
+
+    def kernel(slot_ref, blocks_ref, out_ref, sems):
+        copies = []
+        for r in range(owners):
+            for k in range(2):
+                source = slot_ref[r] if k == 0 else 0
+                copy = pltpu.make_async_copy(
+                    blocks_ref.at[source, :, :, pl.ds(offset, chunk_width)],
+                    out_ref.at[r, k],
+                    sems.at[r, k],
+                )
+                copy.start()
+                copies.append(copy)
+        for copy in copies:
+            copy.wait()
+
+    return pl.pallas_call(
+        kernel,
+        grid_spec=pltpu.PrefetchScalarGridSpec(
+            num_scalar_prefetch=1,
+            grid=(1,),
+            in_specs=[pl.BlockSpec(memory_space=pl.ANY)],
+            out_specs=pl.BlockSpec(memory_space=pl.ANY),
+            scratch_shapes=[pltpu.SemaphoreType.DMA((owners, 2))],
+        ),
+        out_shape=jax.ShapeDtypeStruct(
+            (owners, 2, pair, block_len, chunk_width), blocks.dtype
+        ),
+    )(slots, blocks)
+
+
 def visibility(block_ids, limits, owners, block_len):
     tiles = block_ids.shape[0]
     sinks = block_ids[:, :NSINK]
@@ -120,15 +155,14 @@
     readers_ids = every_list[:, :, NSINK:].reshape(owners, -1)
     asked = jnp.max(jnp.where(readers_ids % owners == me, readers_ids, -1), axis=1)
     asked_slot = jnp.maximum(asked, 0) // owners
-    picks = jnp.stack([asked_slot, jnp.zeros_like(asked_slot)], axis=1).reshape(-1)
+    asked_slot = jnp.minimum(asked_slot, blocks.shape[0] - 1).astype(jnp.int32)
     bias = visibility(block_ids, key_limit[0], owners, block_len)
     chunks = CHUNKS if (width // HS) % CHUNKS == 0 else 1
     chunk_width = width // chunks
     projected = None
     for c in range(chunks):
         cols = slice(c * chunk_width, (c + 1) * chunk_width)
-        outgoing = jnp.take(blocks[..., cols], picks, axis=0, mode="clip")
-        outgoing = outgoing.reshape(owners, 2, 2, block_len, chunk_width)
+        outgoing = pack(asked_slot, blocks, c, chunk_width)
         arrived = lax.all_to_all(outgoing, "seq", split_axis=0, concat_axis=0, tiled=True)
         mixed = attention(block_ids[0, :NSINK], bias, queries[0], arrived, c)
         part = jnp.dot(mixed, weight[cols], preferred_element_type=jnp.float32)

time: 184 us -> 422 us (2.29)
  Pallas kernels: 22.5 us -> 354 us
  waiting for transfers between devices: 98.6 us -> 5.27 us
  local copies, waits for them, and re-layouts: 17.9 us -> 2.11 us
  matrix products: 11.1 us -> 18.5 us
  starting transfers between devices: 10.2 us -> 17 us
    pallas_call x0 -> x4, Pallas kernels: none -> 325 us  [pack(): pl.pallas_call(kernel, grid_spec=pltpu.PrefetchScalarGridSpec(num_scalar_...]
    all_to_all x2 -> x4, waiting for transfers between devices: 97.9 us -> 4.56 us  [shards(): lax.all_to_all(outgoing, 'seq', split_axis=0, concat_axis=0, tiled=True)]
    gather x2 -> x0, local copies, waits for them, and re-layouts: 8.39 us -> none  [shards(): outgoing = jnp.take(blocks[..., cols], picks, axis=0, mode='clip')]
    dot_general x2 -> x4, matrix products: 11.1 us -> 18.5 us  [shards(): part = jnp.dot(mixed, weight[cols], preferred_element_type=jnp.float32)]
    all_to_all x2 -> x4, starting transfers between devices: 10.2 us -> 17 us  [shards(): lax.all_to_all(outgoing, 'seq', split_axis=0, concat_axis=0, tiled=True)]
    pallas_call x2 -> x4, Pallas kernels: 22.5 us -> 29.1 us  [attention(): pl.pallas_call(kernel, grid_spec=grid_spec, out_shape=jax.ShapeDtypeStruc...]
    slice x1 -> x0, local copies, waits for them, and re-layouts: 6.13 us -> none  [shards(): outgoing = jnp.take(blocks[..., cols], picks, axis=0, mode='clip')]
  transfers between devices with their start and end apart: 3 -> 5, of which waited for: 2 -> 1; matrix products, arithmetic and copies ran while one was open for 9% -> 1% of each run, Pallas kernels for 12% -> 84%
where the time goes in v7:
time: 422 us; the launch traced here: 421 us
  Pallas kernels  354 us (84%)
  matrix products  18.5 us (4%)
  starting transfers between devices  17 us (4%)
  between operations  13.6 us (3%)
  blocking collectives  9.7 us (2%)
  waiting for transfers between devices  5.27 us (1%)
    pallas_call x4, Pallas kernels, pack(): pl.pallas_call(kernel, grid_spec=pltpu.PrefetchScalarGridSpec(num_scalar_...  325 us
    pallas_call x4, Pallas kernels, attention(): pl.pallas_call(kernel, grid_spec=grid_spec, out_shape=jax.ShapeDtypeStruc...  29.1 us
    dot_general x4, matrix products, shards(): part = jnp.dot(mixed, weight[cols], preferred_element_type=jnp.float32)  18.5 us
    all_to_all x4, starting transfers between devices, shards(): lax.all_to_all(outgoing, 'seq', split_axis=0, concat_axis=0, tiled=True)  17 us
    all_gather x1, blocking collectives, shards(): every_list = lax.all_gather(block_ids, 'seq')  9.7 us
  transfers between devices with their start and end apart: 5, of which 1 were waited for; matrix products, arithmetic and copies ran while one was open for 1% of the time, Pallas kernels for 84%

profile of v7, /device:TPU:0, one launch (start us, length us, event | category | flops | bytes accessed | tf_op | source)
XLA Modules:
  0.0 421.5 jit_solution(15619048180135582350)
XLA Ops:
  6.5 0.0 all-gather.2.cloned.1.call-start
  6.5 0.7 all-gather.2.cloned.1.call-update
  7.3 9.7 %all_gather.6 = s32[4,4,5]{2,1,0:T(4,128)S(1)} all-gather(s32[1,4,5]{2,1,0:T(4,128)} %param.8), channel_id=1, replica_groups=mesh['seq'=4,'fsdp'=8] {'seq'}, dimensions={0}, use_global_device_ids=true | all-gather | bytes 400 | tf_op jit(solution)/shard_map/all_gather | solution.py:154
  17.0 0.2 select_reduce_fusion
  17.2 0.6 fusion.12.slot_ref
  17.8 81.2 %shard_map.70 = bf16[4,2,2,128,640]{4,3,2,1,0:T(8,128)(2,1)} custom-call(s32[4]{0:T(128)} %fusion.12.slot_ref, bf16[5,2,128,2560]{3,2,1,0:T(8,128)(2,1)} %bitcast.22), custom_call_target="tpu_custom_call" | custom-call | tf_op jit(solution)/shard_map/pallas_call | solution.py:111
  99.1 3.7 all-to-all-start.3
  102.7 81.2 %shard_map.68 = bf16[4,2,2,128,640]{4,3,2,1,0:T(8,128)(2,1)} custom-call(s32[4]{0:T(128)} %fusion.12.slot_ref, bf16[5,2,128,2560]{3,2,1,0:T(8,128)(2,1)} %bitcast.23), custom_call_target="tpu_custom_call" | custom-call | tf_op jit(solution)/shard_map/pallas_call | solution.py:111
  184.0 0.0 all-to-all-done.3.refs_0_.refs_1_.refs_2_.refs_3_.refs_4_.refs_5_.refs_6_.refs_7_.refs_8_.refs_9_.refs_10_.refs_11_
  184.0 0.0 copy-start
  184.0 4.6 %all-to-all-start.2 = ((bf16[4,2,2,128,640]{4,3,2,1,0:T(8,128)(2,1)}), bf16[4,2,2,128,640]{4,3,2,1,0:T(8,128)(2,1)}, u32[]{:S(2)}, u32[]{:S(2)}) async-start(bf16[4,2,2,128,640]{4,3,2,1,0:T(8,128)(2,1)} %shard_map.68), calls=%async_computation.2 | async-start | bytes 5242880 | tf_op jit(solution)/shard_map/all_to_all | solution.py:166
  188.6 81.2 %shard_map.66 = bf16[4,2,2,128,640]{4,3,2,1,0:T(8,128)(2,1)} custom-call(s32[4]{0:T(128)} %fusion.12.slot_ref, bf16[5,2,128,2560]{3,2,1,0:T(8,128)(2,1)} %bitcast.24), custom_call_target="tpu_custom_call" | custom-call | tf_op jit(solution)/shard_map/pallas_call | solution.py:111
  269.8 0.0 copy-done
  269.9 0.0 all-to-all-done.2.refs_0_.refs_1_.refs_2_.refs_3_.refs_4_.refs_5_.refs_6_.refs_7_.refs_8_.refs_9_.refs_10_.refs_11_
  269.9 4.2 all-to-all-start.1
  274.0 0.0 copy-start.5
  274.0 0.0 copy-start.6
  274.0 0.0 copy-start.7
  274.0 81.4 %shard_map.64 = bf16[4,2,2,128,640]{4,3,2,1,0:T(8,128)(2,1)} custom-call(s32[4]{0:T(128)} %fusion.12.slot_ref, bf16[5,2,128,2560]{3,2,1,0:T(8,128)(2,1)} %bitcast.25), custom_call_target="tpu_custom_call" | custom-call | tf_op jit(solution)/shard_map/pallas_call | solution.py:111
  355.4 0.0 all-to-all-done.1.refs_0_.refs_1_.refs_2_.refs_3_.refs_4_.refs_5_.refs_6_.refs_7_.refs_8_.refs_9_.refs_10_.refs_11_
  355.4 0.0 copy-start.1
  355.4 4.6 %all-to-all-start = ((bf16[4,2,2,128,640]{4,3,2,1,0:T(8,128)(2,1)}), bf16[4,2,2,128,640]{4,3,2,1,0:T(8,128)(2,1)}, u32[]{:S(2)}, u32[]{:S(2)}) async-start(bf16[4,2,2,128,640]{4,3,2,1,0:T(8,128)(2,1)} %shard_map.64), calls=%async_computation | async-start | bytes 5242880 | tf_op jit(solution)/shard_map/all_to_all | solution.py:166
  360.0 0.0 copy-done.5
  360.0 0.1 add_select_fusion.1
  360.1 0.1 copy.7
  360.2 0.1 copy.8
  360.3 0.0 copy-done.6
  360.4 0.1 select_reduce_fusion.1
  360.4 0.5 slice_bitcast_fusion.slot_ref
  361.0 0.0 copy-done.7
  361.0 0.1 clamp_select_fusion
  361.0 0.1 broadcast_bitcast_fusion
  361.1 1.3 broadcast_in_dim.43
  362.4 7.3 %shard_map.71 = bf16[512,640]{1,0:T(8,128)(2,1)} custom-call(s32[2]{0:T(128)} %slice_bitcast_fusion.slot_ref, f32[512,768]{1,0:T(8,128)} %bitcast.30, bf16[512,2560]{1,0:T(8,128)(2,1)} %bitcast.26, bf16[4,2,2,128,640]{4,3,2,1,0:T(8,128)(2,1)} %copy-done, bf16[4,2,2,128,640]{4,3,2,1,0:T(8,128)(2,1)} %copy-done, bf16[4,2,2,128,640]{4,3,2,1,0:T(8,128)(2,1)} %copy-done, ...), custom_call_target="tpu_custom_call" | custom-call | flops 1006632960 | bytes 4849664 | tf_op jit(solution)/shard_map/pallas_call | solution.py:82
  369.7 0.0 copy-done.1
  369.7 7.2 %shard_map.69 = bf16[512,640]{1,0:T(8,128)(2,1)} custom-call(s32[2]{0:T(128)} %slice_bitcast_fusion.slot_ref, f32[512,768]{1,0:T(8,128)} %bitcast.31, bf16[512,2560]{1,0:T(8,128)(2,1)} %bitcast.27, bf16[4,2,2,128,640]{4,3,2,1,0:T(8,128)(2,1)} %all-to-all-done.2.refs_0_.refs_1_.refs_2_.refs_3_.refs_4_.refs_5_.refs_6_.refs_7_.refs_8_.refs_9_.refs_10_.refs_11_, ...), custom_call_target="tpu_custom_call" | custom-call | flops 1006632960 | bytes 4849664 | tf_op jit(solution)/shard_map/pallas_call | solution.py:82
  376.9 7.2 %shard_map.67 = bf16[512,640]{1,0:T(8,128)(2,1)} custom-call(s32[2]{0:T(128)} %slice_bitcast_fusion.slot_ref, f32[512,768]{1,0:T(8,128)} %bitcast.32, bf16[512,2560]{1,0:T(8,128)(2,1)} %bitcast.28, bf16[4,2,2,128,640]{4,3,2,1,0:T(8,128)(2,1)} %copy-done.1, bf16[4,2,2,128,640]{4,3,2,1,0:T(8,128)(2,1)} %copy-done.1, bf16[4,2,2,128,640]{4,3,2,1,0:T(8,128)(2,1)} %copy-done.1, ...), custom_call_target="tpu_custom_call" | custom-call | flops 1006632960 | bytes 4849664 | tf_op jit(solution)/shard_map/pallas_call | solution.py:82
  384.1 4.6 %all-to-all-done.refs_0_.refs_1_.refs_2_.refs_3_.refs_4_.refs_5_.refs_6_.refs_7_.refs_8_.refs_9_.refs_10_.refs_11_ = bf16[4,2,2,128,640]{4,3,2,1,0:T(8,128)(2,1)} async-done(((bf16[4,2,2,128,640]{4,3,2,1,0:T(8,128)(2,1)}), bf16[4,2,2,128,640]{4,3,2,1,0:T(8,128)(2,1)}, u32[]{:S(2)}, u32[]{:S(2)}) %all-to-all-start) | async-done | bytes 2621472 | tf_op jit(solution)/shard_map/all_to_all | solution.py:166
  388.7 7.4 %shard_map.65 = bf16[512,640]{1,0:T(8,128)(2,1)} custom-call(s32[2]{0:T(128)} %slice_bitcast_fusion.slot_ref, f32[512,768]{1,0:T(8,128)} %bitcast.33, bf16[512,2560]{1,0:T(8,128)(2,1)} %bitcast.29, bf16[4,2,2,128,640]{4,3,2,1,0:T(8,128)(2,1)} %all-to-all-done.refs_0_.refs_1_.refs_2_.refs_3_.refs_4_.refs_5_.refs_6_.refs_7_.refs_8_.refs_9_.refs_10_.refs_11_, ...), custom_call_target="tpu_custom_call" | custom-call | flops 1006632960 | bytes 4849664 | tf_op jit(solution)/shard_map/pallas_call | solution.py:82
  396.1 4.4 %fusion.6 = f32[512,2560]{1,0:T(8,128)S(1)} fusion(bf16[512,640]{1,0:T(8,128)(2,1)} %shard_map.65, bf16[2560,2560]{1,0:T(8,128)(2,1)} %all-gather.2.cloned.1.call-done), kind=kOutput, calls=%fused_computation.7 | convolution fusion | flops 1677721600 | bytes 9175040 | tf_op jit(solution)/shard_map/dot_general | solution.py:168
  400.5 0.0 copy-done.4
  400.5 0.0 copy-start.3
  400.5 4.2 fusion.4
  404.7 0.0 copy-done.3
  404.7 0.0 copy-start.2
  404.7 4.2 fusion.2
  408.9 0.0 copy-done.2
  408.9 5.7 %fusion = bf16[1,512,2560]{2,1,0:T(8,128)(2,1)} fusion(bf16[512,640]{1,0:T(8,128)(2,1)S(1)} %copy-done.2, f32[512,2560]{1,0:T(8,128)S(1)} %fusion.2, f32[512,2560]{1,0:T(8,128)S(1)} %fusion.6, f32[512,2560]{1,0:T(8,128)S(1)} %fusion.4, bf16[2560,2560]{1,0:T(8,128)(2,1)} %all-gather.2.cloned.1.call-done, f32[2560]{0:T(1024)S(1)} %reduce.1), kind=kOutput, calls=%fused_computation.1 | convolution fusion | flops 1684275200 | bytes 22292480 | tf_op jit(solution)/shard_map/dot_general | solution.py:168
  (5 shorter events, 0.0 us)
Async XLA Ops:
  6.5 389.5 %all-gather.2.cloned.1.call-start = ((), (), s32[]{:S(2)}) async-start(), calls=%async_computation.4 | async-start | bytes 14745600 | tf_op jit(solution)/shard_map/all_gather | solution.py:153
  99.1 84.9 %all-to-all-start.3 = ((bf16[4,2,2,128,640]{4,3,2,1,0:T(8,128)(2,1)}), bf16[4,2,2,128,640]{4,3,2,1,0:T(8,128)(2,1)S(1)}, u32[]{:S(2)}, u32[]{:S(2)}) async-start(bf16[4,2,2,128,640]{4,3,2,1,0:T(8,128)(2,1)} %shard_map.70), calls=%async_computation.3 | async-start | bytes 5242880 | tf_op jit(solution)/shard_map/all_to_all | solution.py:166
  184.0 85.8 %copy-start = (bf16[4,2,2,128,640]{4,3,2,1,0:T(8,128)(2,1)}, bf16[4,2,2,128,640]{4,3,2,1,0:T(8,128)(2,1)S(1)}, u32[]{:S(2)}) copy-start(bf16[4,2,2,128,640]{4,3,2,1,0:T(8,128)(2,1)S(1)} %all-to-all-done.3.refs_0_.refs_1_.refs_2_.refs_3_.refs_4_.refs_5_.refs_6_.refs_7_.refs_8_.refs_9_.refs_10_.refs_11_) | copy-start | bytes 7864324
  184.0 85.8 %all-to-all-start.2 = ((bf16[4,2,2,128,640]{4,3,2,1,0:T(8,128)(2,1)}), bf16[4,2,2,128,640]{4,3,2,1,0:T(8,128)(2,1)}, u32[]{:S(2)}, u32[]{:S(2)}) async-start(bf16[4,2,2,128,640]{4,3,2,1,0:T(8,128)(2,1)} %shard_map.68), calls=%async_computation.2 | async-start | bytes 5242880 | tf_op jit(solution)/shard_map/all_to_all | solution.py:166
  269.9 85.6 %all-to-all-start.1 = ((bf16[4,2,2,128,640]{4,3,2,1,0:T(8,128)(2,1)}), bf16[4,2,2,128,640]{4,3,2,1,0:T(8,128)(2,1)S(1)}, u32[]{:S(2)}, u32[]{:S(2)}) async-start(bf16[4,2,2,128,640]{4,3,2,1,0:T(8,128)(2,1)} %shard_map.66), calls=%async_computation.1 | async-start | bytes 5242880 | tf_op jit(solution)/shard_map/all_to_all | solution.py:166
  274.0 86.0 %copy-start.5 = (s32[1,4,5]{2,1,0:T(4,128)S(1)}, s32[1,4,5]{2,1,0:T(4,128)}, u32[]{:S(2)}) copy-start(s32[1,4,5]{2,1,0:T(4,128)} %param.8) | copy-start | bytes 244
  274.0 86.3 %copy-start.6 = (f32[1,2560]{1,0:T(1,128)S(1)}, f32[1,2560]{1,0:T(1,128)}, u32[]{:S(2)}) copy-start(f32[1,2560]{1,0:T(1,128)} %param.11) | copy-start | bytes 30724
  274.0 86.9 %copy-start.7 = (s32[1,4]{1,0:T(1,128)S(1)}, s32[1,4]{1,0:T(1,128)}, u32[]{:S(2)}) copy-start(s32[1,4]{1,0:T(1,128)} %param.9) | copy-start | bytes 52
  355.4 14.2 %copy-start.1 = (bf16[4,2,2,128,640]{4,3,2,1,0:T(8,128)(2,1)}, bf16[4,2,2,128,640]{4,3,2,1,0:T(8,128)(2,1)S(1)}, u32[]{:S(2)}) copy-start(bf16[4,2,2,128,640]{4,3,2,1,0:T(8,128)(2,1)S(1)} %all-to-all-done.1.refs_0_.refs_1_.refs_2_.refs_3_.refs_4_.refs_5_.refs_6_.refs_7_.refs_8_.refs_9_.refs_10_.refs_11_) | copy-start | bytes 7864324
  355.4 33.2 %all-to-all-start = ((bf16[4,2,2,128,640]{4,3,2,1,0:T(8,128)(2,1)}), bf16[4,2,2,128,640]{4,3,2,1,0:T(8,128)(2,1)}, u32[]{:S(2)}, u32[]{:S(2)}) async-start(bf16[4,2,2,128,640]{4,3,2,1,0:T(8,128)(2,1)} %shard_map.64), calls=%async_computation | async-start | bytes 5242880 | tf_op jit(solution)/shard_map/all_to_all | solution.py:166
  396.1 4.4 %copy-start.4 = (bf16[512,640]{1,0:T(8,128)(2,1)S(1)}, bf16[512,640]{1,0:T(8,128)(2,1)}, u32[]{:S(2)}) copy-start(bf16[512,640]{1,0:T(8,128)(2,1)} %shard_map.67) | copy-start | bytes 1966084
  400.5 4.2 copy-start.3
  404.7 4.2 copy-start.2
Sparse Core Ops, SparseCore 0:
  9.0 123.7 all-gather.1

commit v8 on v6

--- a/solution.py
+++ b/solution.py
@@ -13,26 +13,36 @@
 CHUNKS = 2
 
 
-def attention(sink_ids, bias, query_rows, arrived, chunk):
+def attention(sink_slots, bias, query_rows, candidates, arrived, chunk):
     rows = query_rows.shape[0]
-    width = arrived.shape[-1]
-    block_len = arrived.shape[3]
-    owners = arrived.shape[0]
+    owners, _, block_len, width = arrived.shape
+    held = len(candidates)
     pooled = NSINK + owners
     heads = width // HS
     group = next(g for g in GROUPS if heads % g == 0)
     span = group * HS
+    steps = heads // group
     inv_scale = 1.0 / math.sqrt(HS)
 
     def kernel(slot_ref, bias_ref, q_ref, *refs):
-        key_refs = refs[:pooled]
-        value_refs = refs[pooled : 2 * pooled]
-        out_ref = refs[2 * pooled]
+        cand_refs = refs[: 2 * held]
+        window_refs = refs[2 * held : 2 * held + 2 * owners]
+        out_ref = refs[2 * held + 2 * owners]
         mask = bias_ref[...]
         for h in range(group):
             cols = slice(h * HS, (h + 1) * HS)
-            keys = jnp.concatenate([r[:, cols] for r in key_refs], axis=0)
-            values = jnp.concatenate([r[:, cols] for r in value_refs], axis=0)
+            pools = []
+            for kv in range(2):
+                parts = []
+                for u in range(NSINK):
+                    pick = cand_refs[kv * held][:, cols]
+                    for i in range(1, held):
+                        pick = jnp.where(slot_ref[u] == i, cand_refs[kv * held + i][:, cols], pick)
+                    parts.append(pick)
+                for r in range(owners):
+                    parts.append(window_refs[kv * owners + r][:, cols])
+                pools.append(jnp.concatenate(parts, axis=0))
+            keys, values = pools
             s = lax.dot_general(
                 q_ref[:, cols], keys, (((1,), (1,)), ((), ())), preferred_element_type=jnp.float32
             )
@@ -45,31 +55,30 @@
                 out_ref.dtype
             )
 
-    def sink_spec(u, kv):
+    def cand_spec(kv):
         return pl.BlockSpec(
-            (None, None, None, block_len, span), lambda g, slot_ref: (slot_ref[u], 1, kv, 0, g)
+            (None, block_len, span), lambda g, slot_ref: (kv, 0, g + chunk * steps)
         )
 
     def window_spec(r, kv):
-        return pl.BlockSpec(
-            (None, None, None, block_len, span), lambda g, slot_ref: (r, 0, kv, 0, g)
-        )
+        return pl.BlockSpec((None, None, block_len, span), lambda g, slot_ref: (r, kv, 0, g))
 
     in_specs = [
         pl.BlockSpec((rows, pooled * block_len), lambda g, slot_ref: (0, 0)),
-        pl.BlockSpec((rows, span), lambda g, slot_ref: (0, g + chunk * (heads // group))),
+        pl.BlockSpec((rows, span), lambda g, slot_ref: (0, g + chunk * steps)),
     ]
     operands = [bias, query_rows]
     for kv in range(2):
-        for u in range(NSINK):
-            in_specs.append(sink_spec(u, kv))
-            operands.append(arrived)
+        for cand in candidates:
+            in_specs.append(cand_spec(kv))
+            operands.append(cand)
+    for kv in range(2):
         for r in range(owners):
             in_specs.append(window_spec(r, kv))
             operands.append(arrived)
     grid_spec = pltpu.PrefetchScalarGridSpec(
         num_scalar_prefetch=1,
-        grid=(heads // group,),
+        grid=(steps,),
         in_specs=in_specs,
         out_specs=pl.BlockSpec((rows, span), lambda g, slot_ref: (0, g)),
     )
@@ -85,7 +94,37 @@
         out_shape=jax.ShapeDtypeStruct((rows, width), jnp.bfloat16),
         compiler_params=pltpu.CompilerParams(dimension_semantics=("arbitrary",)),
         cost_estimate=cost,
-    )(sink_ids, *operands)
+    )(sink_slots, *operands)
+
+
+def swap(block, owners, bit):
+    return lax.ppermute(block, "seq", [(s, s ^ bit) for s in range(owners)])
+
+
+def spread_sinks(own, sinks, owners, me):
+    if owners != 4:
+        pool = lax.all_gather(own, "seq")
+        picked = [lax.dynamic_index_in_dim(pool, sinks[u], 0, False) for u in range(NSINK)]
+        return picked, jnp.arange(NSINK, dtype=jnp.int32)
+    first = swap(own, owners, 1)
+    pair = me // 2
+    in_pair = sinks // 2 == pair
+    count = jnp.sum(in_pair.astype(jnp.int32))
+    lone = jnp.where(in_pair[0], sinks[0], sinks[1])
+    relay = jnp.where((count == 1) & (lone != me), first, own)
+    second = swap(relay, owners, 2)
+    third = swap(second, owners, 1)
+    other_count = jnp.sum((sinks // 2 != pair).astype(jnp.int32))
+    slots = jnp.where(
+        sinks == me,
+        0,
+        jnp.where(
+            sinks == (me ^ 1),
+            1,
+            jnp.where((other_count == 1) | (sinks == (me ^ 2)), 2, 3),
+        ),
+    ).astype(jnp.int32)
+    return [own, first, second, third], slots
 
 
 def visibility(block_ids, limits, owners, block_len):
@@ -120,17 +159,16 @@
     readers_ids = every_list[:, :, NSINK:].reshape(owners, -1)
     asked = jnp.max(jnp.where(readers_ids % owners == me, readers_ids, -1), axis=1)
     asked_slot = jnp.maximum(asked, 0) // owners
-    picks = jnp.stack([asked_slot, jnp.zeros_like(asked_slot)], axis=1).reshape(-1)
+    candidates, sink_slots = spread_sinks(blocks[0], block_ids[0, :NSINK], owners, me)
     bias = visibility(block_ids, key_limit[0], owners, block_len)
     chunks = CHUNKS if (width // HS) % CHUNKS == 0 else 1
     chunk_width = width // chunks
     projected = None
     for c in range(chunks):
         cols = slice(c * chunk_width, (c + 1) * chunk_width)
-        outgoing = jnp.take(blocks[..., cols], picks, axis=0, mode="clip")
-        outgoing = outgoing.reshape(owners, 2, 2, block_len, chunk_width)
+        outgoing = jnp.take(blocks[..., cols], asked_slot, axis=0, mode="clip")
         arrived = lax.all_to_all(outgoing, "seq", split_axis=0, concat_axis=0, tiled=True)
-        mixed = attention(block_ids[0, :NSINK], bias, queries[0], arrived, c)
+        mixed = attention(sink_slots, bias, queries[0], candidates, arrived, c)
         part = jnp.dot(mixed, weight[cols], preferred_element_type=jnp.float32)
         projected = part if projected is None else projected + part
     return (gate[0][None, :] * projected).astype(jnp.bfloat16)[None]

time: 184 us -> 203 us (1.10)
  blocking collectives: 9.7 us -> 32.5 us
  waiting for transfers between devices: 98.6 us -> 78.9 us
  starting transfers between devices: 10.2 us -> 16.2 us
  other arithmetic: 0.54 us -> 4.94 us
  between operations: 13.5 us -> 16.1 us
    all_to_all x2, waiting for transfers between devices: 97.9 us -> 18.4 us  [shards(): lax.all_to_all(outgoing, 'seq', split_axis=0, concat_axis=0, tiled=True)]
    ppermute x0 -> x3, waiting for transfers between devices: none -> 59.8 us  [swap(): return lax.ppermute(block, 'seq', [(s, s ^ bit) for s in range(owners)])]
    all_gather x1, blocking collectives: 9.7 us -> 32.5 us  [shards(): every_list = lax.all_gather(block_ids, 'seq')]
    ppermute x0 -> x3, starting transfers between devices: none -> 7.91 us  [swap(): return lax.ppermute(block, 'seq', [(s, s ^ bit) for s in range(owners)])]
    select_n x0 -> x2, other arithmetic: none -> 3.11 us  [the longest x1 2.56 us: spread_sinks(): relay = jnp.where((count == 1) & (lone != me), first, own)]
    slice x1 -> x2, local copies, waits for them, and re-layouts: 6.13 us -> 5.84 us  [the longest x1 5.24 us: shards(): outgoing = jnp.take(blocks[..., cols], asked_slot, axis=0, mode='clip')]
  transfers between devices with their start and end apart: 3 -> 6, of which waited for: 2 -> 3; matrix products, arithmetic and copies ran while one was open for 9% -> 11% of each run, Pallas kernels for 12% -> 12%
where the time goes in v8:
time: 203 us; the launch traced here: 202 us
  waiting for transfers between devices  78.9 us (39%)
  blocking collectives  32.5 us (16%)
  Pallas kernels  23.3 us (11%)
  local copies, waits for them, and re-layouts  19.2 us (9%)
  starting transfers between devices  16.2 us (8%)
  between operations  16.1 us (8%)
  matrix products  11.1 us (5%)
  other arithmetic  4.94 us (2%)
    ppermute x3, waiting for transfers between devices, swap(): return lax.ppermute(block, 'seq', [(s, s ^ bit) for s in range(owners)])  59.8 us
    all_gather x1, blocking collectives, shards(): every_list = lax.all_gather(block_ids, 'seq')  32.5 us
    pallas_call x2, Pallas kernels, attention(): pl.pallas_call(kernel, grid_spec=grid_spec, out_shape=jax.ShapeDtypeStruc...  23.3 us
    all_to_all x2, waiting for transfers between devices, shards(): lax.all_to_all(outgoing, 'seq', split_axis=0, concat_axis=0, tiled=True)  18.4 us
    dot_general x2, matrix products, shards(): part = jnp.dot(mixed, weight[cols], preferred_element_type=jnp.float32)  11.1 us
    all_to_all x2, starting transfers between devices, shards(): lax.all_to_all(outgoing, 'seq', split_axis=0, concat_axis=0, tiled=True)  8.28 us
    ppermute x3, starting transfers between devices, swap(): return lax.ppermute(block, 'seq', [(s, s ^ bit) for s in range(owners)])  7.91 us
    gather x2, local copies, waits for them, and re-layouts, shards(): outgoing = jnp.take(blocks[..., cols], asked_slot, axis=0, mode='clip')  6.37 us
  transfers between devices with their start and end apart: 6, of which 3 were waited for; matrix products, arithmetic and copies ran while one was open for 11% of the time, Pallas kernels for 12%

profile of v8, /device:TPU:0, one launch (start us, length us, event | category | flops | bytes accessed | tf_op | source)
XLA Modules:
  0.0 202.2 jit_solution(224402018170448781)
XLA Ops:
  6.5 0.0 copy-start.3
  6.5 0.0 all-gather.2.cloned.1.call-start
  6.5 0.7 all-gather.2.cloned.1.call-update
  7.3 2.5 %slice_bitcast_fusion.refs_0_.refs_4_ = bf16[2,128,2560]{2,1,0:T(8,128)(2,1)} fusion(bf16[1,5,1,2,128,2560]{5,4,3,2,1,0:T(8,128)(2,1)} %param.7), kind=kLoop, calls=%fused_computation.8 | loop fusion | bytes 2621440 | tf_op jit(solution)/shard_map/squeeze | solution.py:162
  9.7 3.0 %collective-permute-start = (bf16[2,128,2560]{2,1,0:T(8,128)(2,1)}, bf16[2,128,2560]{2,1,0:T(8,128)(2,1)}, u32[]{:S(2)}, u32[]{:S(2)}) collective-permute-start(bf16[2,128,2560]{2,1,0:T(8,128)(2,1)} %slice_bitcast_fusion.refs_0_.refs_4_), channel_id=1, source_target_pairs={{0,8},{8,0},{16,24},{24,16},{1,9},{9,1},{17,25},{25,17},{2,10},{10... | collective-permute-start | bytes 3932168 | tf_op jit(solution)/shard_map/ppermute | solution.py:101
  12.7 0.0 copy-done.3
  12.7 32.5 %all_gather.6 = s32[4,4,5]{2,1,0:T(4,128)S(1)} all-gather(s32[1,4,5]{2,1,0:T(4,128)S(1)} %copy-done.3), channel_id=1, replica_groups=mesh['seq'=4,'fsdp'=8] {'seq'}, dimensions={0}, use_global_device_ids=true | all-gather | bytes 400 | tf_op jit(solution)/shard_map/all_gather | solution.py:158
  45.2 0.2 select_reduce_fusion
  45.4 5.2 %fusion.15 = (bf16[5,2,128,1280]{3,2,1,0:T(8,128)(2,1)S(1)}, bf16[5,2,128,1280]{3,2,1,0:T(8,128)(2,1)}) fusion(bf16[5,2,128,2560]{3,2,1,0:T(8,128)(2,1)} %bitcast.48), kind=kLoop, calls=%fused_computation.43 | loop fusion | bytes 13107200 | tf_op jit(solution)/shard_map/slice | solution.py:169
  50.7 2.2 %gather_fusion = bf16[4,2,128,1280]{3,2,1,0:T(8,128)(2,1)} fusion(bf16[5,2,128,1280]{3,2,1,0:T(8,128)(2,1)S(1)} %get-tuple-element.8, s32[1024]{0:T(1024)S(1)} %pad_clamp_fusion), kind=kCustom, calls=%fused_computation | custom fusion | bytes 5242896 | tf_op jit(solution)/shard_map/jit(_take)/gather | solution.py:169
  52.9 3.7 %all-to-all-start = ((bf16[4,2,128,1280]{3,2,1,0:T(8,128)(2,1)}), bf16[4,2,128,1280]{3,2,1,0:T(8,128)(2,1)S(1)}, u32[]{:S(2)}, u32[]{:S(2)}) async-start(bf16[4,2,128,1280]{3,2,1,0:T(8,128)(2,1)} %gather_fusion), calls=%async_computation | async-start | bytes 5242880 | tf_op jit(solution)/shard_map/all_to_all | solution.py:170
  56.6 0.6 fusion.16
  57.2 0.6 convert_reduce_fusion
  59.8 0.0 collective-permute-done.refs_1_.refs_5_
  59.8 2.6 %broadcast_select_fusion = bf16[2,128,2560]{2,1,0:T(8,128)(2,1)} fusion(bf16[2,128,2560]{2,1,0:T(8,128)(2,1)} %collective-permute-done.refs_1_.refs_5_, pred[]{:T(512)S(6)} %and.53, bf16[1,5,1,2,128,2560]{5,4,3,2,1,0:T(8,128)(2,1)} %param.7), kind=kLoop, calls=%fused_computation.9 | loop fusion | flops 655360 | bytes 3932161 | tf_op jit(solution)/shard_map/jit(_where)/select_n | solution.py:114
  62.3 2.0 collective-permute-start.1
  64.3 4.2 %gather_fusion.1 = bf16[4,2,128,1280]{3,2,1,0:T(8,128)(2,1)} fusion(bf16[5,2,128,1280]{3,2,1,0:T(8,128)(2,1)} %get-tuple-element.9, s32[1024]{0:T(1024)S(1)} %pad_clamp_fusion), kind=kCustom, calls=%fused_computation.1 | custom fusion | bytes 5242896 | tf_op jit(solution)/shard_map/jit(_take)/gather | solution.py:169
  68.5 0.0 copy-start.4
  68.5 0.0 copy-start.5
  68.5 18.4 %all-to-all-done.refs_8_.refs_9_.refs_10_.refs_11_.refs_12_.refs_13_.refs_14_.refs_15_ = bf16[4,2,128,1280]{3,2,1,0:T(8,128)(2,1)S(1)} async-done(((bf16[4,2,128,1280]{3,2,1,0:T(8,128)(2,1)}), bf16[4,2,128,1280]{3,2,1,0:T(8,128)(2,1)S(1)}, u32[]{:S(2)}, u32[]{:S(2)}) %all-to-all-start) | async-done | bytes 2621472 | tf_op jit(solution)/shard_map/all_to_all | solution.py:170
  86.9 0.0 copy-start
  86.9 1.5 copy-done
  88.4 4.6 %all-to-all-start.1 = ((bf16[4,2,128,1280]{3,2,1,0:T(8,128)(2,1)}), bf16[4,2,128,1280]{3,2,1,0:T(8,128)(2,1)}, u32[]{:S(2)}, u32[]{:S(2)}) async-start(bf16[4,2,128,1280]{3,2,1,0:T(8,128)(2,1)} %gather_fusion.1), calls=%async_computation.1 | async-start | bytes 5242880 | tf_op jit(solution)/shard_map/all_to_all | solution.py:170
  93.0 0.7 fusion.13
  94.3 34.9 %collective-permute-done.1.refs_2_.refs_6_ = bf16[2,128,2560]{2,1,0:T(8,128)(2,1)} collective-permute-done((bf16[2,128,2560]{2,1,0:T(8,128)(2,1)}, bf16[2,128,2560]{2,1,0:T(8,128)(2,1)}, u32[]{:S(2)}, u32[]{:S(2)}) %collective-permute-start.1) | collective-permute-done | bytes 1310752 | tf_op jit(solution)/shard_map/ppermute | solution.py:101
  129.1 3.0 %collective-permute-start.2 = (bf16[2,128,2560]{2,1,0:T(8,128)(2,1)}, bf16[2,128,2560]{2,1,0:T(8,128)(2,1)S(1)}, u32[]{:S(2)}, u32[]{:S(2)}) collective-permute-start(bf16[2,128,2560]{2,1,0:T(8,128)(2,1)} %collective-permute-done.1.refs_2_.refs_6_), channel_id=1, source_target_pairs={{0,8},{8,0},{16,24},{24,16},{1,9},{9,1},{17,25},{25,17},{2,10},{10... | collective-permute-start | bytes 3932168 | tf_op jit(solution)/shard_map/ppermute | solution.py:101
  132.1 0.1 add_select_fusion.1
  132.2 0.1 copy.7
  132.3 0.1 copy.8
  132.4 0.0 copy-done.4
  132.4 0.1 select_reduce_fusion.1
  132.5 0.6 compare_select_fusion.1.slot_ref
  133.1 0.0 copy-done.5
  133.1 0.1 clamp_select_fusion
  133.1 0.1 broadcast_bitcast_fusion
  133.2 24.9 %collective-permute-done.2.refs_3_.refs_7_ = bf16[2,128,2560]{2,1,0:T(8,128)(2,1)S(1)} collective-permute-done((bf16[2,128,2560]{2,1,0:T(8,128)(2,1)}, bf16[2,128,2560]{2,1,0:T(8,128)(2,1)S(1)}, u32[]{:S(2)}, u32[]{:S(2)}) %collective-permute-start.2) | collective-permute-done | bytes 1310752 | tf_op jit(solution)/shard_map/ppermute | solution.py:101
  158.2 1.4 broadcast_in_dim.62
  159.5 0.2 copy-done.1
  159.8 11.6 %shard_map.64 = bf16[512,1280]{1,0:T(8,128)(2,1)} custom-call(s32[2]{0:T(128)} %compare_select_fusion.1.slot_ref, f32[512,768]{1,0:T(8,128)} %bitcast.46, bf16[512,2560]{1,0:T(8,128)(2,1)} %bitcast.49, bf16[2,128,2560]{2,1,0:T(8,128)(2,1)} %slice_bitcast_fusion.refs_0_.refs_4_, bf16[2,128,2560]{2,1,0:T(8,128)(2,1)} %collective-permute-done.refs_1_.refs_5_, ...), custom_call_target="tpu_custom_call" | custom-call | flops 2013265920 | bytes 8126464 | tf_op jit(solution)/shard_map/pallas_call | solution.py:91
  171.4 0.0 all-to-all-done.1.refs_8_.refs_9_.refs_10_.refs_11_.refs_12_.refs_13_.refs_14_.refs_15_
  171.4 11.6 %shard_map.65 = bf16[512,1280]{1,0:T(8,128)(2,1)} custom-call(s32[2]{0:T(128)} %compare_select_fusion.1.slot_ref, f32[512,768]{1,0:T(8,128)} %bitcast.47, bf16[512,2560]{1,0:T(8,128)(2,1)} %bitcast.50, bf16[2,128,2560]{2,1,0:T(8,128)(2,1)} %slice_bitcast_fusion.refs_0_.refs_4_, bf16[2,128,2560]{2,1,0:T(8,128)(2,1)} %collective-permute-done.refs_1_.refs_5_, ...), custom_call_target="tpu_custom_call" | custom-call | flops 2013265920 | bytes 8126464 | tf_op jit(solution)/shard_map/pallas_call | solution.py:91
  183.0 0.0 copy-start.2
  183.0 0.0 all-gather.2.cloned.1.call-done
  183.1 0.0 copy-start.6
  183.1 6.2 %fusion = f32[512,2560]{1,0:T(8,128)S(1)} fusion(bf16[512,1280]{1,0:T(8,128)(2,1)} %shard_map.65, bf16[2560,2560]{1,0:T(8,128)(2,1)} %all-gather.2.cloned.1.call-done), kind=kOutput, calls=%fused_computation.2 | convolution fusion | flops 3355443200 | bytes 13107200 | tf_op jit(solution)/shard_map/dot_general | solution.py:172
  189.3 0.0 copy-done.2
  189.3 1.2 copy-done.6
  190.5 4.8 %fusion.6 = bf16[1,512,2560]{2,1,0:T(8,128)(2,1)} fusion(f32[512,2560]{1,0:T(8,128)S(1)} %fusion, bf16[512,1280]{1,0:T(8,128)(2,1)S(1)} %copy-done.2, bf16[2560,2560]{1,0:T(8,128)(2,1)S(1)} %copy-done.6, f32[2560]{0:T(1024)S(1)} %reduce.1), kind=kOutput, calls=%fused_computation.7 | convolution fusion | flops 3359375360 | bytes 15740928 | tf_op jit(solution)/shard_map/dot_general | solution.py:172
  (6 shorter events, 0.1 us)
Async XLA Ops:
  6.5 6.2 %copy-start.3 = (s32[1,4,5]{2,1,0:T(4,128)S(1)}, s32[1,4,5]{2,1,0:T(4,128)}, u32[]{:S(2)}) copy-start(s32[1,4,5]{2,1,0:T(4,128)} %param.8) | copy-start | bytes 244
  6.5 176.5 %all-gather.2.cloned.1.call-start = ((), (), s32[]{:S(2)}) async-start(), calls=%async_computation.2 | async-start | bytes 14745600 | tf_op jit(solution)/shard_map/all_gather | solution.py:157
  9.7 50.1 %collective-permute-start = (bf16[2,128,2560]{2,1,0:T(8,128)(2,1)}, bf16[2,128,2560]{2,1,0:T(8,128)(2,1)}, u32[]{:S(2)}, u32[]{:S(2)}) collective-permute-start(bf16[2,128,2560]{2,1,0:T(8,128)(2,1)} %slice_bitcast_fusion.refs_0_.refs_4_), channel_id=1, source_target_pairs={{0,8},{8,0},{16,24},{24,16},{1,9},{9,1},{17,25},{25,17},{2,10},{10... | collective-permute-start | bytes 3932168 | tf_op jit(solution)/shard_map/ppermute | solution.py:101
  52.9 34.0 %all-to-all-start = ((bf16[4,2,128,1280]{3,2,1,0:T(8,128)(2,1)}), bf16[4,2,128,1280]{3,2,1,0:T(8,128)(2,1)S(1)}, u32[]{:S(2)}, u32[]{:S(2)}) async-start(bf16[4,2,128,1280]{3,2,1,0:T(8,128)(2,1)} %gather_fusion), calls=%async_computation | async-start | bytes 5242880 | tf_op jit(solution)/shard_map/all_to_all | solution.py:170
  62.3 66.8 %collective-permute-start.1 = (bf16[2,128,2560]{2,1,0:T(8,128)(2,1)}, bf16[2,128,2560]{2,1,0:T(8,128)(2,1)}, u32[]{:S(2)}, u32[]{:S(2)}) collective-permute-start(bf16[2,128,2560]{2,1,0:T(8,128)(2,1)} %broadcast_select_fusion), channel_id=1, source_target_pairs={{0,16},{8,24},{16,0},{24,8},{1,17},{9,25},{17,1},{25,9},{2,18},{10... | collective-permute-start | bytes 3932168 | tf_op jit(solution)/shard_map/ppermute | solution.py:101
  68.5 63.9 %copy-start.4 = (f32[1,2560]{1,0:T(1,128)S(1)}, f32[1,2560]{1,0:T(1,128)}, u32[]{:S(2)}) copy-start(f32[1,2560]{1,0:T(1,128)} %param.11) | copy-start | bytes 30724
  68.5 64.6 %copy-start.5 = (s32[1,4]{1,0:T(1,128)S(1)}, s32[1,4]{1,0:T(1,128)}, u32[]{:S(2)}) copy-start(s32[1,4]{1,0:T(1,128)} %param.9) | copy-start | bytes 52
  86.9 1.5 copy-start
  88.4 83.0 %all-to-all-start.1 = ((bf16[4,2,128,1280]{3,2,1,0:T(8,128)(2,1)}), bf16[4,2,128,1280]{3,2,1,0:T(8,128)(2,1)}, u32[]{:S(2)}, u32[]{:S(2)}) async-start(bf16[4,2,128,1280]{3,2,1,0:T(8,128)(2,1)} %gather_fusion.1), calls=%async_computation.1 | async-start | bytes 5242880 | tf_op jit(solution)/shard_map/all_to_all | solution.py:170
  129.1 29.0 %collective-permute-start.2 = (bf16[2,128,2560]{2,1,0:T(8,128)(2,1)}, bf16[2,128,2560]{2,1,0:T(8,128)(2,1)S(1)}, u32[]{:S(2)}, u32[]{:S(2)}) collective-permute-start(bf16[2,128,2560]{2,1,0:T(8,128)(2,1)} %collective-permute-done.1.refs_2_.refs_6_), channel_id=1, source_target_pairs={{0,8},{8,0},{16,24},{24,16},{1,9},{9,1},{17,25},{25,17},{2,10},{10... | collective-permute-start | bytes 3932168 | tf_op jit(solution)/shard_map/ppermute | solution.py:101
  158.2 1.6 copy-start.1
  183.0 6.3 %copy-start.2 = (bf16[512,1280]{1,0:T(8,128)(2,1)S(1)}, bf16[512,1280]{1,0:T(8,128)(2,1)}, u32[]{:S(2)}) copy-start(bf16[512,1280]{1,0:T(8,128)(2,1)} %shard_map.64) | copy-start | bytes 3932164
  183.1 7.4 %copy-start.6 = (bf16[2560,2560]{1,0:T(8,128)(2,1)S(1)}, bf16[2560,2560]{1,0:T(8,128)(2,1)}, u32[]{:S(2)}) copy-start(bf16[2560,2560]{1,0:T(8,128)(2,1)} %all-gather.2.cloned.1.call-done) | copy-start | bytes 39321604
Sparse Core Ops, SparseCore 0:
  9.0 123.7 all-gather.1

commit v9 on v6

--- a/solution.py
+++ b/solution.py
@@ -10,10 +10,9 @@
 HS = 128
 NSINK = 2
 GROUPS = (5, 4, 2, 1)
-CHUNKS = 2
 
 
-def attention(sink_ids, bias, query_rows, arrived, chunk):
+def attention(sink_ids, bias, query_rows, arrived, col_start):
     rows = query_rows.shape[0]
     width = arrived.shape[-1]
     block_len = arrived.shape[3]
@@ -57,7 +56,7 @@
 
     in_specs = [
         pl.BlockSpec((rows, pooled * block_len), lambda g, slot_ref: (0, 0)),
-        pl.BlockSpec((rows, span), lambda g, slot_ref: (0, g + chunk * (heads // group))),
+        pl.BlockSpec((rows, span), lambda g, slot_ref: (0, g + col_start // span)),
     ]
     operands = [bias, query_rows]
     for kv in range(2):
@@ -122,15 +121,19 @@
     asked_slot = jnp.maximum(asked, 0) // owners
     picks = jnp.stack([asked_slot, jnp.zeros_like(asked_slot)], axis=1).reshape(-1)
     bias = visibility(block_ids, key_limit[0], owners, block_len)
-    chunks = CHUNKS if (width // HS) % CHUNKS == 0 else 1
-    chunk_width = width // chunks
+    heads = width // HS
+    tail_heads = heads // 4 if heads % 20 == 0 else heads
+    bounds = [(0, heads - tail_heads), (heads - tail_heads, heads)]
+    bounds = [(lo * HS, hi * HS) for lo, hi in bounds if hi > lo]
     projected = None
-    for c in range(chunks):
-        cols = slice(c * chunk_width, (c + 1) * chunk_width)
+    for lo, hi in bounds:
+        cols = slice(lo, hi)
         outgoing = jnp.take(blocks[..., cols], picks, axis=0, mode="clip")
-        outgoing = outgoing.reshape(owners, 2, 2, block_len, chunk_width)
+        outgoing = outgoing.reshape(owners, 2, 2, block_len, hi - lo)
         arrived = lax.all_to_all(outgoing, "seq", split_axis=0, concat_axis=0, tiled=True)
-        mixed = attention(block_ids[0, :NSINK], bias, queries[0], arrived, c)
+        if projected is not None:
+            projected, arrived = lax.optimization_barrier((projected, arrived))
+        mixed = attention(block_ids[0, :NSINK], bias, queries[0], arrived, lo)
         part = jnp.dot(mixed, weight[cols], preferred_element_type=jnp.float32)
         projected = part if projected is None else projected + part
     return (gate[0][None, :] * projected).astype(jnp.bfloat16)[None]

time: 184 us -> 177 us (0.962)
  waiting for transfers between devices: 98.6 us -> 84.2 us
  matrix products: 11.1 us -> 17.7 us
  local copies, waits for them, and re-layouts: 17.9 us -> 20 us
    all_to_all x2, waiting for transfers between devices: 97.9 us -> 83.5 us  [shards(): lax.all_to_all(outgoing, 'seq', split_axis=0, concat_axis=0, tiled=True)]
    dot_general x2, matrix products: 11.1 us -> 17.7 us  [shards(): part = jnp.dot(mixed, weight[cols], preferred_element_type=jnp.float32)]
    slice x1 -> x2, local copies, waits for them, and re-layouts: 6.13 us -> 6.7 us  [shards(): outgoing = jnp.take(blocks[..., cols], picks, axis=0, mode='clip')]
  transfers between devices with their start and end apart: 3 -> 3, of which waited for: 2 -> 2; matrix products, arithmetic and copies ran while one was open for 9% -> 17% of each run, Pallas kernels for 12% -> 8%
where the time goes in v9:
time: 177 us
  waiting for transfers between devices  84.2 us (48%)
  Pallas kernels  22.1 us (12%)
  local copies, waits for them, and re-layouts  20 us (11%)
  matrix products  17.7 us (10%)
  between operations  13.5 us (8%)
  blocking collectives  9.56 us (5%)
  starting transfers between devices  9.33 us (5%)
    all_to_all x2, waiting for transfers between devices, shards(): lax.all_to_all(outgoing, 'seq', split_axis=0, concat_axis=0, tiled=True)  83.5 us
    pallas_call x2, Pallas kernels, attention(): pl.pallas_call(kernel, grid_spec=grid_spec, out_shape=jax.ShapeDtypeStruc...  22.1 us
    dot_general x2, matrix products, shards(): part = jnp.dot(mixed, weight[cols], preferred_element_type=jnp.float32)  17.7 us
    gather x2, local copies, waits for them, and re-layouts, shards(): outgoing = jnp.take(blocks[..., cols], picks, axis=0, mode='clip')  9.59 us
    all_gather x1, blocking collectives, shards(): every_list = lax.all_gather(block_ids, 'seq')  9.56 us
    all_to_all x2, starting transfers between devices, shards(): lax.all_to_all(outgoing, 'seq', split_axis=0, concat_axis=0, tiled=True)  9.33 us
    slice x2, local copies, waits for them, and re-layouts, shards(): outgoing = jnp.take(blocks[..., cols], picks, axis=0, mode='clip')  6.7 us
  transfers between devices with their start and end apart: 3, of which 2 were waited for; matrix products, arithmetic and copies ran while one was open for 17% of the time, Pallas kernels for 8%

profile of v9, /device:TPU:0, one launch (start us, length us, event | category | flops | bytes accessed | tf_op | source)
XLA Modules:
  0.0 177.0 jit_solution(7975234054386314273)
XLA Ops:
  6.5 0.0 all-gather.2.cloned.1.call-start
  6.5 0.7 all-gather.2.cloned.1.call-update
  7.3 0.0 copy-start.1
  7.3 5.1 %slice.37 = bf16[5,2,128,1920]{3,2,1,0:T(8,128)(2,1)} slice(bf16[5,2,128,2560]{3,2,1,0:T(8,128)(2,1)} %bitcast.32), slice={[0:5], [0:2], [0:128], [0:1920]} | slice | bytes 9830400 | tf_op jit(solution)/shard_map/slice | solution.py:131
  12.4 0.0 copy-done.1
  12.4 9.6 %all_gather.6 = s32[4,4,5]{2,1,0:T(4,128)S(1)} all-gather(s32[1,4,5]{2,1,0:T(4,128)S(1)} %copy-done.1), channel_id=1, replica_groups=mesh['seq'=4,'fsdp'=8] {'seq'}, dimensions={0}, use_global_device_ids=true | all-gather | bytes 400 | tf_op jit(solution)/shard_map/all_gather | solution.py:118
  21.9 0.2 select_reduce_fusion
  22.2 0.1 copy.13
  22.3 0.1 reshape.133
  22.4 7.2 %gather_fusion = bf16[8,2,128,1920]{3,2,1,0:T(8,128)(2,1)} fusion(bf16[5,2,128,1920]{3,2,1,0:T(8,128)(2,1)} %slice.37, s32[1024]{0:T(1024)S(1)} %pad_clamp_fusion), kind=kCustom, calls=%fused_computation | custom fusion | bytes 15728672 | tf_op jit(solution)/shard_map/jit(_take)/gather | solution.py:131
  29.6 5.5 %all-to-all-start = ((bf16[4,2,2,128,1920]{4,3,2,1,0:T(8,128)(2,1)}), bf16[4,2,2,128,1920]{4,3,2,1,0:T(8,128)(2,1)}, u32[]{:S(2)}, u32[]{:S(2)}) async-start(bf16[4,2,2,128,1920]{4,3,2,1,0:T(8,128)(2,1)} %bitcast.26), calls=%async_computation | async-start | bytes 15728640 | tf_op jit(solution)/shard_map/all_to_all | solution.py:133
  35.1 0.0 copy-start.3
  35.1 1.6 slice.40
  36.7 0.1 add_select_fusion.1
  36.8 0.1 copy.10
  36.9 0.1 copy.11
  37.0 0.0 copy-start.2
  37.0 2.4 %gather_fusion.1 = bf16[8,2,128,640]{3,2,1,0:T(8,128)(2,1)} fusion(bf16[5,2,128,640]{3,2,1,0:T(8,128)(2,1)S(1)} %slice.40, s32[1024]{0:T(1024)S(1)} %pad_clamp_fusion), kind=kCustom, calls=%fused_computation.1 | custom fusion | bytes 5242912 | tf_op jit(solution)/shard_map/jit(_take)/gather | solution.py:131
  39.4 0.1 select_reduce_fusion.1
  39.4 0.0 copy-done.3
  39.5 0.1 clamp_select_fusion
  39.5 0.1 broadcast_bitcast_fusion
  39.6 80.8 %all-to-all-done.refs_0_.refs_1_.refs_2_.refs_3_.refs_4_.refs_5_.refs_6_.refs_7_.refs_8_.refs_9_.refs_10_.refs_11_ = bf16[4,2,2,128,1920]{4,3,2,1,0:T(8,128)(2,1)} async-done(((bf16[4,2,2,128,1920]{4,3,2,1,0:T(8,128)(2,1)}), bf16[4,2,2,128,1920]{4,3,2,1,0:T(8,128)(2,1)}, u32[]{:S(2)}, u32[]{:S(2)}) %all-to-all-start) | async-done | bytes 7864352 | tf_op jit(solution)/shard_map/all_to_all | solution.py:133
  120.4 3.8 %all-to-all-start.1 = ((bf16[4,2,2,128,640]{4,3,2,1,0:T(8,128)(2,1)}), bf16[4,2,2,128,640]{4,3,2,1,0:T(8,128)(2,1)S(1)}, u32[]{:S(2)}, u32[]{:S(2)}) async-start(bf16[4,2,2,128,640]{4,3,2,1,0:T(8,128)(2,1)} %bitcast.31), calls=%async_computation.1 | async-start | bytes 5242880 | tf_op jit(solution)/shard_map/all_to_all | solution.py:133
  124.2 0.5 slice_bitcast_fusion.slot_ref
  124.7 0.0 copy-done.2
  124.8 1.3 broadcast_in_dim.49
  126.1 14.9 %shard_map.64 = bf16[512,1920]{1,0:T(8,128)(2,1)} custom-call(s32[2]{0:T(128)} %slice_bitcast_fusion.slot_ref, f32[512,768]{1,0:T(8,128)} %bitcast.27, bf16[512,2560]{1,0:T(8,128)(2,1)} %bitcast.29, bf16[4,2,2,128,1920]{4,3,2,1,0:T(8,128)(2,1)} %all-to-all-done.refs_0_.refs_1_.refs_2_.refs_3_.refs_4_.refs_5_.refs_6_.refs_7_.refs_8_.refs_9_.refs_10_.refs_11_, ...), custom_call_target="tpu_custom_call" | custom-call | flops 3019898880 | bytes 11403264 | tf_op jit(solution)/shard_map/pallas_call | solution.py:81
  141.0 0.0 all-gather.2.cloned.1.call-done
  141.0 10.3 %fusion = f32[512,2560]{1,0:T(8,128)} fusion(bf16[512,1920]{1,0:T(8,128)(2,1)} %shard_map.64, bf16[2560,2560]{1,0:T(8,128)(2,1)} %all-gather.2.cloned.1.call-done), kind=kOutput, calls=%fused_computation.2 | convolution fusion | flops 5033164800 | bytes 17039360 | tf_op jit(solution)/shard_map/dot_general | solution.py:137
  151.3 2.7 %all-to-all-done.1.refs_0_.refs_1_.refs_2_.refs_3_.refs_4_.refs_5_.refs_6_.refs_7_.refs_8_.refs_9_.refs_10_.refs_11_ = bf16[4,2,2,128,640]{4,3,2,1,0:T(8,128)(2,1)S(1)} async-done(((bf16[4,2,2,128,640]{4,3,2,1,0:T(8,128)(2,1)}), bf16[4,2,2,128,640]{4,3,2,1,0:T(8,128)(2,1)S(1)}, u32[]{:S(2)}, u32[]{:S(2)}) %all-to-all-start.1) | async-done | bytes 2621472 | tf_op jit(solution)/shard_map/all_to_all | solution.py:133
  154.0 0.0 copy-start
  154.0 1.5 copy-done
  155.5 7.2 %shard_map.65 = bf16[512,640]{1,0:T(8,128)(2,1)} custom-call(s32[2]{0:T(128)} %slice_bitcast_fusion.slot_ref, f32[512,768]{1,0:T(8,128)} %bitcast.28, bf16[512,2560]{1,0:T(8,128)(2,1)} %bitcast.30, bf16[4,2,2,128,640]{4,3,2,1,0:T(8,128)(2,1)} %copy-done, bf16[4,2,2,128,640]{4,3,2,1,0:T(8,128)(2,1)} %copy-done, bf16[4,2,2,128,640]{4,3,2,1,0:T(8,128)(2,1)} %copy-done, ...), custom_call_target="tpu_custom_call" | custom-call | flops 1006632960 | bytes 4849664 | tf_op jit(solution)/shard_map/pallas_call | solution.py:81
  162.7 7.4 %fusion.2 = bf16[1,512,2560]{2,1,0:T(8,128)(2,1)} fusion(f32[512,2560]{1,0:T(8,128)} %fusion, bf16[512,640]{1,0:T(8,128)(2,1)} %shard_map.65, bf16[2560,2560]{1,0:T(8,128)(2,1)} %all-gather.2.cloned.1.call-done, f32[2560]{0:T(1024)S(1)} %reduce.1), kind=kOutput, calls=%fused_computation.5 | convolution fusion | flops 1681653760 | bytes 11806720 | tf_op jit(solution)/shard_map/dot_general | solution.py:137
  (6 shorter events, 0.1 us)
Async XLA Ops:
  6.5 134.4 %all-gather.2.cloned.1.call-start = ((), (), s32[]{:S(2)}) async-start(), calls=%async_computation.2 | async-start | bytes 14745600 | tf_op jit(solution)/shard_map/all_gather | solution.py:117
  7.3 5.1 %copy-start.1 = (s32[1,4,5]{2,1,0:T(4,128)S(1)}, s32[1,4,5]{2,1,0:T(4,128)}, u32[]{:S(2)}) copy-start(s32[1,4,5]{2,1,0:T(4,128)} %param.8) | copy-start | bytes 244
  29.6 90.8 %all-to-all-start = ((bf16[4,2,2,128,1920]{4,3,2,1,0:T(8,128)(2,1)}), bf16[4,2,2,128,1920]{4,3,2,1,0:T(8,128)(2,1)}, u32[]{:S(2)}, u32[]{:S(2)}) async-start(bf16[4,2,2,128,1920]{4,3,2,1,0:T(8,128)(2,1)} %bitcast.26), calls=%async_computation | async-start | bytes 15728640 | tf_op jit(solution)/shard_map/all_to_all | solution.py:133
  35.1 4.3 %copy-start.3 = (s32[1,4]{1,0:T(1,128)S(1)}, s32[1,4]{1,0:T(1,128)}, u32[]{:S(2)}) copy-start(s32[1,4]{1,0:T(1,128)} %param.9) | copy-start | bytes 52
  37.0 87.7 %copy-start.2 = (f32[1,2560]{1,0:T(1,128)S(1)}, f32[1,2560]{1,0:T(1,128)}, u32[]{:S(2)}) copy-start(f32[1,2560]{1,0:T(1,128)} %param.11) | copy-start | bytes 30724
  120.4 33.6 %all-to-all-start.1 = ((bf16[4,2,2,128,640]{4,3,2,1,0:T(8,128)(2,1)}), bf16[4,2,2,128,640]{4,3,2,1,0:T(8,128)(2,1)S(1)}, u32[]{:S(2)}, u32[]{:S(2)}) async-start(bf16[4,2,2,128,640]{4,3,2,1,0:T(8,128)(2,1)} %bitcast.31), calls=%async_computation.1 | async-start | bytes 5242880 | tf_op jit(solution)/shard_map/all_to_all | solution.py:133
  154.0 1.5 copy-start
Sparse Core Ops, SparseCore 0:
  9.0 123.7 all-gather.1

commit v10 on v9

--- a/solution.py
+++ b/solution.py
@@ -115,10 +115,15 @@
     block_len = blocks.shape[2]
     width = blocks.shape[3]
     weight = lax.all_gather(out_weight, "fsdp", axis=0, tiled=True)
-    every_list = lax.all_gather(block_ids, "seq")
-    readers_ids = every_list[:, :, NSINK:].reshape(owners, -1)
+    window_ids = block_ids[:, NSINK:].reshape(-1)
+    lists = [window_ids]
+    for shift in range(1, owners):
+        lists.append(lax.ppermute(window_ids, "seq", [(s, (s + shift) % owners) for s in range(owners)]))
+    by_reader = jnp.stack(lists)
+    readers = (me - jnp.arange(owners, dtype=jnp.int32)) % owners
+    readers_ids = jnp.zeros_like(by_reader).at[readers].set(by_reader)
     asked = jnp.max(jnp.where(readers_ids % owners == me, readers_ids, -1), axis=1)
-    asked_slot = jnp.maximum(asked, 0) // owners
+    asked_slot = jnp.minimum(jnp.maximum(asked, 0) // owners, blocks.shape[0] - 1)
     picks = jnp.stack([asked_slot, jnp.zeros_like(asked_slot)], axis=1).reshape(-1)
     bias = visibility(block_ids, key_limit[0], owners, block_len)
     heads = width // HS
@@ -128,8 +133,9 @@
     projected = None
     for lo, hi in bounds:
         cols = slice(lo, hi)
-        outgoing = jnp.take(blocks[..., cols], picks, axis=0, mode="clip")
-        outgoing = outgoing.reshape(owners, 2, 2, block_len, hi - lo)
+        outgoing = jnp.stack(
+            [lax.dynamic_index_in_dim(blocks, picks[i], 0, False)[..., cols] for i in range(2 * owners)]
+        ).reshape(owners, 2, 2, block_len, hi - lo)
         arrived = lax.all_to_all(outgoing, "seq", split_axis=0, concat_axis=0, tiled=True)
         if projected is not None:
             projected, arrived = lax.optimization_barrier((projected, arrived))

time: 177 us -> 193 us (1.090)
  between operations: 13.5 us -> 28.8 us
  blocking collectives: 9.56 us -> 0 us
  local copies, waits for them, and re-layouts: 20 us -> 27.7 us
  starting transfers between devices: 9.33 us -> 15.6 us
  waiting for transfers between devices: 84.2 us -> 78.4 us
    unnamed x10 -> x38, local copies, waits for them, and re-layouts: 1.67 us -> 18.8 us
    gather x2 -> x0, local copies, waits for them, and re-layouts: 9.59 us -> none  [shards(): outgoing = jnp.take(blocks[..., cols], picks, axis=0, mode='clip')]
    all_gather x1 -> x0, blocking collectives: 9.56 us -> none  [shards(): every_list = lax.all_gather(block_ids, 'seq')]
    all_to_all x2, waiting for transfers between devices: 83.5 us -> 75.6 us  [shards(): lax.all_to_all(outgoing, 'seq', split_axis=0, concat_axis=0, tiled=True)]
    slice x2 -> x1, local copies, waits for them, and re-layouts: 6.7 us -> 0.69 us  [shards(): picks[i]]
    ppermute x0 -> x3, starting transfers between devices: none -> 5.92 us  [shards(): lax.ppermute(window_ids, 'seq', [(s, (s + shift) % owners) for s in range...]
    squeeze x0 -> x1, local copies, waits for them, and re-layouts: none -> 5.01 us  [shards(): lax.dynamic_index_in_dim(blocks, picks[i], 0, False)[..., cols]]
    ppermute x0 -> x3, waiting for transfers between devices: none -> 2.03 us  [shards(): lax.ppermute(window_ids, 'seq', [(s, (s + shift) % owners) for s in range...]
  transfers between devices with their start and end apart: 3 -> 6, of which waited for: 2 -> 4; matrix products, arithmetic and copies ran while one was open for 17% -> 17% of each run, Pallas kernels for 8% -> 8%
where the time goes in v10:
time: 193 us; the launch traced here: 192 us
  waiting for transfers between devices  78.4 us (41%)
  between operations  28.8 us (15%)
  local copies, waits for them, and re-layouts  27.7 us (14%)
  Pallas kernels  22.1 us (11%)
  matrix products  17.7 us (9%)
  starting transfers between devices  15.6 us (8%)
    all_to_all x2, waiting for transfers between devices, shards(): lax.all_to_all(outgoing, 'seq', split_axis=0, concat_axis=0, tiled=True)  75.6 us
    pallas_call x2, Pallas kernels, attention(): pl.pallas_call(kernel, grid_spec=grid_spec, out_shape=jax.ShapeDtypeStruc...  22.1 us
    unnamed x38, local copies, waits for them, and re-layouts  18.8 us
    dot_general x2, matrix products, shards(): part = jnp.dot(mixed, weight[cols], preferred_element_type=jnp.float32)  17.7 us
    all_to_all x2, starting transfers between devices, shards(): lax.all_to_all(outgoing, 'seq', split_axis=0, concat_axis=0, tiled=True)  9.67 us
    ppermute x3, starting transfers between devices, shards(): lax.ppermute(window_ids, 'seq', [(s, (s + shift) % owners) for s in range...  5.92 us
    squeeze x1, local copies, waits for them, and re-layouts, shards(): lax.dynamic_index_in_dim(blocks, picks[i], 0, False)[..., cols]  5.01 us
  transfers between devices with their start and end apart: 6, of which 4 were waited for; matrix products, arithmetic and copies ran while one was open for 17% of the time, Pallas kernels for 8%

profile of v10, /device:TPU:0, one launch (start us, length us, event | category | flops | bytes accessed | tf_op | source)
XLA Modules:
  0.0 191.9 jit_solution(18308723125994123630)
XLA Ops:
  6.5 0.7 all-gather.2.cloned.1.call-update
  7.3 0.8 add_select_fusion.1
  8.1 3.0 %collective-permute-start = (s32[12]{0:T(128)S(1)}, s32[12]{0:T(128)S(1)}, u32[]{:S(2)}, u32[]{:S(2)}) collective-permute-start(s32[12]{0:T(128)S(1)} %reshape.200), channel_id=1, source_target_pairs={{0,8},{8,16},{16,24},{24,0},{1,9},{9,17},{17,25},{25,1},{2,10},{10... | collective-permute-start | bytes 152 | tf_op jit(solution)/shard_map/ppermute | solution.py:121
  11.1 1.5 collective-permute-start.1
  12.6 1.4 collective-permute-start.2
  14.1 0.5 collective-permute-done.1
  14.6 1.5 collective-permute-done.2
  16.2 0.6 scatter_custom_fusion
  16.8 0.1 select_reduce_fusion.1
  16.9 0.1 copy.12
  17.0 0.1 reshape.201
  17.1 0.7 fusion.36
  33.0 5.0 %dynamic-slice_bitcast_fusion = (bf16[2,128,2560]{2,1,0:T(8,128)(2,1)S(1)}, bf16[2,128,2560]{2,1,0:T(8,128)(2,1)S(1)}, bf16[2,128,2560]{2,1,0:T(8,128)(2,1)S(1)}...) fusion(bf16[1,5,1,2,128,2560]{5,4,3,2,1,0:T(8,128)(2,1)} %param, ...), kind=kLoop, calls=%fused_computation.6 | loop fusion | bytes 20971552 | tf_op jit(solution)/shard_map/jit(dynamic_index_in_dim)/squeeze | solution.py:137
  38.1 0.1 fusion.10
  38.3 0.1 fusion.9
  38.4 0.7 copy-done.5
  39.1 0.4 copy-done.4
  39.5 0.1 fusion.8
  39.6 0.3 copy-done.3
  39.9 0.1 fusion.7
  40.0 0.3 copy-done.2
  40.3 0.1 fusion.6
  40.5 0.1 fusion.5
  40.6 0.1 fusion.4
  40.7 0.4 copy-done.7
  41.1 3.1 %copy-done.1 = bf16[8,2,128,1920]{3,2,1,0:T(8,128)(2,1)} copy-done((bf16[8,2,128,1920]{3,2,1,0:T(8,128)(2,1)}, bf16[8,2,128,1920]{3,2,1,0:T(8,128)(2,1)S(1)}, u32[]{:S(2)}) %copy-start.1) | copy-done | bytes 7864344
  44.3 5.7 %all-to-all-start = ((bf16[4,2,2,128,1920]{4,3,2,1,0:T(8,128)(2,1)}), bf16[4,2,2,128,1920]{4,3,2,1,0:T(8,128)(2,1)}, u32[]{:S(2)}, u32[]{:S(2)}) async-start(bf16[4,2,2,128,1920]{4,3,2,1,0:T(8,128)(2,1)} %bitcast.126), calls=%async_computation | async-start | bytes 15728640 | tf_op jit(solution)/shard_map/all_to_all | solution.py:139
  50.0 0.1 copy.10
  50.1 0.1 copy.9
  50.2 0.1 select_reduce_fusion
  50.4 1.7 fusion.19
  52.1 1.7 fusion.18
  53.9 1.7 fusion.17
  55.6 1.7 fusion.16
  57.3 1.7 fusion.15
  59.0 1.7 fusion.14
  60.8 0.8 fusion.13
  61.5 0.8 fusion.12
  62.3 73.0 %all-to-all-done.refs_0_.refs_1_.refs_2_.refs_3_.refs_4_.refs_5_.refs_6_.refs_7_.refs_8_.refs_9_.refs_10_.refs_11_ = bf16[4,2,2,128,1920]{4,3,2,1,0:T(8,128)(2,1)} async-done(((bf16[4,2,2,128,1920]{4,3,2,1,0:T(8,128)(2,1)}), bf16[4,2,2,128,1920]{4,3,2,1,0:T(8,128)(2,1)}, u32[]{:S(2)}, u32[]{:S(2)}) %all-to-all-start) | async-done | bytes 7864352 | tf_op jit(solution)/shard_map/all_to_all | solution.py:139
  135.2 4.0 %all-to-all-start.1 = ((bf16[4,2,2,128,640]{4,3,2,1,0:T(8,128)(2,1)}), bf16[4,2,2,128,640]{4,3,2,1,0:T(8,128)(2,1)S(1)}, u32[]{:S(2)}, u32[]{:S(2)}) async-start(bf16[4,2,2,128,640]{4,3,2,1,0:T(8,128)(2,1)} %bitcast.45), calls=%async_computation.1 | async-start | bytes 5242880 | tf_op jit(solution)/shard_map/all_to_all | solution.py:139
  139.2 0.6 slice_bitcast_fusion.16.slot_ref
  139.9 1.3 broadcast_in_dim.47
  141.1 14.9 %shard_map.64 = bf16[512,1920]{1,0:T(8,128)(2,1)} custom-call(s32[2]{0:T(128)} %slice_bitcast_fusion.16.slot_ref, f32[512,768]{1,0:T(8,128)} %bitcast.122, bf16[512,2560]{1,0:T(8,128)(2,1)} %bitcast.124, bf16[4,2,2,128,1920]{4,3,2,1,0:T(8,128)(2,1)} %all-to-all-done.refs_0_.refs_1_.refs_2_.refs_3_.refs_4_.refs_5_.refs_6_.refs_7_.refs_8_.refs_9_.refs_10_.refs_11_, ...), custom_call_target="tpu_custom_call" | custom-call | flops 3019898880 | bytes 11403264 | tf_op jit(solution)/shard_map/pallas_call | solution.py:81
  156.0 10.3 %fusion = f32[512,2560]{1,0:T(8,128)} fusion(bf16[512,1920]{1,0:T(8,128)(2,1)} %shard_map.64, bf16[2560,2560]{1,0:T(8,128)(2,1)} %all-gather.2.cloned.1.call-done), kind=kOutput, calls=%fused_computation.1 | convolution fusion | flops 5033164800 | bytes 17039360 | tf_op jit(solution)/shard_map/dot_general | solution.py:143
  166.3 2.7 %all-to-all-done.1.refs_0_.refs_1_.refs_2_.refs_3_.refs_4_.refs_5_.refs_6_.refs_7_.refs_8_.refs_9_.refs_10_.refs_11_ = bf16[4,2,2,128,640]{4,3,2,1,0:T(8,128)(2,1)S(1)} async-done(((bf16[4,2,2,128,640]{4,3,2,1,0:T(8,128)(2,1)}), bf16[4,2,2,128,640]{4,3,2,1,0:T(8,128)(2,1)S(1)}, u32[]{:S(2)}, u32[]{:S(2)}) %all-to-all-start.1) | async-done | bytes 2621472 | tf_op jit(solution)/shard_map/all_to_all | solution.py:139
  169.0 1.5 copy-done
  170.5 7.2 %shard_map.65 = bf16[512,640]{1,0:T(8,128)(2,1)} custom-call(s32[2]{0:T(128)} %slice_bitcast_fusion.16.slot_ref, f32[512,768]{1,0:T(8,128)} %bitcast.123, bf16[512,2560]{1,0:T(8,128)(2,1)} %bitcast.125, bf16[4,2,2,128,640]{4,3,2,1,0:T(8,128)(2,1)} %copy-done, bf16[4,2,2,128,640]{4,3,2,1,0:T(8,128)(2,1)} %copy-done, bf16[4,2,2,128,640]{4,3,2,1,0:T(8,128)(2,1)} %copy-done, ...), custom_call_target="tpu_custom_call" | custom-call | flops 1006632960 | bytes 4849664 | tf_op jit(solution)/shard_map/pallas_call | solution.py:81
  177.7 7.4 %fusion.2 = bf16[1,512,2560]{2,1,0:T(8,128)(2,1)} fusion(f32[512,2560]{1,0:T(8,128)} %fusion, bf16[512,640]{1,0:T(8,128)(2,1)} %shard_map.65, bf16[2560,2560]{1,0:T(8,128)(2,1)} %all-gather.2.cloned.1.call-done, f32[2560]{0:T(1024)S(1)} %reduce), kind=kOutput, calls=%fused_computation.4 | convolution fusion | flops 1681653760 | bytes 11806720 | tf_op jit(solution)/shard_map/dot_general | solution.py:143
  (29 shorter events, 0.5 us)
Async XLA Ops:
  6.5 149.5 %all-gather.2.cloned.1.call-start = ((), (), s32[]{:S(2)}) async-start(), calls=%async_computation.2 | async-start | bytes 14745600 | tf_op jit(solution)/shard_map/all_gather | solution.py:117
  8.1 6.0 %collective-permute-start = (s32[12]{0:T(128)S(1)}, s32[12]{0:T(128)S(1)}, u32[]{:S(2)}, u32[]{:S(2)}) collective-permute-start(s32[12]{0:T(128)S(1)} %reshape.200), channel_id=1, source_target_pairs={{0,8},{8,16},{16,24},{24,0},{1,9},{9,17},{17,25},{25,1},{2,10},{10... | collective-permute-start | bytes 152 | tf_op jit(solution)/shard_map/ppermute | solution.py:121
  11.1 3.6 %collective-permute-start.1 = (s32[12]{0:T(128)S(1)}, s32[12]{0:T(128)S(1)}, u32[]{:S(2)}, u32[]{:S(2)}) collective-permute-start(s32[12]{0:T(128)S(1)} %reshape.200), channel_id=1, source_target_pairs={{0,16},{8,24},{16,0},{24,8},{1,17},{9,25},{17,1},{25,9},{2,18},{10... | collective-permute-start | bytes 152 | tf_op jit(solution)/shard_map/ppermute | solution.py:121
  12.6 3.6 %collective-permute-start.2 = (s32[12]{0:T(128)S(1)}, s32[12]{0:T(128)S(1)}, u32[]{:S(2)}, u32[]{:S(2)}) collective-permute-start(s32[12]{0:T(128)S(1)} %reshape.200), channel_id=1, source_target_pairs={{0,24},{8,0},{16,8},{24,16},{1,25},{9,1},{17,9},{25,17},{2,26},{10... | collective-permute-start | bytes 152 | tf_op jit(solution)/shard_map/ppermute | solution.py:121
  38.0 1.1 copy-start.5
  38.0 1.5 copy-start.4
  38.0 1.9 copy-start.3
  38.0 2.3 %copy-start.2 = (bf16[2,128,2560]{2,1,0:T(8,128)(2,1)}, bf16[2,128,2560]{2,1,0:T(8,128)(2,1)S(1)}, u32[]{:S(2)}) copy-start(bf16[2,128,2560]{2,1,0:T(8,128)(2,1)S(1)} %get-tuple-element.10) | copy-start | bytes 3932164
  38.0 2.7 %copy-start.6 = (bf16[2,128,2560]{2,1,0:T(8,128)(2,1)}, bf16[2,128,2560]{2,1,0:T(8,128)(2,1)S(1)}, u32[]{:S(2)}) copy-start(bf16[2,128,2560]{2,1,0:T(8,128)(2,1)S(1)} %get-tuple-element.14) | copy-start | bytes 3932164
  38.0 3.1 %copy-start.7 = (bf16[2,128,2560]{2,1,0:T(8,128)(2,1)}, bf16[2,128,2560]{2,1,0:T(8,128)(2,1)S(1)}, u32[]{:S(2)}) copy-start(bf16[2,128,2560]{2,1,0:T(8,128)(2,1)S(1)} %get-tuple-element.15) | copy-start | bytes 3932164
  41.1 3.1 %copy-start.1 = (bf16[8,2,128,1920]{3,2,1,0:T(8,128)(2,1)}, bf16[8,2,128,1920]{3,2,1,0:T(8,128)(2,1)S(1)}, u32[]{:S(2)}) copy-start(bf16[8,2,128,1920]{3,2,1,0:T(8,128)(2,1)S(1)} %fusion.4) | copy-start | bytes 23592964
  44.2 6.0 %copy-start.9 = (s32[1,4,5]{2,1,0:T(4,128)S(1)}, s32[1,4,5]{2,1,0:T(4,128)}, u32[]{:S(2)}) copy-start(s32[1,4,5]{2,1,0:T(4,128)} %param.8) | copy-start | bytes 244
  44.3 6.0 %copy-start.10 = (s32[1,4]{1,0:T(1,128)S(1)}, s32[1,4]{1,0:T(1,128)}, u32[]{:S(2)}) copy-start(s32[1,4]{1,0:T(1,128)} %param.9) | copy-start | bytes 52
  44.3 91.0 %all-to-all-start = ((bf16[4,2,2,128,1920]{4,3,2,1,0:T(8,128)(2,1)}), bf16[4,2,2,128,1920]{4,3,2,1,0:T(8,128)(2,1)}, u32[]{:S(2)}, u32[]{:S(2)}) async-start(bf16[4,2,2,128,1920]{4,3,2,1,0:T(8,128)(2,1)} %bitcast.126), calls=%async_computation | async-start | bytes 15728640 | tf_op jit(solution)/shard_map/all_to_all | solution.py:139
  135.2 4.6 %copy-start.8 = (f32[1,2560]{1,0:T(1,128)S(1)}, f32[1,2560]{1,0:T(1,128)}, u32[]{:S(2)}) copy-start(f32[1,2560]{1,0:T(1,128)} %param.11) | copy-start | bytes 30724
  135.2 33.8 %all-to-all-start.1 = ((bf16[4,2,2,128,640]{4,3,2,1,0:T(8,128)(2,1)}), bf16[4,2,2,128,640]{4,3,2,1,0:T(8,128)(2,1)S(1)}, u32[]{:S(2)}, u32[]{:S(2)}) async-start(bf16[4,2,2,128,640]{4,3,2,1,0:T(8,128)(2,1)} %bitcast.45), calls=%async_computation.1 | async-start | bytes 5242880 | tf_op jit(solution)/shard_map/all_to_all | solution.py:139
  169.0 1.5 copy-start
Sparse Core Ops, SparseCore 0:
  9.0 123.7 all-gather.1

commit v11 on v10

--- a/solution.py
+++ b/solution.py
@@ -133,9 +133,8 @@
     projected = None
     for lo, hi in bounds:
         cols = slice(lo, hi)
-        outgoing = jnp.stack(
-            [lax.dynamic_index_in_dim(blocks, picks[i], 0, False)[..., cols] for i in range(2 * owners)]
-        ).reshape(owners, 2, 2, block_len, hi - lo)
+        outgoing = jnp.take(blocks[..., cols], picks, axis=0, mode="clip")
+        outgoing = outgoing.reshape(owners, 2, 2, block_len, hi - lo)
         arrived = lax.all_to_all(outgoing, "seq", split_axis=0, concat_axis=0, tiled=True)
         if projected is not None:
             projected, arrived = lax.optimization_barrier((projected, arrived))

time: 193 us -> 176 us (0.912)
  between operations: 28.8 us -> 13.5 us
  local copies, waits for them, and re-layouts: 27.7 us -> 20.5 us
  waiting for transfers between devices: 78.4 us -> 85.4 us
    unnamed x38 -> x10, local copies, waits for them, and re-layouts: 18.8 us -> 1.67 us
    gather x0 -> x2, local copies, waits for them, and re-layouts: none -> 9.81 us  [shards(): outgoing = jnp.take(blocks[..., cols], picks, axis=0, mode='clip')]
    all_to_all x2, waiting for transfers between devices: 75.6 us -> 84.7 us  [shards(): lax.all_to_all(outgoing, 'seq', split_axis=0, concat_axis=0, tiled=True)]
    slice x1 -> x2, local copies, waits for them, and re-layouts: 0.69 us -> 6.69 us  [shards(): outgoing = jnp.take(blocks[..., cols], picks, axis=0, mode='clip')]
    squeeze x1 -> x0, local copies, waits for them, and re-layouts: 5.01 us -> none  [shards(): lax.dynamic_index_in_dim(blocks, picks[i], 0, False)[..., cols]]
    ppermute x3, waiting for transfers between devices: 2.03 us -> 0.01 us  [shards(): lax.ppermute(window_ids, 'seq', [(s, (s + shift) % owners) for s in range...]
  transfers between devices with their start and end apart: 6 -> 6, of which waited for: 4 -> 2; matrix products, arithmetic and copies ran while one was open for 17% -> 18% of each run, Pallas kernels for 8% -> 8%
where the time goes in v11:
time: 176 us; the launch traced here: 175 us
  waiting for transfers between devices  85.4 us (49%)
  Pallas kernels  22.1 us (13%)
  local copies, waits for them, and re-layouts  20.5 us (12%)
  matrix products  17.7 us (10%)
  starting transfers between devices  14.5 us (8%)
  between operations  13.5 us (8%)
    all_to_all x2, waiting for transfers between devices, shards(): lax.all_to_all(outgoing, 'seq', split_axis=0, concat_axis=0, tiled=True)  84.7 us
    pallas_call x2, Pallas kernels, attention(): pl.pallas_call(kernel, grid_spec=grid_spec, out_shape=jax.ShapeDtypeStruc...  22.1 us
    dot_general x2, matrix products, shards(): part = jnp.dot(mixed, weight[cols], preferred_element_type=jnp.float32)  17.7 us
    gather x2, local copies, waits for them, and re-layouts, shards(): outgoing = jnp.take(blocks[..., cols], picks, axis=0, mode='clip')  9.81 us
    all_to_all x2, starting transfers between devices, shards(): lax.all_to_all(outgoing, 'seq', split_axis=0, concat_axis=0, tiled=True)  9.5 us
    slice x2, local copies, waits for them, and re-layouts, shards(): outgoing = jnp.take(blocks[..., cols], picks, axis=0, mode='clip')  6.69 us
    ppermute x3, starting transfers between devices, shards(): lax.ppermute(window_ids, 'seq', [(s, (s + shift) % owners) for s in range...  5.02 us
  transfers between devices with their start and end apart: 6, of which 2 were waited for; matrix products, arithmetic and copies ran while one was open for 18% of the time, Pallas kernels for 8%

profile of v11, /device:TPU:0, one launch (start us, length us, event | category | flops | bytes accessed | tf_op | source)
XLA Modules:
  0.0 175.4 jit_solution(12286101816383582824)
XLA Ops:
  6.5 0.0 all-gather.2.cloned.1.call-start
  6.5 0.7 all-gather.2.cloned.1.call-update
  7.3 0.8 add_select_fusion.1
  8.0 0.1 reshape.183
  8.1 3.9 %collective-permute-start.2 = (s32[12]{0:T(128)S(1)}, s32[12]{0:T(128)S(1)}, u32[]{:S(2)}, u32[]{:S(2)}) collective-permute-start(s32[12]{0:T(128)S(1)} %reshape.183), channel_id=1, source_target_pairs={{0,24},{8,0},{16,8},{24,16},{1,25},{9,1},{17,9},{25,17},{2,26},{10... | collective-permute-start | bytes 152 | tf_op jit(solution)/shard_map/ppermute | solution.py:121
  12.0 0.0 collective-permute-start
  12.0 1.1 collective-permute-start.1
  13.1 0.1 stack_reshape.3
  13.2 5.1 %slice.34 = bf16[5,2,128,1920]{3,2,1,0:T(8,128)(2,1)} slice(bf16[5,2,128,2560]{3,2,1,0:T(8,128)(2,1)} %bitcast.41), slice={[0:5], [0:2], [0:128], [0:1920]} | slice | bytes 9830400 | tf_op jit(solution)/shard_map/slice | solution.py:136
  18.3 0.0 collective-permute-done.2
  18.3 0.0 collective-permute-done
  18.4 0.0 collective-permute-done.1
  18.4 0.6 scatter_custom_fusion
  19.0 0.1 select_reduce_fusion.1
  19.1 0.1 copy.12
  19.2 0.1 reshape.188
  19.3 7.4 %gather_fusion = bf16[8,2,128,1920]{3,2,1,0:T(8,128)(2,1)} fusion(bf16[5,2,128,1920]{3,2,1,0:T(8,128)(2,1)} %slice.34, s32[1024]{0:T(1024)S(1)} %pad_clamp_fusion), kind=kCustom, calls=%fused_computation | custom fusion | bytes 15728672 | tf_op jit(solution)/shard_map/jit(_take)/gather | solution.py:136
  26.7 0.0 copy-start.2
  26.7 0.0 copy-start.3
  26.8 5.7 %all-to-all-start = ((bf16[4,2,2,128,1920]{4,3,2,1,0:T(8,128)(2,1)}), bf16[4,2,2,128,1920]{4,3,2,1,0:T(8,128)(2,1)}, u32[]{:S(2)}, u32[]{:S(2)}) async-start(bf16[4,2,2,128,1920]{4,3,2,1,0:T(8,128)(2,1)} %bitcast.35), calls=%async_computation | async-start | bytes 15728640 | tf_op jit(solution)/shard_map/all_to_all | solution.py:138
  32.4 0.1 copy.10
  32.5 1.6 slice.36
  34.1 0.1 copy.9
  34.2 0.1 select_reduce_fusion
  34.3 0.0 copy-done.2
  34.3 0.0 copy-done.3
  34.3 0.1 clamp_select_fusion
  34.4 0.1 broadcast_bitcast_fusion
  34.4 0.0 copy-start.1
  34.4 2.4 %gather_fusion.1 = bf16[8,2,128,640]{3,2,1,0:T(8,128)(2,1)} fusion(bf16[5,2,128,640]{3,2,1,0:T(8,128)(2,1)S(1)} %slice.36, s32[1024]{0:T(1024)S(1)} %pad_clamp_fusion), kind=kCustom, calls=%fused_computation.1 | custom fusion | bytes 5242912 | tf_op jit(solution)/shard_map/jit(_take)/gather | solution.py:136
  36.8 82.6 %all-to-all-done.refs_0_.refs_1_.refs_2_.refs_3_.refs_4_.refs_5_.refs_6_.refs_7_.refs_8_.refs_9_.refs_10_.refs_11_ = bf16[4,2,2,128,1920]{4,3,2,1,0:T(8,128)(2,1)} async-done(((bf16[4,2,2,128,1920]{4,3,2,1,0:T(8,128)(2,1)}), bf16[4,2,2,128,1920]{4,3,2,1,0:T(8,128)(2,1)}, u32[]{:S(2)}, u32[]{:S(2)}) %all-to-all-start) | async-done | bytes 7864352 | tf_op jit(solution)/shard_map/all_to_all | solution.py:138
  119.4 3.8 %all-to-all-start.1 = ((bf16[4,2,2,128,640]{4,3,2,1,0:T(8,128)(2,1)}), bf16[4,2,2,128,640]{4,3,2,1,0:T(8,128)(2,1)S(1)}, u32[]{:S(2)}, u32[]{:S(2)}) async-start(bf16[4,2,2,128,640]{4,3,2,1,0:T(8,128)(2,1)} %bitcast.40), calls=%async_computation.1 | async-start | bytes 5242880 | tf_op jit(solution)/shard_map/all_to_all | solution.py:138
  123.3 0.6 slice_bitcast_fusion.slot_ref
  123.8 0.0 copy-done.1
  123.9 1.3 broadcast_in_dim.53
  125.2 14.9 %shard_map.64 = bf16[512,1920]{1,0:T(8,128)(2,1)} custom-call(s32[2]{0:T(128)} %slice_bitcast_fusion.slot_ref, f32[512,768]{1,0:T(8,128)} %bitcast.36, bf16[512,2560]{1,0:T(8,128)(2,1)} %bitcast.38, bf16[4,2,2,128,1920]{4,3,2,1,0:T(8,128)(2,1)} %all-to-all-done.refs_0_.refs_1_.refs_2_.refs_3_.refs_4_.refs_5_.refs_6_.refs_7_.refs_8_.refs_9_.refs_10_.refs_11_, ...), custom_call_target="tpu_custom_call" | custom-call | flops 3019898880 | bytes 11403264 | tf_op jit(solution)/shard_map/pallas_call | solution.py:81
  140.1 0.0 all-gather.2.cloned.1.call-done
  140.1 10.3 %fusion = f32[512,2560]{1,0:T(8,128)} fusion(bf16[512,1920]{1,0:T(8,128)(2,1)} %shard_map.64, bf16[2560,2560]{1,0:T(8,128)(2,1)} %all-gather.2.cloned.1.call-done), kind=kOutput, calls=%fused_computation.3 | convolution fusion | flops 5033164800 | bytes 17039360 | tf_op jit(solution)/shard_map/dot_general | solution.py:142
  150.4 2.1 %all-to-all-done.1.refs_0_.refs_1_.refs_2_.refs_3_.refs_4_.refs_5_.refs_6_.refs_7_.refs_8_.refs_9_.refs_10_.refs_11_ = bf16[4,2,2,128,640]{4,3,2,1,0:T(8,128)(2,1)S(1)} async-done(((bf16[4,2,2,128,640]{4,3,2,1,0:T(8,128)(2,1)}), bf16[4,2,2,128,640]{4,3,2,1,0:T(8,128)(2,1)S(1)}, u32[]{:S(2)}, u32[]{:S(2)}) %all-to-all-start.1) | async-done | bytes 2621472 | tf_op jit(solution)/shard_map/all_to_all | solution.py:138
  152.5 0.0 copy-start
  152.5 1.5 copy-done
  154.0 7.2 %shard_map.65 = bf16[512,640]{1,0:T(8,128)(2,1)} custom-call(s32[2]{0:T(128)} %slice_bitcast_fusion.slot_ref, f32[512,768]{1,0:T(8,128)} %bitcast.37, bf16[512,2560]{1,0:T(8,128)(2,1)} %bitcast.39, bf16[4,2,2,128,640]{4,3,2,1,0:T(8,128)(2,1)} %copy-done, bf16[4,2,2,128,640]{4,3,2,1,0:T(8,128)(2,1)} %copy-done, bf16[4,2,2,128,640]{4,3,2,1,0:T(8,128)(2,1)} %copy-done, ...), custom_call_target="tpu_custom_call" | custom-call | flops 1006632960 | bytes 4849664 | tf_op jit(solution)/shard_map/pallas_call | solution.py:81
  161.2 7.4 %fusion.2 = bf16[1,512,2560]{2,1,0:T(8,128)(2,1)} fusion(f32[512,2560]{1,0:T(8,128)} %fusion, bf16[512,640]{1,0:T(8,128)(2,1)} %shard_map.65, bf16[2560,2560]{1,0:T(8,128)(2,1)} %all-gather.2.cloned.1.call-done, f32[2560]{0:T(1024)S(1)} %reduce), kind=kOutput, calls=%fused_computation.6 | convolution fusion | flops 1681653760 | bytes 11806720 | tf_op jit(solution)/shard_map/dot_general | solution.py:142
  (7 shorter events, 0.1 us)
Async XLA Ops:
  6.5 133.6 %all-gather.2.cloned.1.call-start = ((), (), s32[]{:S(2)}) async-start(), calls=%async_computation.2 | async-start | bytes 14745600 | tf_op jit(solution)/shard_map/all_gather | solution.py:117
  8.1 10.2 %collective-permute-start.2 = (s32[12]{0:T(128)S(1)}, s32[12]{0:T(128)S(1)}, u32[]{:S(2)}, u32[]{:S(2)}) collective-permute-start(s32[12]{0:T(128)S(1)} %reshape.183), channel_id=1, source_target_pairs={{0,24},{8,0},{16,8},{24,16},{1,25},{9,1},{17,9},{25,17},{2,26},{10... | collective-permute-start | bytes 152 | tf_op jit(solution)/shard_map/ppermute | solution.py:121
  12.0 6.3 %collective-permute-start = (s32[12]{0:T(128)S(1)}, s32[12]{0:T(128)S(1)}, u32[]{:S(2)}, u32[]{:S(2)}) collective-permute-start(s32[12]{0:T(128)S(1)} %reshape.183), channel_id=1, source_target_pairs={{0,8},{8,16},{16,24},{24,0},{1,9},{9,17},{17,25},{25,1},{2,10},{10... | collective-permute-start | bytes 152 | tf_op jit(solution)/shard_map/ppermute | solution.py:121
  12.0 6.3 %collective-permute-start.1 = (s32[12]{0:T(128)S(1)}, s32[12]{0:T(128)S(1)}, u32[]{:S(2)}, u32[]{:S(2)}) collective-permute-start(s32[12]{0:T(128)S(1)} %reshape.183), channel_id=1, source_target_pairs={{0,16},{8,24},{16,0},{24,8},{1,17},{9,25},{17,1},{25,9},{2,18},{10... | collective-permute-start | bytes 152 | tf_op jit(solution)/shard_map/ppermute | solution.py:121
  26.7 7.5 %copy-start.2 = (s32[1,4,5]{2,1,0:T(4,128)S(1)}, s32[1,4,5]{2,1,0:T(4,128)}, u32[]{:S(2)}) copy-start(s32[1,4,5]{2,1,0:T(4,128)} %param.8) | copy-start | bytes 244
  26.7 7.5 %copy-start.3 = (s32[1,4]{1,0:T(1,128)S(1)}, s32[1,4]{1,0:T(1,128)}, u32[]{:S(2)}) copy-start(s32[1,4]{1,0:T(1,128)} %param.9) | copy-start | bytes 52
  26.8 92.7 %all-to-all-start = ((bf16[4,2,2,128,1920]{4,3,2,1,0:T(8,128)(2,1)}), bf16[4,2,2,128,1920]{4,3,2,1,0:T(8,128)(2,1)}, u32[]{:S(2)}, u32[]{:S(2)}) async-start(bf16[4,2,2,128,1920]{4,3,2,1,0:T(8,128)(2,1)} %bitcast.35), calls=%async_computation | async-start | bytes 15728640 | tf_op jit(solution)/shard_map/all_to_all | solution.py:138
  34.4 89.4 %copy-start.1 = (f32[1,2560]{1,0:T(1,128)S(1)}, f32[1,2560]{1,0:T(1,128)}, u32[]{:S(2)}) copy-start(f32[1,2560]{1,0:T(1,128)} %param.11) | copy-start | bytes 30724
  119.4 33.1 %all-to-all-start.1 = ((bf16[4,2,2,128,640]{4,3,2,1,0:T(8,128)(2,1)}), bf16[4,2,2,128,640]{4,3,2,1,0:T(8,128)(2,1)S(1)}, u32[]{:S(2)}, u32[]{:S(2)}) async-start(bf16[4,2,2,128,640]{4,3,2,1,0:T(8,128)(2,1)} %bitcast.40), calls=%async_computation.1 | async-start | bytes 5242880 | tf_op jit(solution)/shard_map/all_to_all | solution.py:138
  152.5 1.5 copy-start
Sparse Core Ops, SparseCore 0:
  9.0 123.7 all-gather.1

commit v12 on v11

--- a/solution.py
+++ b/solution.py
@@ -127,16 +127,18 @@
     picks = jnp.stack([asked_slot, jnp.zeros_like(asked_slot)], axis=1).reshape(-1)
     bias = visibility(block_ids, key_limit[0], owners, block_len)
     heads = width // HS
-    tail_heads = heads // 4 if heads % 20 == 0 else heads
-    bounds = [(0, heads - tail_heads), (heads - tail_heads, heads)]
-    bounds = [(lo * HS, hi * HS) for lo, hi in bounds if hi > lo]
+    if heads % 10 == 0:
+        edges = [0, heads * 6 // 10, heads * 9 // 10, heads]
+    else:
+        edges = [0, heads]
+    bounds = [(lo * HS, hi * HS) for lo, hi in zip(edges[:-1], edges[1:])]
     projected = None
     for lo, hi in bounds:
         cols = slice(lo, hi)
         outgoing = jnp.take(blocks[..., cols], picks, axis=0, mode="clip")
         outgoing = outgoing.reshape(owners, 2, 2, block_len, hi - lo)
         arrived = lax.all_to_all(outgoing, "seq", split_axis=0, concat_axis=0, tiled=True)
-        if projected is not None:
+        if hi == bounds[-1][1] and projected is not None:
             projected, arrived = lax.optimization_barrier((projected, arrived))
         mixed = attention(block_ids[0, :NSINK], bias, queries[0], arrived, lo)
         part = jnp.dot(mixed, weight[cols], preferred_element_type=jnp.float32)

time: 176 us -> 184 us (1.045)
  Pallas kernels: 22.1 us -> 27 us
  starting transfers between devices: 14.5 us -> 17.9 us
  waiting for transfers between devices: 85.4 us -> 82.4 us
    pallas_call x2 -> x3, Pallas kernels: 22.1 us -> 27 us  [attention(): pl.pallas_call(kernel, grid_spec=grid_spec, out_shape=jax.ShapeDtypeStruc...]
    all_to_all x2 -> x3, waiting for transfers between devices: 84.7 us -> 80.1 us  [shards(): lax.all_to_all(outgoing, 'seq', split_axis=0, concat_axis=0, tiled=True)]
    all_to_all x2 -> x3, starting transfers between devices: 9.5 us -> 12.9 us  [shards(): lax.all_to_all(outgoing, 'seq', split_axis=0, concat_axis=0, tiled=True)]
    dot_general x2 -> x3, matrix products: 17.7 us -> 19 us  [shards(): part = jnp.dot(mixed, weight[cols], preferred_element_type=jnp.float32)]
    slice x2 -> x3, local copies, waits for them, and re-layouts: 6.69 us -> 7.14 us  [shards(): outgoing = jnp.take(blocks[..., cols], picks, axis=0, mode='clip')]
    gather x2 -> x3, local copies, waits for them, and re-layouts: 9.81 us -> 9.86 us  [shards(): outgoing = jnp.take(blocks[..., cols], picks, axis=0, mode='clip')]
  transfers between devices with their start and end apart: 6 -> 7, of which waited for: 2 -> 3; matrix products, arithmetic and copies ran while one was open for 18% -> 19% of each run, Pallas kernels for 8% -> 12%
where the time goes in v12:
time: 184 us
  waiting for transfers between devices  82.4 us (45%)
  Pallas kernels  27 us (15%)
  local copies, waits for them, and re-layouts  22 us (12%)
  matrix products  19 us (10%)
  starting transfers between devices  17.9 us (10%)
  between operations  13.5 us (7%)
    all_to_all x3, waiting for transfers between devices, shards(): lax.all_to_all(outgoing, 'seq', split_axis=0, concat_axis=0, tiled=True)  80.1 us
    pallas_call x3, Pallas kernels, attention(): pl.pallas_call(kernel, grid_spec=grid_spec, out_shape=jax.ShapeDtypeStruc...  27 us
    dot_general x3, matrix products, shards(): part = jnp.dot(mixed, weight[cols], preferred_element_type=jnp.float32)  19 us
    all_to_all x3, starting transfers between devices, shards(): lax.all_to_all(outgoing, 'seq', split_axis=0, concat_axis=0, tiled=True)  12.9 us
    gather x3, local copies, waits for them, and re-layouts, shards(): outgoing = jnp.take(blocks[..., cols], picks, axis=0, mode='clip')  9.86 us
    slice x3, local copies, waits for them, and re-layouts, shards(): outgoing = jnp.take(blocks[..., cols], picks, axis=0, mode='clip')  7.14 us
    ppermute x3, starting transfers between devices, shards(): lax.ppermute(window_ids, 'seq', [(s, (s + shift) % owners) for s in range...  5.02 us
  transfers between devices with their start and end apart: 7, of which 3 were waited for; matrix products, arithmetic and copies ran while one was open for 19% of the time, Pallas kernels for 12%

profile of v12, /device:TPU:0, one launch (start us, length us, event | category | flops | bytes accessed | tf_op | source)
XLA Modules:
  0.0 183.5 jit_solution(4266241389284281151)
XLA Ops:
  6.5 0.0 all-gather.2.cloned.1.call-start
  6.5 0.7 all-gather.2.cloned.1.call-update
  7.3 0.8 add_select_fusion.1
  8.0 0.1 reshape.186
  8.1 3.9 %collective-permute-start.2 = (s32[12]{0:T(128)S(1)}, s32[12]{0:T(128)S(1)}, u32[]{:S(2)}, u32[]{:S(2)}) collective-permute-start(s32[12]{0:T(128)S(1)} %reshape.186), channel_id=1, source_target_pairs={{0,24},{8,0},{16,8},{24,16},{1,25},{9,1},{17,9},{25,17},{2,26},{10... | collective-permute-start | bytes 152 | tf_op jit(solution)/shard_map/ppermute | solution.py:121
  12.0 0.0 collective-permute-start
  12.0 1.1 collective-permute-start.1
  13.1 0.1 stack_reshape.3
  13.2 1.7 slice.47
  14.9 0.0 collective-permute-done.2
  14.9 1.6 collective-permute-done
  16.5 0.0 collective-permute-done.1
  16.5 0.6 scatter_custom_fusion
  17.1 0.1 select_reduce_fusion.1
  17.2 0.1 copy.12
  17.3 0.1 reshape.192
  17.4 2.5 %gather_fusion.1 = bf16[8,2,128,768]{3,2,1,0:T(8,128)(2,1)} fusion(bf16[5,2,128,768]{3,2,1,0:T(8,128)(2,1)S(1)} %slice.47, s32[1024]{0:T(1024)S(1)} %pad_clamp_fusion), kind=kCustom, calls=%fused_computation.1 | custom fusion | bytes 6291488 | tf_op jit(solution)/shard_map/jit(_take)/gather | solution.py:138
  19.9 3.9 %all-to-all-start.1 = ((bf16[4,2,2,128,768]{4,3,2,1,0:T(8,128)(2,1)}), bf16[4,2,2,128,768]{4,3,2,1,0:T(8,128)(2,1)S(1)}, u32[]{:S(2)}, u32[]{:S(2)}) async-start(bf16[4,2,2,128,768]{4,3,2,1,0:T(8,128)(2,1)} %bitcast.44), calls=%async_computation.1 | async-start | bytes 6291456 | tf_op jit(solution)/shard_map/all_to_all | solution.py:140
  23.8 4.3 %slice.45 = bf16[5,2,128,1536]{3,2,1,0:T(8,128)(2,1)} slice(bf16[5,2,128,2560]{3,2,1,0:T(8,128)(2,1)} %bitcast.46), slice={[0:5], [0:2], [0:128], [0:1536]} | slice | bytes 7864320 | tf_op jit(solution)/shard_map/slice | solution.py:138
  28.2 5.8 %gather_fusion = bf16[8,2,128,1536]{3,2,1,0:T(8,128)(2,1)} fusion(bf16[5,2,128,1536]{3,2,1,0:T(8,128)(2,1)} %slice.45, s32[1024]{0:T(1024)S(1)} %pad_clamp_fusion), kind=kCustom, calls=%fused_computation | custom fusion | bytes 12582944 | tf_op jit(solution)/shard_map/jit(_take)/gather | solution.py:138
  33.9 24.7 %all-to-all-done.1.refs_0_.refs_1_.refs_2_.refs_3_.refs_4_.refs_5_.refs_6_.refs_7_.refs_8_.refs_9_.refs_10_.refs_11_ = bf16[4,2,2,128,768]{4,3,2,1,0:T(8,128)(2,1)S(1)} async-done(((bf16[4,2,2,128,768]{4,3,2,1,0:T(8,128)(2,1)}), bf16[4,2,2,128,768]{4,3,2,1,0:T(8,128)(2,1)S(1)}, u32[]{:S(2)}, u32[]{:S(2)}) %all-to-all-start.1) | async-done | bytes 3145760 | tf_op jit(solution)/shard_map/all_to_all | solution.py:140
  58.7 1.6 copy-done
  60.3 5.2 %all-to-all-start = ((bf16[4,2,2,128,1536]{4,3,2,1,0:T(8,128)(2,1)}), bf16[4,2,2,128,1536]{4,3,2,1,0:T(8,128)(2,1)}, u32[]{:S(2)}, u32[]{:S(2)}) async-start(bf16[4,2,2,128,1536]{4,3,2,1,0:T(8,128)(2,1)} %bitcast.40), calls=%async_computation | async-start | bytes 12582912 | tf_op jit(solution)/shard_map/all_to_all | solution.py:140
  65.5 0.1 copy.10
  65.6 1.1 slice.49
  66.8 0.1 copy.9
  66.9 0.0 copy-done.3
  66.9 0.1 select_reduce_fusion
  67.0 0.0 copy-done.4
  67.0 0.5 slice_bitcast_fusion.slot_ref
  67.5 0.0 copy-done.5
  67.5 0.1 clamp_select_fusion
  67.6 0.1 broadcast_bitcast_fusion
  67.7 1.6 gather_fusion.2
  69.3 1.3 broadcast_in_dim.55
  70.6 9.1 %shard_map.65 = bf16[512,768]{1,0:T(8,128)(2,1)} custom-call(s32[2]{0:T(128)} %slice_bitcast_fusion.slot_ref, f32[512,768]{1,0:T(8,128)} %bitcast.37, bf16[512,2560]{1,0:T(8,128)(2,1)} %bitcast.41, bf16[4,2,2,128,768]{4,3,2,1,0:T(8,128)(2,1)} %copy-done, bf16[4,2,2,128,768]{4,3,2,1,0:T(8,128)(2,1)} %copy-done, bf16[4,2,2,128,768]{4,3,2,1,0:T(8,128)(2,1)} %copy-done, ...), custom_call_target="tpu_custom_call" | custom-call | flops 1207959552 | bytes 5505024 | tf_op jit(solution)/shard_map/pallas_call | solution.py:81
  79.7 55.3 %all-to-all-done.refs_0_.refs_1_.refs_2_.refs_3_.refs_4_.refs_5_.refs_6_.refs_7_.refs_8_.refs_9_.refs_10_.refs_11_ = bf16[4,2,2,128,1536]{4,3,2,1,0:T(8,128)(2,1)} async-done(((bf16[4,2,2,128,1536]{4,3,2,1,0:T(8,128)(2,1)}), bf16[4,2,2,128,1536]{4,3,2,1,0:T(8,128)(2,1)}, u32[]{:S(2)}, u32[]{:S(2)}) %all-to-all-start) | async-done | bytes 6291488 | tf_op jit(solution)/shard_map/all_to_all | solution.py:140
  135.1 3.7 %all-to-all-start.2 = ((bf16[4,2,2,128,256]{4,3,2,1,0:T(8,128)(2,1)}), bf16[4,2,2,128,256]{4,3,2,1,0:T(8,128)(2,1)S(1)}, u32[]{:S(2)}, u32[]{:S(2)}) async-start(bf16[4,2,2,128,256]{4,3,2,1,0:T(8,128)(2,1)} %bitcast.15), calls=%async_computation.2 | async-start | bytes 2097152 | tf_op jit(solution)/shard_map/all_to_all | solution.py:140
  138.8 13.0 %shard_map.64 = bf16[512,1536]{1,0:T(8,128)(2,1)} custom-call(s32[2]{0:T(128)} %slice_bitcast_fusion.slot_ref, f32[512,768]{1,0:T(8,128)} %bitcast.38, bf16[512,2560]{1,0:T(8,128)(2,1)} %bitcast.42, bf16[4,2,2,128,1536]{4,3,2,1,0:T(8,128)(2,1)} %all-to-all-done.refs_0_.refs_1_.refs_2_.refs_3_.refs_4_.refs_5_.refs_6_.refs_7_.refs_8_.refs_9_.refs_10_.refs_11_, ...), custom_call_target="tpu_custom_call" | custom-call | flops 2415919104 | bytes 9437184 | tf_op jit(solution)/shard_map/pallas_call | solution.py:81
  151.7 0.0 copy-start.2
  151.7 0.0 all-gather.2.cloned.1.call-done
  151.8 7.1 %fusion = f32[512,2560]{1,0:T(8,128)S(1)} fusion(bf16[512,1536]{1,0:T(8,128)(2,1)} %shard_map.64, bf16[2560,2560]{1,0:T(8,128)(2,1)} %all-gather.2.cloned.1.call-done), kind=kOutput, calls=%fused_computation.4 | convolution fusion | flops 4026531840 | bytes 14680064 | tf_op jit(solution)/shard_map/dot_general | solution.py:144
  158.9 0.0 copy-done.2
  158.9 6.6 %convolution_add_fusion = f32[512,2560]{1,0:T(8,128)} fusion(f32[512,2560]{1,0:T(8,128)S(1)} %fusion, bf16[512,768]{1,0:T(8,128)(2,1)S(1)} %copy-done.2, bf16[2560,2560]{1,0:T(8,128)(2,1)} %all-gather.2.cloned.1.call-done), kind=kOutput, calls=%fused_computation.7 | convolution fusion | flops 2014576640 | bytes 15204352 | tf_op jit(solution)/shard_map/dot_general | solution.py:144
  165.5 0.0 all-to-all-done.2.refs_0_.refs_1_.refs_2_.refs_3_.refs_4_.refs_5_.refs_6_.refs_7_.refs_8_.refs_9_.refs_10_.refs_11_
  165.5 1.0 copy-done.1
  166.5 4.9 %shard_map.66 = bf16[512,256]{1,0:T(8,128)(2,1)} custom-call(s32[2]{0:T(128)} %slice_bitcast_fusion.slot_ref, f32[512,768]{1,0:T(8,128)} %bitcast.39, bf16[512,2560]{1,0:T(8,128)(2,1)} %bitcast.43, bf16[4,2,2,128,256]{4,3,2,1,0:T(8,128)(2,1)} %copy-done.1, bf16[4,2,2,128,256]{4,3,2,1,0:T(8,128)(2,1)} %copy-done.1, bf16[4,2,2,128,256]{4,3,2,1,0:T(8,128)(2,1)} %copy-done.1, ...), custom_call_target="tpu_custom_call" | custom-call | flops 402653184 | bytes 2883584 | tf_op jit(solution)/shard_map/pallas_call | solution.py:81
  171.4 5.3 %fusion.2 = bf16[1,512,2560]{2,1,0:T(8,128)(2,1)} fusion(f32[512,2560]{1,0:T(8,128)} %convolution_add_fusion, bf16[512,256]{1,0:T(8,128)(2,1)} %shard_map.66, f32[2560]{0:T(1024)S(1)} %reduce, bf16[2560,2560]{1,0:T(8,128)(2,1)} %all-gather.2.cloned.1.call-done), kind=kOutput, calls=%fused_computation.8 | convolution fusion | flops 675020800 | bytes 9447424 | tf_op jit(solution)/shard_map/dot_general | solution.py:144
  (12 shorter events, 0.1 us)
Async XLA Ops:
  6.5 145.2 %all-gather.2.cloned.1.call-start = ((), (), s32[]{:S(2)}) async-start(), calls=%async_computation.3 | async-start | bytes 14745600 | tf_op jit(solution)/shard_map/all_gather | solution.py:117
  8.1 6.8 %collective-permute-start.2 = (s32[12]{0:T(128)S(1)}, s32[12]{0:T(128)S(1)}, u32[]{:S(2)}, u32[]{:S(2)}) collective-permute-start(s32[12]{0:T(128)S(1)} %reshape.186), channel_id=1, source_target_pairs={{0,24},{8,0},{16,8},{24,16},{1,25},{9,1},{17,9},{25,17},{2,26},{10... | collective-permute-start | bytes 152 | tf_op jit(solution)/shard_map/ppermute | solution.py:121
  12.0 4.5 %collective-permute-start = (s32[12]{0:T(128)S(1)}, s32[12]{0:T(128)S(1)}, u32[]{:S(2)}, u32[]{:S(2)}) collective-permute-start(s32[12]{0:T(128)S(1)} %reshape.186), channel_id=1, source_target_pairs={{0,8},{8,16},{16,24},{24,0},{1,9},{9,17},{17,25},{25,1},{2,10},{10... | collective-permute-start | bytes 152 | tf_op jit(solution)/shard_map/ppermute | solution.py:121
  12.0 4.5 %collective-permute-start.1 = (s32[12]{0:T(128)S(1)}, s32[12]{0:T(128)S(1)}, u32[]{:S(2)}, u32[]{:S(2)}) collective-permute-start(s32[12]{0:T(128)S(1)} %reshape.186), channel_id=1, source_target_pairs={{0,16},{8,24},{16,0},{24,8},{1,17},{9,25},{17,1},{25,9},{2,18},{10... | collective-permute-start | bytes 152 | tf_op jit(solution)/shard_map/ppermute | solution.py:121
  19.9 38.8 %all-to-all-start.1 = ((bf16[4,2,2,128,768]{4,3,2,1,0:T(8,128)(2,1)}), bf16[4,2,2,128,768]{4,3,2,1,0:T(8,128)(2,1)S(1)}, u32[]{:S(2)}, u32[]{:S(2)}) async-start(bf16[4,2,2,128,768]{4,3,2,1,0:T(8,128)(2,1)} %bitcast.44), calls=%async_computation.1 | async-start | bytes 6291456 | tf_op jit(solution)/shard_map/all_to_all | solution.py:140
  58.6 1.6 copy-start
  58.6 8.2 %copy-start.3 = (f32[1,2560]{1,0:T(1,128)S(1)}, f32[1,2560]{1,0:T(1,128)}, u32[]{:S(2)}) copy-start(f32[1,2560]{1,0:T(1,128)} %param.11) | copy-start | bytes 30724
  58.6 8.3 %copy-start.4 = (s32[1,4,5]{2,1,0:T(4,128)S(1)}, s32[1,4,5]{2,1,0:T(4,128)}, u32[]{:S(2)}) copy-start(s32[1,4,5]{2,1,0:T(4,128)} %param.8) | copy-start | bytes 244
  58.6 8.9 %copy-start.5 = (s32[1,4]{1,0:T(1,128)S(1)}, s32[1,4]{1,0:T(1,128)}, u32[]{:S(2)}) copy-start(s32[1,4]{1,0:T(1,128)} %param.9) | copy-start | bytes 52
  60.3 74.8 %all-to-all-start = ((bf16[4,2,2,128,1536]{4,3,2,1,0:T(8,128)(2,1)}), bf16[4,2,2,128,1536]{4,3,2,1,0:T(8,128)(2,1)}, u32[]{:S(2)}, u32[]{:S(2)}) async-start(bf16[4,2,2,128,1536]{4,3,2,1,0:T(8,128)(2,1)} %bitcast.40), calls=%async_computation | async-start | bytes 12582912 | tf_op jit(solution)/shard_map/all_to_all | solution.py:140
  135.1 30.4 %all-to-all-start.2 = ((bf16[4,2,2,128,256]{4,3,2,1,0:T(8,128)(2,1)}), bf16[4,2,2,128,256]{4,3,2,1,0:T(8,128)(2,1)S(1)}, u32[]{:S(2)}, u32[]{:S(2)}) async-start(bf16[4,2,2,128,256]{4,3,2,1,0:T(8,128)(2,1)} %bitcast.15), calls=%async_computation.2 | async-start | bytes 2097152 | tf_op jit(solution)/shard_map/all_to_all | solution.py:140
  151.7 7.1 %copy-start.2 = (bf16[512,768]{1,0:T(8,128)(2,1)S(1)}, bf16[512,768]{1,0:T(8,128)(2,1)}, u32[]{:S(2)}) copy-start(bf16[512,768]{1,0:T(8,128)(2,1)} %shard_map.65) | copy-start | bytes 2359300
  165.5 1.0 copy-start.1
Sparse Core Ops, SparseCore 0:
  9.0 123.7 all-gather.1

commit v13 on v11

--- a/solution.py
+++ b/solution.py
@@ -12,10 +12,10 @@
 GROUPS = (5, 4, 2, 1)
 
 
-def attention(sink_ids, bias, query_rows, arrived, col_start):
+def attention(sink_ids, bias, query_rows, sink_pool, arrived, col_start):
     rows = query_rows.shape[0]
     width = arrived.shape[-1]
-    block_len = arrived.shape[3]
+    block_len = arrived.shape[2]
     owners = arrived.shape[0]
     pooled = NSINK + owners
     heads = width // HS
@@ -46,13 +46,12 @@
 
     def sink_spec(u, kv):
         return pl.BlockSpec(
-            (None, None, None, block_len, span), lambda g, slot_ref: (slot_ref[u], 1, kv, 0, g)
+            (None, None, block_len, span),
+            lambda g, slot_ref: (slot_ref[u], kv, 0, g + col_start // span),
         )
 
     def window_spec(r, kv):
-        return pl.BlockSpec(
-            (None, None, None, block_len, span), lambda g, slot_ref: (r, 0, kv, 0, g)
-        )
+        return pl.BlockSpec((None, None, block_len, span), lambda g, slot_ref: (r, kv, 0, g))
 
     in_specs = [
         pl.BlockSpec((rows, pooled * block_len), lambda g, slot_ref: (0, 0)),
@@ -62,7 +61,7 @@
     for kv in range(2):
         for u in range(NSINK):
             in_specs.append(sink_spec(u, kv))
-            operands.append(arrived)
+            operands.append(sink_pool)
         for r in range(owners):
             in_specs.append(window_spec(r, kv))
             operands.append(arrived)
@@ -120,11 +119,13 @@
     for shift in range(1, owners):
         lists.append(lax.ppermute(window_ids, "seq", [(s, (s + shift) % owners) for s in range(owners)]))
     by_reader = jnp.stack(lists)
+    first = jnp.broadcast_to(blocks[0][None], (owners,) + blocks.shape[1:])
+    by_reader, first = lax.optimization_barrier((by_reader, first))
+    sink_pool = lax.all_to_all(first, "seq", split_axis=0, concat_axis=0, tiled=True)
     readers = (me - jnp.arange(owners, dtype=jnp.int32)) % owners
     readers_ids = jnp.zeros_like(by_reader).at[readers].set(by_reader)
     asked = jnp.max(jnp.where(readers_ids % owners == me, readers_ids, -1), axis=1)
     asked_slot = jnp.minimum(jnp.maximum(asked, 0) // owners, blocks.shape[0] - 1)
-    picks = jnp.stack([asked_slot, jnp.zeros_like(asked_slot)], axis=1).reshape(-1)
     bias = visibility(block_ids, key_limit[0], owners, block_len)
     heads = width // HS
     tail_heads = heads // 4 if heads % 20 == 0 else heads
@@ -133,12 +134,13 @@
     projected = None
     for lo, hi in bounds:
         cols = slice(lo, hi)
-        outgoing = jnp.take(blocks[..., cols], picks, axis=0, mode="clip")
-        outgoing = outgoing.reshape(owners, 2, 2, block_len, hi - lo)
+        outgoing = jnp.take(blocks[..., cols], asked_slot, axis=0, mode="clip")
+        if lo == 0:
+            outgoing, sink_pool = lax.optimization_barrier((outgoing, sink_pool))
         arrived = lax.all_to_all(outgoing, "seq", split_axis=0, concat_axis=0, tiled=True)
         if projected is not None:
             projected, arrived = lax.optimization_barrier((projected, arrived))
-        mixed = attention(block_ids[0, :NSINK], bias, queries[0], arrived, lo)
+        mixed = attention(block_ids[0, :NSINK], bias, queries[0], sink_pool, arrived, lo)
         part = jnp.dot(mixed, weight[cols], preferred_element_type=jnp.float32)
         projected = part if projected is None else projected + part
     return (gate[0][None, :] * projected).astype(jnp.bfloat16)[None]

time: 176 us -> 184 us (1.045)
  starting transfers between devices: 14.5 us -> 18.7 us
  waiting for transfers between devices: 85.4 us -> 88.4 us
    all_to_all x0 -> x1, waiting for transfers between devices: none -> 46.1 us  [shards(): lax.all_to_all(first, 'seq', split_axis=0, concat_axis=0, tiled=True)]
    all_to_all x2, waiting for transfers between devices: 84.7 us -> 39.6 us  [shards(): lax.all_to_all(outgoing, 'seq', split_axis=0, concat_axis=0, tiled=True)]
    all_to_all x0 -> x1, starting transfers between devices: none -> 5.22 us  [shards(): lax.all_to_all(first, 'seq', split_axis=0, concat_axis=0, tiled=True)]
    broadcast_in_dim x1 -> x2, local copies, waits for them, and re-layouts: 0.09 us -> 4.23 us  [shards(): first = jnp.broadcast_to(blocks[0][None], (owners,) + blocks.shape[1:])]
    gather x2, local copies, waits for them, and re-layouts: 9.81 us -> 7.18 us  [shards(): outgoing = jnp.take(blocks[..., cols], asked_slot, axis=0, mode='clip')]
    ppermute x3, waiting for transfers between devices: 0.01 us -> 1.88 us  [shards(): lax.ppermute(window_ids, 'seq', [(s, (s + shift) % owners) for s in range...]
  transfers between devices with their start and end apart: 6 -> 7, of which waited for: 2 -> 3; matrix products, arithmetic and copies ran while one was open for 18% -> 18% of each run, Pallas kernels for 8% -> 8%
where the time goes in v13:
time: 184 us
  waiting for transfers between devices  88.4 us (48%)
  local copies, waits for them, and re-layouts  22.1 us (12%)
  Pallas kernels  22.1 us (12%)
  starting transfers between devices  18.7 us (10%)
  matrix products  17.7 us (10%)
  between operations  13.5 us (7%)
    all_to_all x1, waiting for transfers between devices, shards(): lax.all_to_all(first, 'seq', split_axis=0, concat_axis=0, tiled=True)  46.1 us
    all_to_all x2, waiting for transfers between devices, shards(): lax.all_to_all(outgoing, 'seq', split_axis=0, concat_axis=0, tiled=True)  39.6 us
    pallas_call x2, Pallas kernels, attention(): pl.pallas_call(kernel, grid_spec=grid_spec, out_shape=jax.ShapeDtypeStruc...  22.1 us
    dot_general x2, matrix products, shards(): part = jnp.dot(mixed, weight[cols], preferred_element_type=jnp.float32)  17.7 us
    all_to_all x2, starting transfers between devices, shards(): lax.all_to_all(outgoing, 'seq', split_axis=0, concat_axis=0, tiled=True)  8.5 us
    gather x2, local copies, waits for them, and re-layouts, shards(): outgoing = jnp.take(blocks[..., cols], asked_slot, axis=0, mode='clip')  7.18 us
    slice x2, local copies, waits for them, and re-layouts, shards(): outgoing = jnp.take(blocks[..., cols], asked_slot, axis=0, mode='clip')  6.78 us
    all_to_all x1, starting transfers between devices, shards(): lax.all_to_all(first, 'seq', split_axis=0, concat_axis=0, tiled=True)  5.22 us
  transfers between devices with their start and end apart: 7, of which 3 were waited for; matrix products, arithmetic and copies ran while one was open for 18% of the time, Pallas kernels for 8%

profile of v13, /device:TPU:0, one launch (start us, length us, event | category | flops | bytes accessed | tf_op | source)
XLA Modules:
  0.0 183.6 jit_solution(10008695793152792613)
XLA Ops:
  6.5 0.0 all-gather.2.cloned.1.call-start
  6.5 0.7 all-gather.2.cloned.1.call-update
  7.3 0.8 add_select_fusion.1
  8.0 0.1 reshape.177
  8.1 3.9 %collective-permute-start.2 = (s32[12]{0:T(128)S(1)}, s32[12]{0:T(128)S(1)}, u32[]{:S(2)}, u32[]{:S(2)}) collective-permute-start(s32[12]{0:T(128)S(1)} %reshape.177), channel_id=1, source_target_pairs={{0,24},{8,0},{16,8},{24,16},{1,25},{9,1},{17,9},{25,17},{2,26},{10... | collective-permute-start | bytes 152 | tf_op jit(solution)/shard_map/ppermute | solution.py:120
  12.0 0.0 collective-permute-start
  12.0 1.1 collective-permute-start.1
  13.1 0.1 stack_reshape.3
  13.2 1.4 slice_bitcast_fusion
  14.6 0.0 collective-permute-done.2
  14.6 1.9 %collective-permute-done = s32[12]{0:T(128)S(1)} collective-permute-done((s32[12]{0:T(128)S(1)}, s32[12]{0:T(128)S(1)}, u32[]{:S(2)}, u32[]{:S(2)}) %collective-permute-start) | collective-permute-done | bytes 80 | tf_op jit(solution)/shard_map/ppermute | solution.py:120
  16.5 0.0 collective-permute-done.1
  16.5 2.8 %broadcast_in_dim.61 = bf16[4,2,128,2560]{3,2,1,0:T(8,128)(2,1)} broadcast(bf16[2,128,2560]{2,1,0:T(8,128)(2,1)S(1)} %slice_bitcast_fusion), dimensions={1,2,3} | broadcast | bytes 6553600 | tf_op jit(solution)/shard_map/broadcast_in_dim | solution.py:122
  19.3 5.2 %all-to-all-start = ((bf16[4,2,128,2560]{3,2,1,0:T(8,128)(2,1)}), bf16[4,2,128,2560]{3,2,1,0:T(8,128)(2,1)}, u32[]{:S(2)}, u32[]{:S(2)}) async-start(bf16[4,2,128,2560]{3,2,1,0:T(8,128)(2,1)} %broadcast_in_dim.61), calls=%async_computation | async-start | bytes 10485760 | tf_op jit(solution)/shard_map/all_to_all | solution.py:124
  24.6 5.2 %slice.39 = bf16[5,2,128,1920]{3,2,1,0:T(8,128)(2,1)} slice(bf16[5,2,128,2560]{3,2,1,0:T(8,128)(2,1)} %bitcast.41), slice={[0:5], [0:2], [0:128], [0:1920]} | slice | bytes 9830400 | tf_op jit(solution)/shard_map/slice | solution.py:137
  29.8 0.6 scatter_custom_fusion
  30.4 0.1 select_reduce_fusion.1
  30.5 5.3 %gather_fusion = bf16[4,2,128,1920]{3,2,1,0:T(8,128)(2,1)} fusion(bf16[5,2,128,1920]{3,2,1,0:T(8,128)(2,1)} %slice.39, s32[1024]{0:T(1024)S(1)} %pad_clamp_fusion), kind=kCustom, calls=%fused_computation | custom fusion | bytes 7864336 | tf_op jit(solution)/shard_map/jit(_take)/gather | solution.py:137
  35.9 0.0 copy-start.1
  35.9 0.0 copy-start.2
  35.9 0.0 copy-start.3
  35.9 46.1 %all-to-all-done.refs_0_.refs_1_.refs_6_.refs_7_ = bf16[4,2,128,2560]{3,2,1,0:T(8,128)(2,1)} async-done(((bf16[4,2,128,2560]{3,2,1,0:T(8,128)(2,1)}), bf16[4,2,128,2560]{3,2,1,0:T(8,128)(2,1)}, u32[]{:S(2)}, u32[]{:S(2)}) %all-to-all-start) | async-done | bytes 5242912 | tf_op jit(solution)/shard_map/all_to_all | solution.py:124
  82.0 4.8 %all-to-all-start.1 = ((bf16[4,2,128,1920]{3,2,1,0:T(8,128)(2,1)}), bf16[4,2,128,1920]{3,2,1,0:T(8,128)(2,1)}, u32[]{:S(2)}, u32[]{:S(2)}) async-start(bf16[4,2,128,1920]{3,2,1,0:T(8,128)(2,1)} %gather_fusion), calls=%async_computation.1 | async-start | bytes 7864320 | tf_op jit(solution)/shard_map/all_to_all | solution.py:140
  86.8 0.1 copy.8
  86.9 1.6 slice.41
  88.4 0.1 copy.7
  88.5 0.0 copy-done.1
  88.6 0.1 select_reduce_fusion
  88.7 0.0 copy-done.2
  88.7 0.5 slice_bitcast_fusion.1.slot_ref
  89.2 0.0 copy-done.3
  89.2 0.1 clamp_select_fusion
  89.3 0.1 broadcast_bitcast_fusion
  89.4 1.9 %gather_fusion.1 = bf16[4,2,128,640]{3,2,1,0:T(8,128)(2,1)} fusion(bf16[5,2,128,640]{3,2,1,0:T(8,128)(2,1)S(1)} %slice.41, s32[1024]{0:T(1024)S(1)} %pad_clamp_fusion), kind=kCustom, calls=%fused_computation.1 | custom fusion | bytes 2621456 | tf_op jit(solution)/shard_map/jit(_take)/gather | solution.py:137
  91.2 39.6 %all-to-all-done.1.refs_2_.refs_3_.refs_4_.refs_5_.refs_8_.refs_9_.refs_10_.refs_11_ = bf16[4,2,128,1920]{3,2,1,0:T(8,128)(2,1)} async-done(((bf16[4,2,128,1920]{3,2,1,0:T(8,128)(2,1)}), bf16[4,2,128,1920]{3,2,1,0:T(8,128)(2,1)}, u32[]{:S(2)}, u32[]{:S(2)}) %all-to-all-start.1) | async-done | bytes 3932192 | tf_op jit(solution)/shard_map/all_to_all | solution.py:140
  130.9 3.7 %all-to-all-start.2 = ((bf16[4,2,128,640]{3,2,1,0:T(8,128)(2,1)}), bf16[4,2,128,640]{3,2,1,0:T(8,128)(2,1)S(1)}, u32[]{:S(2)}, u32[]{:S(2)}) async-start(bf16[4,2,128,640]{3,2,1,0:T(8,128)(2,1)} %gather_fusion.1), calls=%async_computation.2 | async-start | bytes 2621440 | tf_op jit(solution)/shard_map/all_to_all | solution.py:140
  134.6 1.3 broadcast_in_dim.58
  135.9 14.9 %shard_map.64 = bf16[512,1920]{1,0:T(8,128)(2,1)} custom-call(s32[2]{0:T(128)} %slice_bitcast_fusion.1.slot_ref, f32[512,768]{1,0:T(8,128)} %bitcast.37, bf16[512,2560]{1,0:T(8,128)(2,1)} %bitcast.39, bf16[4,2,128,2560]{3,2,1,0:T(8,128)(2,1)} %all-to-all-done.refs_0_.refs_1_.refs_6_.refs_7_, ...), custom_call_target="tpu_custom_call" | custom-call | flops 3019898880 | bytes 11403264 | tf_op jit(solution)/shard_map/pallas_call | solution.py:80
  150.7 0.0 all-gather.2.cloned.1.call-done
  150.8 10.3 %fusion = f32[512,2560]{1,0:T(8,128)} fusion(bf16[512,1920]{1,0:T(8,128)(2,1)} %shard_map.64, bf16[2560,2560]{1,0:T(8,128)(2,1)} %all-gather.2.cloned.1.call-done), kind=kOutput, calls=%fused_computation.3 | convolution fusion | flops 5033164800 | bytes 17039360 | tf_op jit(solution)/shard_map/dot_general | solution.py:144
  161.1 0.0 all-to-all-done.2.refs_2_.refs_3_.refs_4_.refs_5_.refs_8_.refs_9_.refs_10_.refs_11_
  161.1 0.0 copy-start
  161.1 1.1 copy-done
  162.2 7.3 %shard_map.65 = bf16[512,640]{1,0:T(8,128)(2,1)} custom-call(s32[2]{0:T(128)} %slice_bitcast_fusion.1.slot_ref, f32[512,768]{1,0:T(8,128)} %bitcast.38, bf16[512,2560]{1,0:T(8,128)(2,1)} %bitcast.40, bf16[4,2,128,2560]{3,2,1,0:T(8,128)(2,1)} %all-to-all-done.refs_0_.refs_1_.refs_6_.refs_7_, ...), custom_call_target="tpu_custom_call" | custom-call | flops 1006632960 | bytes 4849664 | tf_op jit(solution)/shard_map/pallas_call | solution.py:80
  169.4 7.4 %fusion.2 = bf16[1,512,2560]{2,1,0:T(8,128)(2,1)} fusion(f32[512,2560]{1,0:T(8,128)} %fusion, bf16[512,640]{1,0:T(8,128)(2,1)} %shard_map.65, bf16[2560,2560]{1,0:T(8,128)(2,1)} %all-gather.2.cloned.1.call-done, f32[2560]{0:T(1024)S(1)} %reduce), kind=kOutput, calls=%fused_computation.6 | convolution fusion | flops 1681653760 | bytes 11806720 | tf_op jit(solution)/shard_map/dot_general | solution.py:144
  (7 shorter events, 0.1 us)
Async XLA Ops:
  6.5 144.2 %all-gather.2.cloned.1.call-start = ((), (), s32[]{:S(2)}) async-start(), calls=%async_computation.3 | async-start | bytes 14745600 | tf_op jit(solution)/shard_map/all_gather | solution.py:116
  8.1 6.5 %collective-permute-start.2 = (s32[12]{0:T(128)S(1)}, s32[12]{0:T(128)S(1)}, u32[]{:S(2)}, u32[]{:S(2)}) collective-permute-start(s32[12]{0:T(128)S(1)} %reshape.177), channel_id=1, source_target_pairs={{0,24},{8,0},{16,8},{24,16},{1,25},{9,1},{17,9},{25,17},{2,26},{10... | collective-permute-start | bytes 152 | tf_op jit(solution)/shard_map/ppermute | solution.py:120
  12.0 4.5 %collective-permute-start = (s32[12]{0:T(128)S(1)}, s32[12]{0:T(128)S(1)}, u32[]{:S(2)}, u32[]{:S(2)}) collective-permute-start(s32[12]{0:T(128)S(1)} %reshape.177), channel_id=1, source_target_pairs={{0,8},{8,16},{16,24},{24,0},{1,9},{9,17},{17,25},{25,1},{2,10},{10... | collective-permute-start | bytes 152 | tf_op jit(solution)/shard_map/ppermute | solution.py:120
  12.0 4.5 %collective-permute-start.1 = (s32[12]{0:T(128)S(1)}, s32[12]{0:T(128)S(1)}, u32[]{:S(2)}, u32[]{:S(2)}) collective-permute-start(s32[12]{0:T(128)S(1)} %reshape.177), channel_id=1, source_target_pairs={{0,16},{8,24},{16,0},{24,8},{1,17},{9,25},{17,1},{25,9},{2,18},{10... | collective-permute-start | bytes 152 | tf_op jit(solution)/shard_map/ppermute | solution.py:120
  19.3 62.6 %all-to-all-start = ((bf16[4,2,128,2560]{3,2,1,0:T(8,128)(2,1)}), bf16[4,2,128,2560]{3,2,1,0:T(8,128)(2,1)}, u32[]{:S(2)}, u32[]{:S(2)}) async-start(bf16[4,2,128,2560]{3,2,1,0:T(8,128)(2,1)} %broadcast_in_dim.61), calls=%async_computation | async-start | bytes 10485760 | tf_op jit(solution)/shard_map/all_to_all | solution.py:124
  35.9 52.7 %copy-start.1 = (f32[1,2560]{1,0:T(1,128)S(1)}, f32[1,2560]{1,0:T(1,128)}, u32[]{:S(2)}) copy-start(f32[1,2560]{1,0:T(1,128)} %param.11) | copy-start | bytes 30724
  35.9 52.8 %copy-start.2 = (s32[1,4,5]{2,1,0:T(4,128)S(1)}, s32[1,4,5]{2,1,0:T(4,128)}, u32[]{:S(2)}) copy-start(s32[1,4,5]{2,1,0:T(4,128)} %param.8) | copy-start | bytes 244
  35.9 53.4 %copy-start.3 = (s32[1,4]{1,0:T(1,128)S(1)}, s32[1,4]{1,0:T(1,128)}, u32[]{:S(2)}) copy-start(s32[1,4]{1,0:T(1,128)} %param.9) | copy-start | bytes 52
  82.0 48.9 %all-to-all-start.1 = ((bf16[4,2,128,1920]{3,2,1,0:T(8,128)(2,1)}), bf16[4,2,128,1920]{3,2,1,0:T(8,128)(2,1)}, u32[]{:S(2)}, u32[]{:S(2)}) async-start(bf16[4,2,128,1920]{3,2,1,0:T(8,128)(2,1)} %gather_fusion), calls=%async_computation.1 | async-start | bytes 7864320 | tf_op jit(solution)/shard_map/all_to_all | solution.py:140
  130.9 30.2 %all-to-all-start.2 = ((bf16[4,2,128,640]{3,2,1,0:T(8,128)(2,1)}), bf16[4,2,128,640]{3,2,1,0:T(8,128)(2,1)S(1)}, u32[]{:S(2)}, u32[]{:S(2)}) async-start(bf16[4,2,128,640]{3,2,1,0:T(8,128)(2,1)} %gather_fusion.1), calls=%async_computation.2 | async-start | bytes 2621440 | tf_op jit(solution)/shard_map/all_to_all | solution.py:140
  161.1 1.1 copy-start
Sparse Core Ops, SparseCore 0:
  9.0 123.7 all-gather.1

commit v14 on v13

--- a/solution.py
+++ b/solution.py
@@ -128,7 +128,7 @@
     asked_slot = jnp.minimum(jnp.maximum(asked, 0) // owners, blocks.shape[0] - 1)
     bias = visibility(block_ids, key_limit[0], owners, block_len)
     heads = width // HS
-    tail_heads = heads // 4 if heads % 20 == 0 else heads
+    tail_heads = heads * 2 // 5 if heads % 5 == 0 else heads
     bounds = [(0, heads - tail_heads), (heads - tail_heads, heads)]
     bounds = [(lo * HS, hi * HS) for lo, hi in bounds if hi > lo]
     projected = None

time: 184 us -> 177 us (0.962)
  waiting for transfers between devices: 88.4 us -> 77.5 us
    all_to_all x2, waiting for transfers between devices: 39.6 us -> 27.3 us  [shards(): lax.all_to_all(outgoing, 'seq', split_axis=0, concat_axis=0, tiled=True)]
  transfers between devices with their start and end apart: 7 -> 7, of which waited for: 3 -> 4; matrix products, arithmetic and copies ran while one was open for 18% -> 20% of each run, Pallas kernels for 8% -> 7%
where the time goes in v14:
time: 177 us; the launch traced here: 176 us
  waiting for transfers between devices  77.5 us (44%)
  local copies, waits for them, and re-layouts  23.4 us (13%)
  Pallas kernels  22.7 us (13%)
  matrix products  19 us (11%)
  starting transfers between devices  18.8 us (11%)
  between operations  13.5 us (8%)
    all_to_all x1, waiting for transfers between devices, shards(): lax.all_to_all(first, 'seq', split_axis=0, concat_axis=0, tiled=True)  47.1 us
    all_to_all x2, waiting for transfers between devices, shards(): lax.all_to_all(outgoing, 'seq', split_axis=0, concat_axis=0, tiled=True)  27.3 us
    pallas_call x2, Pallas kernels, attention(): pl.pallas_call(kernel, grid_spec=grid_spec, out_shape=jax.ShapeDtypeStruc...  22.7 us
    dot_general x2, matrix products, shards(): part = jnp.dot(mixed, weight[cols], preferred_element_type=jnp.float32)  19 us
    gather x2, local copies, waits for them, and re-layouts, shards(): outgoing = jnp.take(blocks[..., cols], asked_slot, axis=0, mode='clip')  8.44 us
    all_to_all x2, starting transfers between devices, shards(): lax.all_to_all(outgoing, 'seq', split_axis=0, concat_axis=0, tiled=True)  8.32 us
    slice x2, local copies, waits for them, and re-layouts, shards(): outgoing = jnp.take(blocks[..., cols], asked_slot, axis=0, mode='clip')  7.81 us
    all_to_all x1, starting transfers between devices, shards(): lax.all_to_all(first, 'seq', split_axis=0, concat_axis=0, tiled=True)  5.41 us
  transfers between devices with their start and end apart: 7, of which 4 were waited for; matrix products, arithmetic and copies ran while one was open for 20% of the time, Pallas kernels for 7%

profile of v14, /device:TPU:0, one launch (start us, length us, event | category | flops | bytes accessed | tf_op | source)
XLA Modules:
  0.0 176.1 jit_solution(3538906099487431356)
XLA Ops:
  6.5 0.0 all-gather.2.cloned.1.call-start
  6.5 0.7 all-gather.2.cloned.1.call-update
  7.3 0.8 add_select_fusion.1
  8.0 0.1 reshape.177
  8.1 3.9 %collective-permute-start.2 = (s32[12]{0:T(128)S(1)}, s32[12]{0:T(128)S(1)}, u32[]{:S(2)}, u32[]{:S(2)}) collective-permute-start(s32[12]{0:T(128)S(1)} %reshape.177), channel_id=1, source_target_pairs={{0,24},{8,0},{16,8},{24,16},{1,25},{9,1},{17,9},{25,17},{2,26},{10... | collective-permute-start | bytes 152 | tf_op jit(solution)/shard_map/ppermute | solution.py:120
  12.0 0.5 collective-permute-start.1
  12.5 0.6 collective-permute-start
  13.1 0.1 stack_reshape.3
  13.2 1.4 slice_bitcast_fusion
  14.6 0.0 collective-permute-done.2
  14.6 1.0 collective-permute-done.1
  15.6 1.4 collective-permute-done
  17.0 2.9 %broadcast_in_dim.61 = bf16[4,2,128,2560]{3,2,1,0:T(8,128)(2,1)} broadcast(bf16[2,128,2560]{2,1,0:T(8,128)(2,1)S(1)} %slice_bitcast_fusion), dimensions={1,2,3} | broadcast | bytes 6553600 | tf_op jit(solution)/shard_map/broadcast_in_dim | solution.py:122
  19.9 5.4 %all-to-all-start = ((bf16[4,2,128,2560]{3,2,1,0:T(8,128)(2,1)}), bf16[4,2,128,2560]{3,2,1,0:T(8,128)(2,1)}, u32[]{:S(2)}, u32[]{:S(2)}) async-start(bf16[4,2,128,2560]{3,2,1,0:T(8,128)(2,1)} %broadcast_in_dim.61), calls=%async_computation | async-start | bytes 10485760 | tf_op jit(solution)/shard_map/all_to_all | solution.py:124
  25.4 4.3 %slice.39 = bf16[5,2,128,1536]{3,2,1,0:T(8,128)(2,1)} slice(bf16[5,2,128,2560]{3,2,1,0:T(8,128)(2,1)} %bitcast.42), slice={[0:5], [0:2], [0:128], [0:1536]} | slice | bytes 7864320 | tf_op jit(solution)/shard_map/slice | solution.py:137
  29.7 0.6 scatter_custom_fusion
  30.3 0.1 select_reduce_fusion.1
  30.5 4.6 %gather_fusion = bf16[4,2,128,1536]{3,2,1,0:T(8,128)(2,1)} fusion(bf16[5,2,128,1536]{3,2,1,0:T(8,128)(2,1)} %slice.39, s32[1024]{0:T(1024)S(1)} %pad_clamp_fusion), kind=kCustom, calls=%fused_computation | custom fusion | bytes 6291472 | tf_op jit(solution)/shard_map/jit(_take)/gather | solution.py:137
  35.1 47.1 %all-to-all-done.refs_0_.refs_1_.refs_6_.refs_7_ = bf16[4,2,128,2560]{3,2,1,0:T(8,128)(2,1)} async-done(((bf16[4,2,128,2560]{3,2,1,0:T(8,128)(2,1)}), bf16[4,2,128,2560]{3,2,1,0:T(8,128)(2,1)}, u32[]{:S(2)}, u32[]{:S(2)}) %all-to-all-start) | async-done | bytes 5242912 | tf_op jit(solution)/shard_map/all_to_all | solution.py:124
  82.2 3.7 %all-to-all-start.1 = ((bf16[4,2,128,1536]{3,2,1,0:T(8,128)(2,1)}), bf16[4,2,128,1536]{3,2,1,0:T(8,128)(2,1)S(1)}, u32[]{:S(2)}, u32[]{:S(2)}) async-start(bf16[4,2,128,1536]{3,2,1,0:T(8,128)(2,1)} %gather_fusion), calls=%async_computation.1 | async-start | bytes 6291456 | tf_op jit(solution)/shard_map/all_to_all | solution.py:140
  85.9 0.0 copy-start.1
  85.9 0.0 copy-start.2
  86.0 0.0 copy-start.3
  86.0 0.1 copy.8
  86.1 3.5 %slice.41 = bf16[5,2,128,1024]{3,2,1,0:T(8,128)(2,1)} slice(bf16[5,2,128,2560]{3,2,1,0:T(8,128)(2,1)} %bitcast.43), slice={[0:5], [0:2], [0:128], [1536:2560]} | slice | bytes 5242880 | tf_op jit(solution)/shard_map/slice | solution.py:137
  89.5 0.1 copy.7
  89.6 0.0 copy-done.1
  89.7 0.1 select_reduce_fusion
  89.7 0.0 copy-done.2
  89.8 0.5 slice_bitcast_fusion.1.slot_ref
  90.3 0.0 copy-done.3
  90.3 0.1 clamp_select_fusion
  90.4 0.1 broadcast_bitcast_fusion
  90.4 3.8 %gather_fusion.1 = bf16[4,2,128,1024]{3,2,1,0:T(8,128)(2,1)} fusion(bf16[5,2,128,1024]{3,2,1,0:T(8,128)(2,1)} %slice.41, s32[1024]{0:T(1024)S(1)} %pad_clamp_fusion), kind=kCustom, calls=%fused_computation.1 | custom fusion | bytes 4194320 | tf_op jit(solution)/shard_map/jit(_take)/gather | solution.py:137
  94.3 27.3 %all-to-all-done.1.refs_2_.refs_3_.refs_4_.refs_5_.refs_8_.refs_9_.refs_10_.refs_11_ = bf16[4,2,128,1536]{3,2,1,0:T(8,128)(2,1)S(1)} async-done(((bf16[4,2,128,1536]{3,2,1,0:T(8,128)(2,1)}), bf16[4,2,128,1536]{3,2,1,0:T(8,128)(2,1)S(1)}, u32[]{:S(2)}, u32[]{:S(2)}) %all-to-all-start.1) | async-done | bytes 3145760 | tf_op jit(solution)/shard_map/all_to_all | solution.py:140
  121.5 0.0 copy-start
  121.5 4.6 %all-to-all-start.2 = ((bf16[4,2,128,1024]{3,2,1,0:T(8,128)(2,1)}), bf16[4,2,128,1024]{3,2,1,0:T(8,128)(2,1)}, u32[]{:S(2)}, u32[]{:S(2)}) async-start(bf16[4,2,128,1024]{3,2,1,0:T(8,128)(2,1)} %gather_fusion.1), calls=%async_computation.2 | async-start | bytes 4194304 | tf_op jit(solution)/shard_map/all_to_all | solution.py:140
  126.2 1.3 broadcast_in_dim.58
  127.4 0.0 copy-done
  127.4 12.9 %shard_map.64 = bf16[512,1536]{1,0:T(8,128)(2,1)} custom-call(s32[2]{0:T(128)} %slice_bitcast_fusion.1.slot_ref, f32[512,768]{1,0:T(8,128)} %bitcast.38, bf16[512,2560]{1,0:T(8,128)(2,1)} %bitcast.40, bf16[4,2,128,2560]{3,2,1,0:T(8,128)(2,1)} %all-to-all-done.refs_0_.refs_1_.refs_6_.refs_7_, ...), custom_call_target="tpu_custom_call" | custom-call | flops 2415919104 | bytes 9437184 | tf_op jit(solution)/shard_map/pallas_call | solution.py:80
  140.3 0.0 all-gather.2.cloned.1.call-done
  140.4 10.3 %fusion = f32[512,2560]{1,0:T(8,128)} fusion(bf16[512,1536]{1,0:T(8,128)(2,1)} %shard_map.64, bf16[2560,2560]{1,0:T(8,128)(2,1)} %all-gather.2.cloned.1.call-done), kind=kOutput, calls=%fused_computation.3 | convolution fusion | flops 4026531840 | bytes 14680064 | tf_op jit(solution)/shard_map/dot_general | solution.py:144
  150.7 0.0 all-to-all-done.2.refs_2_.refs_3_.refs_4_.refs_5_.refs_8_.refs_9_.refs_10_.refs_11_
  150.7 9.8 %shard_map.65 = bf16[512,1024]{1,0:T(8,128)(2,1)} custom-call(s32[2]{0:T(128)} %slice_bitcast_fusion.1.slot_ref, f32[512,768]{1,0:T(8,128)} %bitcast.39, bf16[512,2560]{1,0:T(8,128)(2,1)} %bitcast.41, bf16[4,2,128,2560]{3,2,1,0:T(8,128)(2,1)} %all-to-all-done.refs_0_.refs_1_.refs_6_.refs_7_, ...), custom_call_target="tpu_custom_call" | custom-call | flops 1610612736 | bytes 6815744 | tf_op jit(solution)/shard_map/pallas_call | solution.py:80
  160.5 8.7 %fusion.6 = bf16[1,512,2560]{2,1,0:T(8,128)(2,1)} fusion(f32[512,2560]{1,0:T(8,128)} %fusion, bf16[512,1024]{1,0:T(8,128)(2,1)} %shard_map.65, bf16[2560,2560]{1,0:T(8,128)(2,1)} %all-gather.2.cloned.1.call-done, f32[2560]{0:T(1024)S(1)} %reduce), kind=kOutput, calls=%fused_computation.8 | convolution fusion | flops 2688286720 | bytes 14166016 | tf_op jit(solution)/shard_map/dot_general | solution.py:144
  (7 shorter events, 0.1 us)
Async XLA Ops:
  6.5 133.8 %all-gather.2.cloned.1.call-start = ((), (), s32[]{:S(2)}) async-start(), calls=%async_computation.3 | async-start | bytes 14745600 | tf_op jit(solution)/shard_map/all_gather | solution.py:116
  8.1 6.5 %collective-permute-start.2 = (s32[12]{0:T(128)S(1)}, s32[12]{0:T(128)S(1)}, u32[]{:S(2)}, u32[]{:S(2)}) collective-permute-start(s32[12]{0:T(128)S(1)} %reshape.177), channel_id=1, source_target_pairs={{0,24},{8,0},{16,8},{24,16},{1,25},{9,1},{17,9},{25,17},{2,26},{10... | collective-permute-start | bytes 152 | tf_op jit(solution)/shard_map/ppermute | solution.py:120
  12.0 3.6 %collective-permute-start.1 = (s32[12]{0:T(128)S(1)}, s32[12]{0:T(128)S(1)}, u32[]{:S(2)}, u32[]{:S(2)}) collective-permute-start(s32[12]{0:T(128)S(1)} %reshape.177), channel_id=1, source_target_pairs={{0,16},{8,24},{16,0},{24,8},{1,17},{9,25},{17,1},{25,9},{2,18},{10... | collective-permute-start | bytes 152 | tf_op jit(solution)/shard_map/ppermute | solution.py:120
  12.5 4.5 %collective-permute-start = (s32[12]{0:T(128)S(1)}, s32[12]{0:T(128)S(1)}, u32[]{:S(2)}, u32[]{:S(2)}) collective-permute-start(s32[12]{0:T(128)S(1)} %reshape.177), channel_id=1, source_target_pairs={{0,8},{8,16},{16,24},{24,0},{1,9},{9,17},{17,25},{25,1},{2,10},{10... | collective-permute-start | bytes 152 | tf_op jit(solution)/shard_map/ppermute | solution.py:120
  19.9 62.3 %all-to-all-start = ((bf16[4,2,128,2560]{3,2,1,0:T(8,128)(2,1)}), bf16[4,2,128,2560]{3,2,1,0:T(8,128)(2,1)}, u32[]{:S(2)}, u32[]{:S(2)}) async-start(bf16[4,2,128,2560]{3,2,1,0:T(8,128)(2,1)} %broadcast_in_dim.61), calls=%async_computation | async-start | bytes 10485760 | tf_op jit(solution)/shard_map/all_to_all | solution.py:124
  82.2 39.3 %all-to-all-start.1 = ((bf16[4,2,128,1536]{3,2,1,0:T(8,128)(2,1)}), bf16[4,2,128,1536]{3,2,1,0:T(8,128)(2,1)S(1)}, u32[]{:S(2)}, u32[]{:S(2)}) async-start(bf16[4,2,128,1536]{3,2,1,0:T(8,128)(2,1)} %gather_fusion), calls=%async_computation.1 | async-start | bytes 6291456 | tf_op jit(solution)/shard_map/all_to_all | solution.py:140
  85.9 3.7 %copy-start.1 = (f32[1,2560]{1,0:T(1,128)S(1)}, f32[1,2560]{1,0:T(1,128)}, u32[]{:S(2)}) copy-start(f32[1,2560]{1,0:T(1,128)} %param.11) | copy-start | bytes 30724
  85.9 3.8 %copy-start.2 = (s32[1,4,5]{2,1,0:T(4,128)S(1)}, s32[1,4,5]{2,1,0:T(4,128)}, u32[]{:S(2)}) copy-start(s32[1,4,5]{2,1,0:T(4,128)} %param.8) | copy-start | bytes 244
  86.0 4.3 %copy-start.3 = (s32[1,4]{1,0:T(1,128)S(1)}, s32[1,4]{1,0:T(1,128)}, u32[]{:S(2)}) copy-start(s32[1,4]{1,0:T(1,128)} %param.9) | copy-start | bytes 52
  121.5 5.9 %copy-start = (bf16[4,2,128,1536]{3,2,1,0:T(8,128)(2,1)}, bf16[4,2,128,1536]{3,2,1,0:T(8,128)(2,1)S(1)}, u32[]{:S(2)}) copy-start(bf16[4,2,128,1536]{3,2,1,0:T(8,128)(2,1)S(1)} %all-to-all-done.1.refs_2_.refs_3_.refs_4_.refs_5_.refs_8_.refs_9_.refs_10_.refs_11_) | copy-start | bytes 9437188
  121.5 29.1 %all-to-all-start.2 = ((bf16[4,2,128,1024]{3,2,1,0:T(8,128)(2,1)}), bf16[4,2,128,1024]{3,2,1,0:T(8,128)(2,1)}, u32[]{:S(2)}, u32[]{:S(2)}) async-start(bf16[4,2,128,1024]{3,2,1,0:T(8,128)(2,1)} %gather_fusion.1), calls=%async_computation.2 | async-start | bytes 4194304 | tf_op jit(solution)/shard_map/all_to_all | solution.py:140
Sparse Core Ops, SparseCore 0:
  9.0 123.7 all-gather.1

commit v15 on v14

--- a/solution.py
+++ b/solution.py
@@ -120,7 +120,6 @@
         lists.append(lax.ppermute(window_ids, "seq", [(s, (s + shift) % owners) for s in range(owners)]))
     by_reader = jnp.stack(lists)
     first = jnp.broadcast_to(blocks[0][None], (owners,) + blocks.shape[1:])
-    by_reader, first = lax.optimization_barrier((by_reader, first))
     sink_pool = lax.all_to_all(first, "seq", split_axis=0, concat_axis=0, tiled=True)
     readers = (me - jnp.arange(owners, dtype=jnp.int32)) % owners
     readers_ids = jnp.zeros_like(by_reader).at[readers].set(by_reader)

time: 177 us -> 178 us (level)
    ppermute x3, waiting for transfers between devices: 2.38 us -> 50.8 us  [shards(): lax.ppermute(window_ids, 'seq', [(s, (s + shift) % owners) for s in range...]
    all_to_all x1, waiting for transfers between devices: 47.1 us -> 0.01 us  [shards(): lax.all_to_all(first, 'seq', split_axis=0, concat_axis=0, tiled=True)]
  transfers between devices with their start and end apart: 7 -> 7, of which waited for: 4 -> 3; matrix products, arithmetic and copies ran while one was open for 20% -> 20% of each run, Pallas kernels for 7% -> 7%
where the time goes in v15:
time: 178 us; the launch traced here: 177 us
  waiting for transfers between devices  79.1 us (44%)
  local copies, waits for them, and re-layouts  23.3 us (13%)
  Pallas kernels  22.7 us (13%)
  matrix products  19 us (11%)
  starting transfers between devices  18.5 us (10%)
  between operations  13.5 us (8%)
    ppermute x3, waiting for transfers between devices, shards(): lax.ppermute(window_ids, 'seq', [(s, (s + shift) % owners) for s in range...  50.8 us
    all_to_all x2, waiting for transfers between devices, shards(): lax.all_to_all(outgoing, 'seq', split_axis=0, concat_axis=0, tiled=True)  27.5 us
    pallas_call x2, Pallas kernels, attention(): pl.pallas_call(kernel, grid_spec=grid_spec, out_shape=jax.ShapeDtypeStruc...  22.7 us
    dot_general x2, matrix products, shards(): part = jnp.dot(mixed, weight[cols], preferred_element_type=jnp.float32)  19 us
    gather x2, local copies, waits for them, and re-layouts, shards(): outgoing = jnp.take(blocks[..., cols], asked_slot, axis=0, mode='clip')  8.53 us
    slice x2, local copies, waits for them, and re-layouts, shards(): outgoing = jnp.take(blocks[..., cols], asked_slot, axis=0, mode='clip')  8.4 us
    all_to_all x2, starting transfers between devices, shards(): lax.all_to_all(outgoing, 'seq', split_axis=0, concat_axis=0, tiled=True)  8.32 us
    all_to_all x1, starting transfers between devices, shards(): lax.all_to_all(first, 'seq', split_axis=0, concat_axis=0, tiled=True)  5.32 us
  transfers between devices with their start and end apart: 7, of which 3 were waited for; matrix products, arithmetic and copies ran while one was open for 20% of the time, Pallas kernels for 7%

profile of v15, /device:TPU:0, one launch (start us, length us, event | category | flops | bytes accessed | tf_op | source)
XLA Modules:
  0.0 177.1 jit_solution(10738257594481743972)
XLA Ops:
  6.5 0.0 all-gather.2.cloned.1.call-start
  6.5 0.7 all-gather.2.cloned.1.call-update
  7.3 1.4 slice_bitcast_fusion
  8.7 2.8 %broadcast_in_dim.62 = bf16[4,2,128,2560]{3,2,1,0:T(8,128)(2,1)} broadcast(bf16[2,128,2560]{2,1,0:T(8,128)(2,1)S(1)} %slice_bitcast_fusion), dimensions={1,2,3} | broadcast | bytes 6553600 | tf_op jit(solution)/shard_map/broadcast_in_dim | solution.py:122
  11.4 0.0 copy-start.2
  11.4 5.3 %all-to-all-start = ((bf16[4,2,128,2560]{3,2,1,0:T(8,128)(2,1)}), bf16[4,2,128,2560]{3,2,1,0:T(8,128)(2,1)}, u32[]{:S(2)}, u32[]{:S(2)}) async-start(bf16[4,2,128,2560]{3,2,1,0:T(8,128)(2,1)} %broadcast_in_dim.62), calls=%async_computation | async-start | bytes 10485760 | tf_op jit(solution)/shard_map/all_to_all | solution.py:123
  16.7 0.0 copy-done.2
  16.7 0.1 add_select_fusion.1
  16.8 0.1 reshape.177
  16.9 3.8 %collective-permute-start.2 = (s32[12]{0:T(128)S(1)}, s32[12]{0:T(128)S(1)}, u32[]{:S(2)}, u32[]{:S(2)}) collective-permute-start(s32[12]{0:T(128)S(1)} %reshape.177), channel_id=1, source_target_pairs={{0,24},{8,0},{16,8},{24,16},{1,25},{9,1},{17,9},{25,17},{2,26},{10... | collective-permute-start | bytes 152 | tf_op jit(solution)/shard_map/ppermute | solution.py:120
  20.7 0.5 collective-permute-start.1
  21.2 0.6 collective-permute-start
  21.8 0.1 stack_reshape.3
  21.9 4.9 %slice.39 = bf16[5,2,128,1536]{3,2,1,0:T(8,128)(2,1)} slice(bf16[5,2,128,2560]{3,2,1,0:T(8,128)(2,1)} %bitcast.42), slice={[0:5], [0:2], [0:128], [0:1536]} | slice | bytes 7864320 | tf_op jit(solution)/shard_map/slice | solution.py:136
  26.8 50.0 %collective-permute-done.2 = s32[12]{0:T(128)S(1)} collective-permute-done((s32[12]{0:T(128)S(1)}, s32[12]{0:T(128)S(1)}, u32[]{:S(2)}, u32[]{:S(2)}) %collective-permute-start.2) | collective-permute-done | bytes 80 | tf_op jit(solution)/shard_map/ppermute | solution.py:120
  76.8 0.0 collective-permute-done.1
  76.8 0.8 collective-permute-done
  77.6 0.6 scatter_custom_fusion
  78.2 0.1 select_reduce_fusion.1
  78.4 4.7 %gather_fusion = bf16[4,2,128,1536]{3,2,1,0:T(8,128)(2,1)} fusion(bf16[5,2,128,1536]{3,2,1,0:T(8,128)(2,1)} %slice.39, s32[1024]{0:T(1024)S(1)} %pad_clamp_fusion), kind=kCustom, calls=%fused_computation | custom fusion | bytes 6291472 | tf_op jit(solution)/shard_map/jit(_take)/gather | solution.py:136
  83.1 0.0 all-to-all-done.refs_0_.refs_1_.refs_6_.refs_7_
  83.1 3.7 %all-to-all-start.1 = ((bf16[4,2,128,1536]{3,2,1,0:T(8,128)(2,1)}), bf16[4,2,128,1536]{3,2,1,0:T(8,128)(2,1)S(1)}, u32[]{:S(2)}, u32[]{:S(2)}) async-start(bf16[4,2,128,1536]{3,2,1,0:T(8,128)(2,1)} %gather_fusion), calls=%async_computation.1 | async-start | bytes 6291456 | tf_op jit(solution)/shard_map/all_to_all | solution.py:139
  86.8 0.0 copy-start.1
  86.8 0.0 copy-start.3
  86.8 0.1 copy.8
  86.9 3.5 %slice.41 = bf16[5,2,128,1024]{3,2,1,0:T(8,128)(2,1)} slice(bf16[5,2,128,2560]{3,2,1,0:T(8,128)(2,1)} %bitcast.43), slice={[0:5], [0:2], [0:128], [1536:2560]} | slice | bytes 5242880 | tf_op jit(solution)/shard_map/slice | solution.py:136
  90.4 0.1 copy.7
  90.5 0.0 copy-done.1
  90.5 0.1 select_reduce_fusion
  90.6 0.5 slice_bitcast_fusion.1.slot_ref
  91.1 0.0 copy-done.3
  91.1 0.1 clamp_select_fusion
  91.2 0.1 broadcast_bitcast_fusion
  91.3 3.8 %gather_fusion.1 = bf16[4,2,128,1024]{3,2,1,0:T(8,128)(2,1)} fusion(bf16[5,2,128,1024]{3,2,1,0:T(8,128)(2,1)} %slice.41, s32[1024]{0:T(1024)S(1)} %pad_clamp_fusion), kind=kCustom, calls=%fused_computation.1 | custom fusion | bytes 4194320 | tf_op jit(solution)/shard_map/jit(_take)/gather | solution.py:136
  95.1 27.5 %all-to-all-done.1.refs_2_.refs_3_.refs_4_.refs_5_.refs_8_.refs_9_.refs_10_.refs_11_ = bf16[4,2,128,1536]{3,2,1,0:T(8,128)(2,1)S(1)} async-done(((bf16[4,2,128,1536]{3,2,1,0:T(8,128)(2,1)}), bf16[4,2,128,1536]{3,2,1,0:T(8,128)(2,1)S(1)}, u32[]{:S(2)}, u32[]{:S(2)}) %all-to-all-start.1) | async-done | bytes 3145760 | tf_op jit(solution)/shard_map/all_to_all | solution.py:139
  122.6 0.0 copy-start
  122.6 4.6 %all-to-all-start.2 = ((bf16[4,2,128,1024]{3,2,1,0:T(8,128)(2,1)}), bf16[4,2,128,1024]{3,2,1,0:T(8,128)(2,1)}, u32[]{:S(2)}, u32[]{:S(2)}) async-start(bf16[4,2,128,1024]{3,2,1,0:T(8,128)(2,1)} %gather_fusion.1), calls=%async_computation.2 | async-start | bytes 4194304 | tf_op jit(solution)/shard_map/all_to_all | solution.py:139
  127.3 1.3 broadcast_in_dim.58
  128.5 0.0 copy-done
  128.5 12.9 %shard_map.64 = bf16[512,1536]{1,0:T(8,128)(2,1)} custom-call(s32[2]{0:T(128)} %slice_bitcast_fusion.1.slot_ref, f32[512,768]{1,0:T(8,128)} %bitcast.38, bf16[512,2560]{1,0:T(8,128)(2,1)} %bitcast.40, bf16[4,2,128,2560]{3,2,1,0:T(8,128)(2,1)} %all-to-all-done.refs_0_.refs_1_.refs_6_.refs_7_, ...), custom_call_target="tpu_custom_call" | custom-call | flops 2415919104 | bytes 9437184 | tf_op jit(solution)/shard_map/pallas_call | solution.py:80
  141.4 0.0 all-gather.2.cloned.1.call-done
  141.4 10.3 %fusion = f32[512,2560]{1,0:T(8,128)} fusion(bf16[512,1536]{1,0:T(8,128)(2,1)} %shard_map.64, bf16[2560,2560]{1,0:T(8,128)(2,1)} %all-gather.2.cloned.1.call-done), kind=kOutput, calls=%fused_computation.3 | convolution fusion | flops 4026531840 | bytes 14680064 | tf_op jit(solution)/shard_map/dot_general | solution.py:143
  151.7 0.0 all-to-all-done.2.refs_2_.refs_3_.refs_4_.refs_5_.refs_8_.refs_9_.refs_10_.refs_11_
  151.7 9.8 %shard_map.65 = bf16[512,1024]{1,0:T(8,128)(2,1)} custom-call(s32[2]{0:T(128)} %slice_bitcast_fusion.1.slot_ref, f32[512,768]{1,0:T(8,128)} %bitcast.39, bf16[512,2560]{1,0:T(8,128)(2,1)} %bitcast.41, bf16[4,2,128,2560]{3,2,1,0:T(8,128)(2,1)} %all-to-all-done.refs_0_.refs_1_.refs_6_.refs_7_, ...), custom_call_target="tpu_custom_call" | custom-call | flops 1610612736 | bytes 6815744 | tf_op jit(solution)/shard_map/pallas_call | solution.py:80
  161.6 8.7 %fusion.6 = bf16[1,512,2560]{2,1,0:T(8,128)(2,1)} fusion(f32[512,2560]{1,0:T(8,128)} %fusion, bf16[512,1024]{1,0:T(8,128)(2,1)} %shard_map.65, bf16[2560,2560]{1,0:T(8,128)(2,1)} %all-gather.2.cloned.1.call-done, f32[2560]{0:T(1024)S(1)} %reduce), kind=kOutput, calls=%fused_computation.8 | convolution fusion | flops 2688286720 | bytes 14166016 | tf_op jit(solution)/shard_map/dot_general | solution.py:143
  (6 shorter events, 0.1 us)
Async XLA Ops:
  6.5 134.9 %all-gather.2.cloned.1.call-start = ((), (), s32[]{:S(2)}) async-start(), calls=%async_computation.3 | async-start | bytes 14745600 | tf_op jit(solution)/shard_map/all_gather | solution.py:116
  11.4 5.3 %copy-start.2 = (s32[1,4,5]{2,1,0:T(4,128)S(1)}, s32[1,4,5]{2,1,0:T(4,128)}, u32[]{:S(2)}) copy-start(s32[1,4,5]{2,1,0:T(4,128)} %param.8) | copy-start | bytes 244
  11.4 71.7 %all-to-all-start = ((bf16[4,2,128,2560]{3,2,1,0:T(8,128)(2,1)}), bf16[4,2,128,2560]{3,2,1,0:T(8,128)(2,1)}, u32[]{:S(2)}, u32[]{:S(2)}) async-start(bf16[4,2,128,2560]{3,2,1,0:T(8,128)(2,1)} %broadcast_in_dim.62), calls=%async_computation | async-start | bytes 10485760 | tf_op jit(solution)/shard_map/all_to_all | solution.py:123
  16.9 59.9 %collective-permute-start.2 = (s32[12]{0:T(128)S(1)}, s32[12]{0:T(128)S(1)}, u32[]{:S(2)}, u32[]{:S(2)}) collective-permute-start(s32[12]{0:T(128)S(1)} %reshape.177), channel_id=1, source_target_pairs={{0,24},{8,0},{16,8},{24,16},{1,25},{9,1},{17,9},{25,17},{2,26},{10... | collective-permute-start | bytes 152 | tf_op jit(solution)/shard_map/ppermute | solution.py:120
  20.7 56.1 %collective-permute-start.1 = (s32[12]{0:T(128)S(1)}, s32[12]{0:T(128)S(1)}, u32[]{:S(2)}, u32[]{:S(2)}) collective-permute-start(s32[12]{0:T(128)S(1)} %reshape.177), channel_id=1, source_target_pairs={{0,16},{8,24},{16,0},{24,8},{1,17},{9,25},{17,1},{25,9},{2,18},{10... | collective-permute-start | bytes 152 | tf_op jit(solution)/shard_map/ppermute | solution.py:120
  21.2 56.4 %collective-permute-start = (s32[12]{0:T(128)S(1)}, s32[12]{0:T(128)S(1)}, u32[]{:S(2)}, u32[]{:S(2)}) collective-permute-start(s32[12]{0:T(128)S(1)} %reshape.177), channel_id=1, source_target_pairs={{0,8},{8,16},{16,24},{24,0},{1,9},{9,17},{17,25},{25,1},{2,10},{10... | collective-permute-start | bytes 152 | tf_op jit(solution)/shard_map/ppermute | solution.py:120
  83.1 39.5 %all-to-all-start.1 = ((bf16[4,2,128,1536]{3,2,1,0:T(8,128)(2,1)}), bf16[4,2,128,1536]{3,2,1,0:T(8,128)(2,1)S(1)}, u32[]{:S(2)}, u32[]{:S(2)}) async-start(bf16[4,2,128,1536]{3,2,1,0:T(8,128)(2,1)} %gather_fusion), calls=%async_computation.1 | async-start | bytes 6291456 | tf_op jit(solution)/shard_map/all_to_all | solution.py:139
  86.8 3.7 %copy-start.1 = (f32[1,2560]{1,0:T(1,128)S(1)}, f32[1,2560]{1,0:T(1,128)}, u32[]{:S(2)}) copy-start(f32[1,2560]{1,0:T(1,128)} %param.11) | copy-start | bytes 30724
  86.8 4.3 %copy-start.3 = (s32[1,4]{1,0:T(1,128)S(1)}, s32[1,4]{1,0:T(1,128)}, u32[]{:S(2)}) copy-start(s32[1,4]{1,0:T(1,128)} %param.9) | copy-start | bytes 52
  122.6 5.9 %copy-start = (bf16[4,2,128,1536]{3,2,1,0:T(8,128)(2,1)}, bf16[4,2,128,1536]{3,2,1,0:T(8,128)(2,1)S(1)}, u32[]{:S(2)}) copy-start(bf16[4,2,128,1536]{3,2,1,0:T(8,128)(2,1)S(1)} %all-to-all-done.1.refs_2_.refs_3_.refs_4_.refs_5_.refs_8_.refs_9_.refs_10_.refs_11_) | copy-start | bytes 9437188
  122.6 29.1 %all-to-all-start.2 = ((bf16[4,2,128,1024]{3,2,1,0:T(8,128)(2,1)}), bf16[4,2,128,1024]{3,2,1,0:T(8,128)(2,1)}, u32[]{:S(2)}, u32[]{:S(2)}) async-start(bf16[4,2,128,1024]{3,2,1,0:T(8,128)(2,1)} %gather_fusion.1), calls=%async_computation.2 | async-start | bytes 4194304 | tf_op jit(solution)/shard_map/all_to_all | solution.py:139
Sparse Core Ops, SparseCore 0:
  9.0 123.7 all-gather.1

commit v16 on v12

--- a/solution.py
+++ b/solution.py
@@ -127,8 +127,8 @@
     picks = jnp.stack([asked_slot, jnp.zeros_like(asked_slot)], axis=1).reshape(-1)
     bias = visibility(block_ids, key_limit[0], owners, block_len)
     heads = width // HS
-    if heads % 10 == 0:
-        edges = [0, heads * 6 // 10, heads * 9 // 10, heads]
+    if heads % 20 == 0:
+        edges = [0, heads // 5, heads * 4 // 5, heads]
     else:
         edges = [0, heads]
     bounds = [(lo * HS, hi * HS) for lo, hi in zip(edges[:-1], edges[1:])]
@@ -137,7 +137,10 @@
         cols = slice(lo, hi)
         outgoing = jnp.take(blocks[..., cols], picks, axis=0, mode="clip")
         outgoing = outgoing.reshape(owners, 2, 2, block_len, hi - lo)
+        if lo > 0:
+            previous, outgoing = lax.optimization_barrier((previous, outgoing))
         arrived = lax.all_to_all(outgoing, "seq", split_axis=0, concat_axis=0, tiled=True)
+        previous = arrived
         if hi == bounds[-1][1] and projected is not None:
             projected, arrived = lax.optimization_barrier((projected, arrived))
         mixed = attention(block_ids[0, :NSINK], bias, queries[0], arrived, lo)

time: 184 us -> 174 us (0.946)
  waiting for transfers between devices: 82.4 us -> 74.5 us
    all_to_all x3, waiting for transfers between devices: 80.1 us -> 71.9 us  [shards(): lax.all_to_all(outgoing, 'seq', split_axis=0, concat_axis=0, tiled=True)]
    slice x3 -> x2, local copies, waits for them, and re-layouts: 7.14 us -> 6.28 us  [shards(): outgoing = jnp.take(blocks[..., cols], picks, axis=0, mode='clip')]
  transfers between devices with their start and end apart: 7 -> 7, of which waited for: 3 -> 4; matrix products, arithmetic and copies ran while one was open for 19% -> 19% of each run, Pallas kernels for 12% -> 11%
where the time goes in v16:
time: 174 us
  waiting for transfers between devices  74.5 us (43%)
  Pallas kernels  25.8 us (15%)
  local copies, waits for them, and re-layouts  21.2 us (12%)
  matrix products  19.1 us (11%)
  starting transfers between devices  17.8 us (10%)
  between operations  13.5 us (8%)
    all_to_all x3, waiting for transfers between devices, shards(): lax.all_to_all(outgoing, 'seq', split_axis=0, concat_axis=0, tiled=True)  71.9 us
    pallas_call x3, Pallas kernels, attention(): pl.pallas_call(kernel, grid_spec=grid_spec, out_shape=jax.ShapeDtypeStruc...  25.8 us
    dot_general x3, matrix products, shards(): part = jnp.dot(mixed, weight[cols], preferred_element_type=jnp.float32)  19.1 us
    all_to_all x3, starting transfers between devices, shards(): lax.all_to_all(outgoing, 'seq', split_axis=0, concat_axis=0, tiled=True)  12.8 us
    gather x3, local copies, waits for them, and re-layouts, shards(): outgoing = jnp.take(blocks[..., cols], picks, axis=0, mode='clip')  9.81 us
    slice x2, local copies, waits for them, and re-layouts, shards(): outgoing = jnp.take(blocks[..., cols], picks, axis=0, mode='clip')  6.28 us
    ppermute x3, starting transfers between devices, shards(): lax.ppermute(window_ids, 'seq', [(s, (s + shift) % owners) for s in range...  5.02 us
  transfers between devices with their start and end apart: 7, of which 4 were waited for; matrix products, arithmetic and copies ran while one was open for 19% of the time, Pallas kernels for 11%

profile of v16, /device:TPU:0, one launch (start us, length us, event | category | flops | bytes accessed | tf_op | source)
XLA Modules:
  0.0 173.5 jit_solution(3424800066945437071)
XLA Ops:
  6.5 0.0 all-gather.2.cloned.1.call-start
  6.5 0.7 all-gather.2.cloned.1.call-update
  7.3 0.8 add_select_fusion.1
  8.0 0.1 reshape.186
  8.1 3.9 %collective-permute-start.2 = (s32[12]{0:T(128)S(1)}, s32[12]{0:T(128)S(1)}, u32[]{:S(2)}, u32[]{:S(2)}) collective-permute-start(s32[12]{0:T(128)S(1)} %reshape.186), channel_id=1, source_target_pairs={{0,24},{8,0},{16,8},{24,16},{1,25},{9,1},{17,9},{25,17},{2,26},{10... | collective-permute-start | bytes 152 | tf_op jit(solution)/shard_map/ppermute | solution.py:121
  12.0 0.5 collective-permute-start.1
  12.5 0.6 collective-permute-start
  13.1 0.1 stack_reshape.3
  13.2 2.0 %fusion.21 = (bf16[5,2,128,512]{3,2,1,0:T(8,128)(2,1)S(1)}, bf16[5,2,128,512]{3,2,1,0:T(8,128)(2,1)S(1)}) fusion(bf16[5,2,128,2560]{3,2,1,0:T(8,128)(2,1)} %bitcast.47), kind=kLoop, calls=%fused_computation.48 | loop fusion | bytes 5242880 | tf_op jit(solution)/shard_map/slice | solution.py:138
  15.2 0.0 collective-permute-done.2
  15.2 0.4 collective-permute-done.1
  15.6 1.4 collective-permute-done
  17.0 0.6 scatter_custom_fusion
  17.6 0.1 select_reduce_fusion.1
  17.7 0.1 copy.12
  17.8 0.1 reshape.192
  17.9 2.0 %gather_fusion = bf16[8,2,128,512]{3,2,1,0:T(8,128)(2,1)} fusion(bf16[5,2,128,512]{3,2,1,0:T(8,128)(2,1)S(1)} %get-tuple-element.14, s32[1024]{0:T(1024)S(1)} %pad_clamp_fusion), kind=kCustom, calls=%fused_computation | custom fusion | bytes 4194336 | tf_op jit(solution)/shard_map/jit(_take)/gather | solution.py:138
  19.9 3.8 %all-to-all-start = ((bf16[4,2,2,128,512]{4,3,2,1,0:T(8,128)(2,1)}), bf16[4,2,2,128,512]{4,3,2,1,0:T(8,128)(2,1)S(1)}, u32[]{:S(2)}, u32[]{:S(2)}) async-start(bf16[4,2,2,128,512]{4,3,2,1,0:T(8,128)(2,1)} %bitcast.46), calls=%async_computation | async-start | bytes 4194304 | tf_op jit(solution)/shard_map/all_to_all | solution.py:142
  23.7 4.3 %slice.47 = bf16[5,2,128,1536]{3,2,1,0:T(8,128)(2,1)} slice(bf16[5,2,128,2560]{3,2,1,0:T(8,128)(2,1)} %bitcast.48), slice={[0:5], [0:2], [0:128], [512:2048]} | slice | bytes 7864320 | tf_op jit(solution)/shard_map/slice | solution.py:138
  28.0 5.8 %gather_fusion.1 = bf16[8,2,128,1536]{3,2,1,0:T(8,128)(2,1)} fusion(bf16[5,2,128,1536]{3,2,1,0:T(8,128)(2,1)} %slice.47, s32[1024]{0:T(1024)S(1)} %pad_clamp_fusion), kind=kCustom, calls=%fused_computation.1 | custom fusion | bytes 12582944 | tf_op jit(solution)/shard_map/jit(_take)/gather | solution.py:138
  33.8 13.2 %all-to-all-done.refs_0_.refs_1_.refs_2_.refs_3_.refs_4_.refs_5_.refs_6_.refs_7_.refs_8_.refs_9_.refs_10_.refs_11_ = bf16[4,2,2,128,512]{4,3,2,1,0:T(8,128)(2,1)S(1)} async-done(((bf16[4,2,2,128,512]{4,3,2,1,0:T(8,128)(2,1)}), bf16[4,2,2,128,512]{4,3,2,1,0:T(8,128)(2,1)S(1)}, u32[]{:S(2)}, u32[]{:S(2)}) %all-to-all-start) | async-done | bytes 2097184 | tf_op jit(solution)/shard_map/all_to_all | solution.py:142
  47.0 0.0 copy-start
  47.0 1.3 copy-done
  48.4 5.2 %all-to-all-start.1 = ((bf16[4,2,2,128,1536]{4,3,2,1,0:T(8,128)(2,1)}), bf16[4,2,2,128,1536]{4,3,2,1,0:T(8,128)(2,1)}, u32[]{:S(2)}, u32[]{:S(2)}) async-start(bf16[4,2,2,128,1536]{4,3,2,1,0:T(8,128)(2,1)} %bitcast.41), calls=%async_computation.1 | async-start | bytes 12582912 | tf_op jit(solution)/shard_map/all_to_all | solution.py:142
  53.6 0.1 copy.10
  53.7 0.1 copy.9
  53.8 0.0 copy-done.3
  53.8 0.1 select_reduce_fusion
  53.9 0.0 copy-done.4
  53.9 0.5 slice_bitcast_fusion.slot_ref
  54.4 0.0 copy-done.5
  54.5 0.1 clamp_select_fusion
  54.5 0.1 broadcast_bitcast_fusion
  54.6 2.1 %gather_fusion.2 = bf16[8,2,128,512]{3,2,1,0:T(8,128)(2,1)} fusion(bf16[5,2,128,512]{3,2,1,0:T(8,128)(2,1)S(1)} %get-tuple-element.13, s32[1024]{0:T(1024)S(1)} %pad_clamp_fusion), kind=kCustom, calls=%fused_computation.2 | custom fusion | bytes 4194336 | tf_op jit(solution)/shard_map/jit(_take)/gather | solution.py:138
  56.7 1.3 broadcast_in_dim.54
  58.0 6.4 %shard_map.64 = bf16[512,512]{1,0:T(8,128)(2,1)} custom-call(s32[2]{0:T(128)} %slice_bitcast_fusion.slot_ref, f32[512,768]{1,0:T(8,128)} %bitcast.38, bf16[512,2560]{1,0:T(8,128)(2,1)} %bitcast.42, bf16[4,2,2,128,512]{4,3,2,1,0:T(8,128)(2,1)} %copy-done, bf16[4,2,2,128,512]{4,3,2,1,0:T(8,128)(2,1)} %copy-done, bf16[4,2,2,128,512]{4,3,2,1,0:T(8,128)(2,1)} %copy-done, ...), custom_call_target="tpu_custom_call" | custom-call | flops 805306368 | bytes 4194304 | tf_op jit(solution)/shard_map/pallas_call | solution.py:81
  64.4 58.7 %all-to-all-done.1.refs_0_.refs_1_.refs_2_.refs_3_.refs_4_.refs_5_.refs_6_.refs_7_.refs_8_.refs_9_.refs_10_.refs_11_ = bf16[4,2,2,128,1536]{4,3,2,1,0:T(8,128)(2,1)} async-done(((bf16[4,2,2,128,1536]{4,3,2,1,0:T(8,128)(2,1)}), bf16[4,2,2,128,1536]{4,3,2,1,0:T(8,128)(2,1)}, u32[]{:S(2)}, u32[]{:S(2)}) %all-to-all-start.1) | async-done | bytes 6291488 | tf_op jit(solution)/shard_map/all_to_all | solution.py:142
  123.1 3.8 %all-to-all-start.2 = ((bf16[4,2,2,128,512]{4,3,2,1,0:T(8,128)(2,1)}), bf16[4,2,2,128,512]{4,3,2,1,0:T(8,128)(2,1)S(1)}, u32[]{:S(2)}, u32[]{:S(2)}) async-start(bf16[4,2,2,128,512]{4,3,2,1,0:T(8,128)(2,1)} %bitcast.45), calls=%async_computation.2 | async-start | bytes 4194304 | tf_op jit(solution)/shard_map/all_to_all | solution.py:142
  126.9 12.9 %shard_map.65 = bf16[512,1536]{1,0:T(8,128)(2,1)} custom-call(s32[2]{0:T(128)} %slice_bitcast_fusion.slot_ref, f32[512,768]{1,0:T(8,128)} %bitcast.39, bf16[512,2560]{1,0:T(8,128)(2,1)} %bitcast.43, bf16[4,2,2,128,1536]{4,3,2,1,0:T(8,128)(2,1)} %all-to-all-done.1.refs_0_.refs_1_.refs_2_.refs_3_.refs_4_.refs_5_.refs_6_.refs_7_.refs_8_.refs_9_.refs_10_.refs_11_, ...), custom_call_target="tpu_custom_call" | custom-call | flops 2415919104 | bytes 9437184 | tf_op jit(solution)/shard_map/pallas_call | solution.py:81
  139.8 0.0 copy-start.2
  139.8 0.0 all-gather.2.cloned.1.call-done
  139.9 7.1 %fusion = f32[512,2560]{1,0:T(8,128)S(1)} fusion(bf16[512,1536]{1,0:T(8,128)(2,1)} %shard_map.65, bf16[2560,2560]{1,0:T(8,128)(2,1)} %all-gather.2.cloned.1.call-done), kind=kOutput, calls=%fused_computation.4 | convolution fusion | flops 4026531840 | bytes 14680064 | tf_op jit(solution)/shard_map/dot_general | solution.py:147
  147.0 0.0 copy-done.2
  147.0 5.5 %convolution_add_fusion = f32[512,2560]{1,0:T(8,128)} fusion(f32[512,2560]{1,0:T(8,128)S(1)} %fusion, bf16[512,512]{1,0:T(8,128)(2,1)S(1)} %copy-done.2, bf16[2560,2560]{1,0:T(8,128)(2,1)} %all-gather.2.cloned.1.call-done), kind=kOutput, calls=%fused_computation.7 | convolution fusion | flops 1343488000 | bytes 13631488 | tf_op jit(solution)/shard_map/dot_general | solution.py:147
  152.5 0.0 all-to-all-done.2.refs_0_.refs_1_.refs_2_.refs_3_.refs_4_.refs_5_.refs_6_.refs_7_.refs_8_.refs_9_.refs_10_.refs_11_
  152.5 1.3 copy-done.1
  153.8 6.4 %shard_map.66 = bf16[512,512]{1,0:T(8,128)(2,1)} custom-call(s32[2]{0:T(128)} %slice_bitcast_fusion.slot_ref, f32[512,768]{1,0:T(8,128)} %bitcast.40, bf16[512,2560]{1,0:T(8,128)(2,1)} %bitcast.44, bf16[4,2,2,128,512]{4,3,2,1,0:T(8,128)(2,1)} %copy-done.1, bf16[4,2,2,128,512]{4,3,2,1,0:T(8,128)(2,1)} %copy-done.1, bf16[4,2,2,128,512]{4,3,2,1,0:T(8,128)(2,1)} %copy-done.1, ...), custom_call_target="tpu_custom_call" | custom-call | flops 805306368 | bytes 4194304 | tf_op jit(solution)/shard_map/pallas_call | solution.py:81
  160.2 6.5 %fusion.2 = bf16[1,512,2560]{2,1,0:T(8,128)(2,1)} fusion(f32[512,2560]{1,0:T(8,128)} %convolution_add_fusion, bf16[512,512]{1,0:T(8,128)(2,1)} %shard_map.66, bf16[2560,2560]{1,0:T(8,128)(2,1)} %all-gather.2.cloned.1.call-done, f32[2560]{0:T(1024)S(1)} %reduce), kind=kOutput, calls=%fused_computation.8 | convolution fusion | flops 1346109440 | bytes 11020288 | tf_op jit(solution)/shard_map/dot_general | solution.py:147
  (11 shorter events, 0.1 us)
Async XLA Ops:
  6.5 133.3 %all-gather.2.cloned.1.call-start = ((), (), s32[]{:S(2)}) async-start(), calls=%async_computation.3 | async-start | bytes 14745600 | tf_op jit(solution)/shard_map/all_gather | solution.py:117
  8.1 7.1 %collective-permute-start.2 = (s32[12]{0:T(128)S(1)}, s32[12]{0:T(128)S(1)}, u32[]{:S(2)}, u32[]{:S(2)}) collective-permute-start(s32[12]{0:T(128)S(1)} %reshape.186), channel_id=1, source_target_pairs={{0,24},{8,0},{16,8},{24,16},{1,25},{9,1},{17,9},{25,17},{2,26},{10... | collective-permute-start | bytes 152 | tf_op jit(solution)/shard_map/ppermute | solution.py:121
  12.0 3.6 %collective-permute-start.1 = (s32[12]{0:T(128)S(1)}, s32[12]{0:T(128)S(1)}, u32[]{:S(2)}, u32[]{:S(2)}) collective-permute-start(s32[12]{0:T(128)S(1)} %reshape.186), channel_id=1, source_target_pairs={{0,16},{8,24},{16,0},{24,8},{1,17},{9,25},{17,1},{25,9},{2,18},{10... | collective-permute-start | bytes 152 | tf_op jit(solution)/shard_map/ppermute | solution.py:121
  12.5 4.5 %collective-permute-start = (s32[12]{0:T(128)S(1)}, s32[12]{0:T(128)S(1)}, u32[]{:S(2)}, u32[]{:S(2)}) collective-permute-start(s32[12]{0:T(128)S(1)} %reshape.186), channel_id=1, source_target_pairs={{0,8},{8,16},{16,24},{24,0},{1,9},{9,17},{17,25},{25,1},{2,10},{10... | collective-permute-start | bytes 152 | tf_op jit(solution)/shard_map/ppermute | solution.py:121
  19.9 27.1 %all-to-all-start = ((bf16[4,2,2,128,512]{4,3,2,1,0:T(8,128)(2,1)}), bf16[4,2,2,128,512]{4,3,2,1,0:T(8,128)(2,1)S(1)}, u32[]{:S(2)}, u32[]{:S(2)}) async-start(bf16[4,2,2,128,512]{4,3,2,1,0:T(8,128)(2,1)} %bitcast.46), calls=%async_computation | async-start | bytes 4194304 | tf_op jit(solution)/shard_map/all_to_all | solution.py:142
  47.0 1.3 copy-start
  47.0 6.8 %copy-start.3 = (f32[1,2560]{1,0:T(1,128)S(1)}, f32[1,2560]{1,0:T(1,128)}, u32[]{:S(2)}) copy-start(f32[1,2560]{1,0:T(1,128)} %param.11) | copy-start | bytes 30724
  47.0 6.9 %copy-start.4 = (s32[1,4,5]{2,1,0:T(4,128)S(1)}, s32[1,4,5]{2,1,0:T(4,128)}, u32[]{:S(2)}) copy-start(s32[1,4,5]{2,1,0:T(4,128)} %param.8) | copy-start | bytes 244
  47.0 7.4 %copy-start.5 = (s32[1,4]{1,0:T(1,128)S(1)}, s32[1,4]{1,0:T(1,128)}, u32[]{:S(2)}) copy-start(s32[1,4]{1,0:T(1,128)} %param.9) | copy-start | bytes 52
  48.4 74.7 %all-to-all-start.1 = ((bf16[4,2,2,128,1536]{4,3,2,1,0:T(8,128)(2,1)}), bf16[4,2,2,128,1536]{4,3,2,1,0:T(8,128)(2,1)}, u32[]{:S(2)}, u32[]{:S(2)}) async-start(bf16[4,2,2,128,1536]{4,3,2,1,0:T(8,128)(2,1)} %bitcast.41), calls=%async_computation.1 | async-start | bytes 12582912 | tf_op jit(solution)/shard_map/all_to_all | solution.py:142
  123.1 29.4 %all-to-all-start.2 = ((bf16[4,2,2,128,512]{4,3,2,1,0:T(8,128)(2,1)}), bf16[4,2,2,128,512]{4,3,2,1,0:T(8,128)(2,1)S(1)}, u32[]{:S(2)}, u32[]{:S(2)}) async-start(bf16[4,2,2,128,512]{4,3,2,1,0:T(8,128)(2,1)} %bitcast.45), calls=%async_computation.2 | async-start | bytes 4194304 | tf_op jit(solution)/shard_map/all_to_all | solution.py:142
  139.8 7.1 %copy-start.2 = (bf16[512,512]{1,0:T(8,128)(2,1)S(1)}, bf16[512,512]{1,0:T(8,128)(2,1)}, u32[]{:S(2)}) copy-start(bf16[512,512]{1,0:T(8,128)(2,1)} %shard_map.64) | copy-start | bytes 1572868
  152.5 1.3 copy-start.1
Sparse Core Ops, SparseCore 0:
  9.0 123.7 all-gather.1

commit v17 on v16

--- a/solution.py
+++ b/solution.py
@@ -19,7 +19,7 @@
     owners = arrived.shape[0]
     pooled = NSINK + owners
     heads = width // HS
-    group = next(g for g in GROUPS if heads % g == 0)
+    group = next(g for g in GROUPS if heads % g == 0 and (heads // g > 1 or g == 1))
     span = group * HS
     inv_scale = 1.0 / math.sqrt(HS)
 

time: 174 us -> 175 us (level)
  no operation moved by 1% of the time
where the time goes in v17:
time: 175 us; the launch traced here: 174 us
  waiting for transfers between devices  73.9 us (42%)
  Pallas kernels  27 us (15%)
  local copies, waits for them, and re-layouts  21.2 us (12%)
  matrix products  19.1 us (11%)
  starting transfers between devices  17.8 us (10%)
  between operations  13.5 us (8%)
    all_to_all x3, waiting for transfers between devices, shards(): lax.all_to_all(outgoing, 'seq', split_axis=0, concat_axis=0, tiled=True)  71.3 us
    pallas_call x3, Pallas kernels, attention(): pl.pallas_call(kernel, grid_spec=grid_spec, out_shape=jax.ShapeDtypeStruc...  27 us
    dot_general x3, matrix products, shards(): part = jnp.dot(mixed, weight[cols], preferred_element_type=jnp.float32)  19.1 us
    all_to_all x3, starting transfers between devices, shards(): lax.all_to_all(outgoing, 'seq', split_axis=0, concat_axis=0, tiled=True)  12.8 us
    gather x3, local copies, waits for them, and re-layouts, shards(): outgoing = jnp.take(blocks[..., cols], picks, axis=0, mode='clip')  9.81 us
    slice x2, local copies, waits for them, and re-layouts, shards(): outgoing = jnp.take(blocks[..., cols], picks, axis=0, mode='clip')  6.28 us
    ppermute x3, starting transfers between devices, shards(): lax.ppermute(window_ids, 'seq', [(s, (s + shift) % owners) for s in range...  5.02 us
  transfers between devices with their start and end apart: 7, of which 4 were waited for; matrix products, arithmetic and copies ran while one was open for 19% of the time, Pallas kernels for 11%

profile of v17, /device:TPU:0, one launch (start us, length us, event | category | flops | bytes accessed | tf_op | source)
XLA Modules:
  0.0 174.2 jit_solution(7341743662622276055)
XLA Ops:
  6.5 0.0 all-gather.2.cloned.1.call-start
  6.5 0.7 all-gather.2.cloned.1.call-update
  7.3 0.8 add_select_fusion.1
  8.0 0.1 reshape.186
  8.1 3.9 %collective-permute-start.2 = (s32[12]{0:T(128)S(1)}, s32[12]{0:T(128)S(1)}, u32[]{:S(2)}, u32[]{:S(2)}) collective-permute-start(s32[12]{0:T(128)S(1)} %reshape.186), channel_id=1, source_target_pairs={{0,24},{8,0},{16,8},{24,16},{1,25},{9,1},{17,9},{25,17},{2,26},{10... | collective-permute-start | bytes 152 | tf_op jit(solution)/shard_map/ppermute | solution.py:121
  12.0 0.5 collective-permute-start.1
  12.5 0.6 collective-permute-start
  13.1 0.1 stack_reshape.3
  13.2 2.0 %fusion.21 = (bf16[5,2,128,512]{3,2,1,0:T(8,128)(2,1)S(1)}, bf16[5,2,128,512]{3,2,1,0:T(8,128)(2,1)S(1)}) fusion(bf16[5,2,128,2560]{3,2,1,0:T(8,128)(2,1)} %bitcast.47), kind=kLoop, calls=%fused_computation.48 | loop fusion | bytes 5242880 | tf_op jit(solution)/shard_map/slice | solution.py:138
  15.2 0.0 collective-permute-done.2
  15.2 0.4 collective-permute-done.1
  15.6 1.4 collective-permute-done
  17.0 0.6 scatter_custom_fusion
  17.6 0.1 select_reduce_fusion.1
  17.7 0.1 copy.12
  17.8 0.1 reshape.192
  17.9 2.0 %gather_fusion = bf16[8,2,128,512]{3,2,1,0:T(8,128)(2,1)} fusion(bf16[5,2,128,512]{3,2,1,0:T(8,128)(2,1)S(1)} %get-tuple-element.14, s32[1024]{0:T(1024)S(1)} %pad_clamp_fusion), kind=kCustom, calls=%fused_computation | custom fusion | bytes 4194336 | tf_op jit(solution)/shard_map/jit(_take)/gather | solution.py:138
  19.9 3.8 %all-to-all-start = ((bf16[4,2,2,128,512]{4,3,2,1,0:T(8,128)(2,1)}), bf16[4,2,2,128,512]{4,3,2,1,0:T(8,128)(2,1)S(1)}, u32[]{:S(2)}, u32[]{:S(2)}) async-start(bf16[4,2,2,128,512]{4,3,2,1,0:T(8,128)(2,1)} %bitcast.46), calls=%async_computation | async-start | bytes 4194304 | tf_op jit(solution)/shard_map/all_to_all | solution.py:142
  23.7 4.3 %slice.47 = bf16[5,2,128,1536]{3,2,1,0:T(8,128)(2,1)} slice(bf16[5,2,128,2560]{3,2,1,0:T(8,128)(2,1)} %bitcast.48), slice={[0:5], [0:2], [0:128], [512:2048]} | slice | bytes 7864320 | tf_op jit(solution)/shard_map/slice | solution.py:138
  28.0 5.8 %gather_fusion.1 = bf16[8,2,128,1536]{3,2,1,0:T(8,128)(2,1)} fusion(bf16[5,2,128,1536]{3,2,1,0:T(8,128)(2,1)} %slice.47, s32[1024]{0:T(1024)S(1)} %pad_clamp_fusion), kind=kCustom, calls=%fused_computation.1 | custom fusion | bytes 12582944 | tf_op jit(solution)/shard_map/jit(_take)/gather | solution.py:138
  33.8 13.2 %all-to-all-done.refs_0_.refs_1_.refs_2_.refs_3_.refs_4_.refs_5_.refs_6_.refs_7_.refs_8_.refs_9_.refs_10_.refs_11_ = bf16[4,2,2,128,512]{4,3,2,1,0:T(8,128)(2,1)S(1)} async-done(((bf16[4,2,2,128,512]{4,3,2,1,0:T(8,128)(2,1)}), bf16[4,2,2,128,512]{4,3,2,1,0:T(8,128)(2,1)S(1)}, u32[]{:S(2)}, u32[]{:S(2)}) %all-to-all-start) | async-done | bytes 2097184 | tf_op jit(solution)/shard_map/all_to_all | solution.py:142
  47.0 0.0 copy-start
  47.0 1.3 copy-done
  48.4 5.2 %all-to-all-start.1 = ((bf16[4,2,2,128,1536]{4,3,2,1,0:T(8,128)(2,1)}), bf16[4,2,2,128,1536]{4,3,2,1,0:T(8,128)(2,1)}, u32[]{:S(2)}, u32[]{:S(2)}) async-start(bf16[4,2,2,128,1536]{4,3,2,1,0:T(8,128)(2,1)} %bitcast.41), calls=%async_computation.1 | async-start | bytes 12582912 | tf_op jit(solution)/shard_map/all_to_all | solution.py:142
  53.6 0.1 copy.10
  53.7 0.1 copy.9
  53.8 0.0 copy-done.3
  53.8 0.1 select_reduce_fusion
  53.9 0.0 copy-done.4
  53.9 0.5 slice_bitcast_fusion.slot_ref
  54.4 0.0 copy-done.5
  54.5 0.1 clamp_select_fusion
  54.5 0.1 broadcast_bitcast_fusion
  54.6 2.1 %gather_fusion.2 = bf16[8,2,128,512]{3,2,1,0:T(8,128)(2,1)} fusion(bf16[5,2,128,512]{3,2,1,0:T(8,128)(2,1)S(1)} %get-tuple-element.13, s32[1024]{0:T(1024)S(1)} %pad_clamp_fusion), kind=kCustom, calls=%fused_computation.2 | custom fusion | bytes 4194336 | tf_op jit(solution)/shard_map/jit(_take)/gather | solution.py:138
  56.7 1.3 broadcast_in_dim.54
  58.0 7.0 %shard_map.64 = bf16[512,512]{1,0:T(8,128)(2,1)} custom-call(s32[2]{0:T(128)} %slice_bitcast_fusion.slot_ref, f32[512,768]{1,0:T(8,128)} %bitcast.38, bf16[512,2560]{1,0:T(8,128)(2,1)} %bitcast.42, bf16[4,2,2,128,512]{4,3,2,1,0:T(8,128)(2,1)} %copy-done, bf16[4,2,2,128,512]{4,3,2,1,0:T(8,128)(2,1)} %copy-done, bf16[4,2,2,128,512]{4,3,2,1,0:T(8,128)(2,1)} %copy-done, ...), custom_call_target="tpu_custom_call" | custom-call | flops 805306368 | bytes 4194304 | tf_op jit(solution)/shard_map/pallas_call | solution.py:81
  65.0 58.1 %all-to-all-done.1.refs_0_.refs_1_.refs_2_.refs_3_.refs_4_.refs_5_.refs_6_.refs_7_.refs_8_.refs_9_.refs_10_.refs_11_ = bf16[4,2,2,128,1536]{4,3,2,1,0:T(8,128)(2,1)} async-done(((bf16[4,2,2,128,1536]{4,3,2,1,0:T(8,128)(2,1)}), bf16[4,2,2,128,1536]{4,3,2,1,0:T(8,128)(2,1)}, u32[]{:S(2)}, u32[]{:S(2)}) %all-to-all-start.1) | async-done | bytes 6291488 | tf_op jit(solution)/shard_map/all_to_all | solution.py:142
  123.1 3.8 %all-to-all-start.2 = ((bf16[4,2,2,128,512]{4,3,2,1,0:T(8,128)(2,1)}), bf16[4,2,2,128,512]{4,3,2,1,0:T(8,128)(2,1)S(1)}, u32[]{:S(2)}, u32[]{:S(2)}) async-start(bf16[4,2,2,128,512]{4,3,2,1,0:T(8,128)(2,1)} %bitcast.45), calls=%async_computation.2 | async-start | bytes 4194304 | tf_op jit(solution)/shard_map/all_to_all | solution.py:142
  126.9 12.9 %shard_map.65 = bf16[512,1536]{1,0:T(8,128)(2,1)} custom-call(s32[2]{0:T(128)} %slice_bitcast_fusion.slot_ref, f32[512,768]{1,0:T(8,128)} %bitcast.39, bf16[512,2560]{1,0:T(8,128)(2,1)} %bitcast.43, bf16[4,2,2,128,1536]{4,3,2,1,0:T(8,128)(2,1)} %all-to-all-done.1.refs_0_.refs_1_.refs_2_.refs_3_.refs_4_.refs_5_.refs_6_.refs_7_.refs_8_.refs_9_.refs_10_.refs_11_, ...), custom_call_target="tpu_custom_call" | custom-call | flops 2415919104 | bytes 9437184 | tf_op jit(solution)/shard_map/pallas_call | solution.py:81
  139.8 0.0 copy-start.2
  139.8 0.0 all-gather.2.cloned.1.call-done
  139.9 7.1 %fusion = f32[512,2560]{1,0:T(8,128)S(1)} fusion(bf16[512,1536]{1,0:T(8,128)(2,1)} %shard_map.65, bf16[2560,2560]{1,0:T(8,128)(2,1)} %all-gather.2.cloned.1.call-done), kind=kOutput, calls=%fused_computation.4 | convolution fusion | flops 4026531840 | bytes 14680064 | tf_op jit(solution)/shard_map/dot_general | solution.py:147
  147.0 0.0 copy-done.2
  147.0 5.5 %convolution_add_fusion = f32[512,2560]{1,0:T(8,128)} fusion(f32[512,2560]{1,0:T(8,128)S(1)} %fusion, bf16[512,512]{1,0:T(8,128)(2,1)S(1)} %copy-done.2, bf16[2560,2560]{1,0:T(8,128)(2,1)} %all-gather.2.cloned.1.call-done), kind=kOutput, calls=%fused_computation.7 | convolution fusion | flops 1343488000 | bytes 13631488 | tf_op jit(solution)/shard_map/dot_general | solution.py:147
  152.5 0.0 all-to-all-done.2.refs_0_.refs_1_.refs_2_.refs_3_.refs_4_.refs_5_.refs_6_.refs_7_.refs_8_.refs_9_.refs_10_.refs_11_
  152.5 1.3 copy-done.1
  153.8 7.1 %shard_map.66 = bf16[512,512]{1,0:T(8,128)(2,1)} custom-call(s32[2]{0:T(128)} %slice_bitcast_fusion.slot_ref, f32[512,768]{1,0:T(8,128)} %bitcast.40, bf16[512,2560]{1,0:T(8,128)(2,1)} %bitcast.44, bf16[4,2,2,128,512]{4,3,2,1,0:T(8,128)(2,1)} %copy-done.1, bf16[4,2,2,128,512]{4,3,2,1,0:T(8,128)(2,1)} %copy-done.1, bf16[4,2,2,128,512]{4,3,2,1,0:T(8,128)(2,1)} %copy-done.1, ...), custom_call_target="tpu_custom_call" | custom-call | flops 805306368 | bytes 4194304 | tf_op jit(solution)/shard_map/pallas_call | solution.py:81
  160.9 6.5 %fusion.2 = bf16[1,512,2560]{2,1,0:T(8,128)(2,1)} fusion(f32[512,2560]{1,0:T(8,128)} %convolution_add_fusion, bf16[512,512]{1,0:T(8,128)(2,1)} %shard_map.66, bf16[2560,2560]{1,0:T(8,128)(2,1)} %all-gather.2.cloned.1.call-done, f32[2560]{0:T(1024)S(1)} %reduce), kind=kOutput, calls=%fused_computation.8 | convolution fusion | flops 1346109440 | bytes 11020288 | tf_op jit(solution)/shard_map/dot_general | solution.py:147
  (11 shorter events, 0.1 us)
Async XLA Ops:
  6.5 133.3 %all-gather.2.cloned.1.call-start = ((), (), s32[]{:S(2)}) async-start(), calls=%async_computation.3 | async-start | bytes 14745600 | tf_op jit(solution)/shard_map/all_gather | solution.py:117
  8.1 7.1 %collective-permute-start.2 = (s32[12]{0:T(128)S(1)}, s32[12]{0:T(128)S(1)}, u32[]{:S(2)}, u32[]{:S(2)}) collective-permute-start(s32[12]{0:T(128)S(1)} %reshape.186), channel_id=1, source_target_pairs={{0,24},{8,0},{16,8},{24,16},{1,25},{9,1},{17,9},{25,17},{2,26},{10... | collective-permute-start | bytes 152 | tf_op jit(solution)/shard_map/ppermute | solution.py:121
  12.0 3.6 %collective-permute-start.1 = (s32[12]{0:T(128)S(1)}, s32[12]{0:T(128)S(1)}, u32[]{:S(2)}, u32[]{:S(2)}) collective-permute-start(s32[12]{0:T(128)S(1)} %reshape.186), channel_id=1, source_target_pairs={{0,16},{8,24},{16,0},{24,8},{1,17},{9,25},{17,1},{25,9},{2,18},{10... | collective-permute-start | bytes 152 | tf_op jit(solution)/shard_map/ppermute | solution.py:121
  12.5 4.5 %collective-permute-start = (s32[12]{0:T(128)S(1)}, s32[12]{0:T(128)S(1)}, u32[]{:S(2)}, u32[]{:S(2)}) collective-permute-start(s32[12]{0:T(128)S(1)} %reshape.186), channel_id=1, source_target_pairs={{0,8},{8,16},{16,24},{24,0},{1,9},{9,17},{17,25},{25,1},{2,10},{10... | collective-permute-start | bytes 152 | tf_op jit(solution)/shard_map/ppermute | solution.py:121
  19.9 27.1 %all-to-all-start = ((bf16[4,2,2,128,512]{4,3,2,1,0:T(8,128)(2,1)}), bf16[4,2,2,128,512]{4,3,2,1,0:T(8,128)(2,1)S(1)}, u32[]{:S(2)}, u32[]{:S(2)}) async-start(bf16[4,2,2,128,512]{4,3,2,1,0:T(8,128)(2,1)} %bitcast.46), calls=%async_computation | async-start | bytes 4194304 | tf_op jit(solution)/shard_map/all_to_all | solution.py:142
  47.0 1.3 copy-start
  47.0 6.8 %copy-start.3 = (f32[1,2560]{1,0:T(1,128)S(1)}, f32[1,2560]{1,0:T(1,128)}, u32[]{:S(2)}) copy-start(f32[1,2560]{1,0:T(1,128)} %param.11) | copy-start | bytes 30724
  47.0 6.9 %copy-start.4 = (s32[1,4,5]{2,1,0:T(4,128)S(1)}, s32[1,4,5]{2,1,0:T(4,128)}, u32[]{:S(2)}) copy-start(s32[1,4,5]{2,1,0:T(4,128)} %param.8) | copy-start | bytes 244
  47.0 7.4 %copy-start.5 = (s32[1,4]{1,0:T(1,128)S(1)}, s32[1,4]{1,0:T(1,128)}, u32[]{:S(2)}) copy-start(s32[1,4]{1,0:T(1,128)} %param.9) | copy-start | bytes 52
  48.4 74.7 %all-to-all-start.1 = ((bf16[4,2,2,128,1536]{4,3,2,1,0:T(8,128)(2,1)}), bf16[4,2,2,128,1536]{4,3,2,1,0:T(8,128)(2,1)}, u32[]{:S(2)}, u32[]{:S(2)}) async-start(bf16[4,2,2,128,1536]{4,3,2,1,0:T(8,128)(2,1)} %bitcast.41), calls=%async_computation.1 | async-start | bytes 12582912 | tf_op jit(solution)/shard_map/all_to_all | solution.py:142
  123.1 29.4 %all-to-all-start.2 = ((bf16[4,2,2,128,512]{4,3,2,1,0:T(8,128)(2,1)}), bf16[4,2,2,128,512]{4,3,2,1,0:T(8,128)(2,1)S(1)}, u32[]{:S(2)}, u32[]{:S(2)}) async-start(bf16[4,2,2,128,512]{4,3,2,1,0:T(8,128)(2,1)} %bitcast.45), calls=%async_computation.2 | async-start | bytes 4194304 | tf_op jit(solution)/shard_map/all_to_all | solution.py:142
  139.8 7.1 %copy-start.2 = (bf16[512,512]{1,0:T(8,128)(2,1)S(1)}, bf16[512,512]{1,0:T(8,128)(2,1)}, u32[]{:S(2)}) copy-start(bf16[512,512]{1,0:T(8,128)(2,1)} %shard_map.64) | copy-start | bytes 1572868
  152.5 1.3 copy-start.1
Sparse Core Ops, SparseCore 0:
  9.0 123.7 all-gather.1

commit v18 on v16

--- a/solution.py
+++ b/solution.py
@@ -128,7 +128,7 @@
     bias = visibility(block_ids, key_limit[0], owners, block_len)
     heads = width // HS
     if heads % 20 == 0:
-        edges = [0, heads // 5, heads * 4 // 5, heads]
+        edges = [0, heads // 10, heads * 4 // 5, heads]
     else:
         edges = [0, heads]
     bounds = [(lo * HS, hi * HS) for lo, hi in zip(edges[:-1], edges[1:])]

time: 174 us -> 177 us (1.017)
  Pallas kernels: 25.8 us -> 28.3 us
    pallas_call x3, Pallas kernels: 25.8 us -> 28.3 us  [attention(): pl.pallas_call(kernel, grid_spec=grid_spec, out_shape=jax.ShapeDtypeStruc...]
    slice x2 -> x3, local copies, waits for them, and re-layouts: 6.28 us -> 7.53 us  [shards(): outgoing = jnp.take(blocks[..., cols], picks, axis=0, mode='clip')]
  transfers between devices with their start and end apart: 7 -> 7, of which waited for: 4 -> 3; matrix products, arithmetic and copies ran while one was open for 19% -> 19% of each run, Pallas kernels for 11% -> 12%
where the time goes in v18:
time: 177 us
  waiting for transfers between devices  74.1 us (42%)
  Pallas kernels  28.3 us (16%)
  local copies, waits for them, and re-layouts  22.2 us (13%)
  matrix products  19 us (11%)
  starting transfers between devices  17.8 us (10%)
  between operations  13.5 us (8%)
    all_to_all x3, waiting for transfers between devices, shards(): lax.all_to_all(outgoing, 'seq', split_axis=0, concat_axis=0, tiled=True)  71.3 us
    pallas_call x3, Pallas kernels, attention(): pl.pallas_call(kernel, grid_spec=grid_spec, out_shape=jax.ShapeDtypeStruc...  28.3 us
    dot_general x3, matrix products, shards(): part = jnp.dot(mixed, weight[cols], preferred_element_type=jnp.float32)  19 us
    all_to_all x3, starting transfers between devices, shards(): lax.all_to_all(outgoing, 'seq', split_axis=0, concat_axis=0, tiled=True)  12.8 us
    gather x3, local copies, waits for them, and re-layouts, shards(): outgoing = jnp.take(blocks[..., cols], picks, axis=0, mode='clip')  9.86 us
    slice x3, local copies, waits for them, and re-layouts, shards(): outgoing = jnp.take(blocks[..., cols], picks, axis=0, mode='clip')  7.53 us
    ppermute x3, starting transfers between devices, shards(): lax.ppermute(window_ids, 'seq', [(s, (s + shift) % owners) for s in range...  5.02 us
  transfers between devices with their start and end apart: 7, of which 3 were waited for; matrix products, arithmetic and copies ran while one was open for 19% of the time, Pallas kernels for 12%

profile of v18, /device:TPU:0, one launch (start us, length us, event | category | flops | bytes accessed | tf_op | source)
XLA Modules:
  0.0 176.7 jit_solution(5246654040758015860)
XLA Ops:
  6.5 0.0 all-gather.2.cloned.1.call-start
  6.5 0.7 all-gather.2.cloned.1.call-update
  7.3 0.8 add_select_fusion.1
  8.0 0.1 reshape.186
  8.1 3.9 %collective-permute-start.2 = (s32[12]{0:T(128)S(1)}, s32[12]{0:T(128)S(1)}, u32[]{:S(2)}, u32[]{:S(2)}) collective-permute-start(s32[12]{0:T(128)S(1)} %reshape.186), channel_id=1, source_target_pairs={{0,24},{8,0},{16,8},{24,16},{1,25},{9,1},{17,9},{25,17},{2,26},{10... | collective-permute-start | bytes 152 | tf_op jit(solution)/shard_map/ppermute | solution.py:121
  12.0 0.0 collective-permute-start
  12.0 1.1 collective-permute-start.1
  13.1 0.1 stack_reshape.3
  13.2 1.1 slice.45
  14.4 0.0 collective-permute-done.2
  14.4 2.1 %collective-permute-done = s32[12]{0:T(128)S(1)} collective-permute-done((s32[12]{0:T(128)S(1)}, s32[12]{0:T(128)S(1)}, u32[]{:S(2)}, u32[]{:S(2)}) %collective-permute-start) | collective-permute-done | bytes 80 | tf_op jit(solution)/shard_map/ppermute | solution.py:121
  16.5 0.0 collective-permute-done.1
  16.5 0.6 scatter_custom_fusion
  17.1 0.1 select_reduce_fusion.1
  17.2 0.1 copy.12
  17.3 0.1 reshape.192
  17.4 1.6 gather_fusion
  19.0 3.5 %all-to-all-start = ((bf16[4,2,2,128,256]{4,3,2,1,0:T(8,128)(2,1)}), bf16[4,2,2,128,256]{4,3,2,1,0:T(8,128)(2,1)S(1)}, u32[]{:S(2)}, u32[]{:S(2)}) async-start(bf16[4,2,2,128,256]{4,3,2,1,0:T(8,128)(2,1)} %bitcast.13), calls=%async_computation | async-start | bytes 2097152 | tf_op jit(solution)/shard_map/all_to_all | solution.py:142
  22.6 5.0 %slice.47 = bf16[5,2,128,1792]{3,2,1,0:T(8,128)(2,1)} slice(bf16[5,2,128,2560]{3,2,1,0:T(8,128)(2,1)} %bitcast.46), slice={[0:5], [0:2], [0:128], [256:2048]} | slice | bytes 9175040 | tf_op jit(solution)/shard_map/slice | solution.py:138
  27.5 6.3 %gather_fusion.1 = bf16[8,2,128,1792]{3,2,1,0:T(8,128)(2,1)} fusion(bf16[5,2,128,1792]{3,2,1,0:T(8,128)(2,1)} %slice.47, s32[1024]{0:T(1024)S(1)} %pad_clamp_fusion), kind=kCustom, calls=%fused_computation.1 | custom fusion | bytes 14680096 | tf_op jit(solution)/shard_map/jit(_take)/gather | solution.py:138
  33.8 1.2 all-to-all-done.refs_0_.refs_1_.refs_2_.refs_3_.refs_4_.refs_5_.refs_6_.refs_7_.refs_8_.refs_9_.refs_10_.refs_11_
  35.0 1.0 copy-done.1
  36.1 5.5 %all-to-all-start.1 = ((bf16[4,2,2,128,1792]{4,3,2,1,0:T(8,128)(2,1)}), bf16[4,2,2,128,1792]{4,3,2,1,0:T(8,128)(2,1)}, u32[]{:S(2)}, u32[]{:S(2)}) async-start(bf16[4,2,2,128,1792]{4,3,2,1,0:T(8,128)(2,1)} %bitcast.37), calls=%async_computation.1 | async-start | bytes 14680064 | tf_op jit(solution)/shard_map/all_to_all | solution.py:142
  41.6 0.1 copy.10
  41.7 1.4 slice.49
  43.1 0.1 copy.9
  43.2 0.0 copy-done.3
  43.3 0.1 select_reduce_fusion
  43.3 0.0 copy-done.4
  43.3 0.5 slice_bitcast_fusion.slot_ref
  43.9 0.0 copy-done.5
  43.9 0.1 clamp_select_fusion
  44.0 0.1 broadcast_bitcast_fusion
  44.1 2.0 %gather_fusion.2 = bf16[8,2,128,512]{3,2,1,0:T(8,128)(2,1)} fusion(bf16[5,2,128,512]{3,2,1,0:T(8,128)(2,1)S(1)} %slice.49, s32[1024]{0:T(1024)S(1)} %pad_clamp_fusion), kind=kCustom, calls=%fused_computation.2 | custom fusion | bytes 4194336 | tf_op jit(solution)/shard_map/jit(_take)/gather | solution.py:138
  46.1 1.3 broadcast_in_dim.55
  47.3 4.9 %shard_map.64 = bf16[512,256]{1,0:T(8,128)(2,1)} custom-call(s32[2]{0:T(128)} %slice_bitcast_fusion.slot_ref, f32[512,768]{1,0:T(8,128)} %bitcast.38, bf16[512,2560]{1,0:T(8,128)(2,1)} %bitcast.41, bf16[4,2,2,128,256]{4,3,2,1,0:T(8,128)(2,1)} %copy-done.1, bf16[4,2,2,128,256]{4,3,2,1,0:T(8,128)(2,1)} %copy-done.1, bf16[4,2,2,128,256]{4,3,2,1,0:T(8,128)(2,1)} %copy-done.1, ...), custom_call_target="tpu_custom_call" | custom-call | flops 402653184 | bytes 2883584 | tf_op jit(solution)/shard_map/pallas_call | solution.py:81
  52.2 70.1 %all-to-all-done.1.refs_0_.refs_1_.refs_2_.refs_3_.refs_4_.refs_5_.refs_6_.refs_7_.refs_8_.refs_9_.refs_10_.refs_11_ = bf16[4,2,2,128,1792]{4,3,2,1,0:T(8,128)(2,1)} async-done(((bf16[4,2,2,128,1792]{4,3,2,1,0:T(8,128)(2,1)}), bf16[4,2,2,128,1792]{4,3,2,1,0:T(8,128)(2,1)}, u32[]{:S(2)}, u32[]{:S(2)}) %all-to-all-start.1) | async-done | bytes 7340064 | tf_op jit(solution)/shard_map/all_to_all | solution.py:142
  122.3 3.8 %all-to-all-start.2 = ((bf16[4,2,2,128,512]{4,3,2,1,0:T(8,128)(2,1)}), bf16[4,2,2,128,512]{4,3,2,1,0:T(8,128)(2,1)S(1)}, u32[]{:S(2)}, u32[]{:S(2)}) async-start(bf16[4,2,2,128,512]{4,3,2,1,0:T(8,128)(2,1)} %bitcast.44), calls=%async_computation.2 | async-start | bytes 4194304 | tf_op jit(solution)/shard_map/all_to_all | solution.py:142
  126.1 17.0 %shard_map.65 = bf16[512,1792]{1,0:T(8,128)(2,1)} custom-call(s32[2]{0:T(128)} %slice_bitcast_fusion.slot_ref, f32[512,768]{1,0:T(8,128)} %bitcast.39, bf16[512,2560]{1,0:T(8,128)(2,1)} %bitcast.42, bf16[4,2,2,128,1792]{4,3,2,1,0:T(8,128)(2,1)} %all-to-all-done.1.refs_0_.refs_1_.refs_2_.refs_3_.refs_4_.refs_5_.refs_6_.refs_7_.refs_8_.refs_9_.refs_10_.refs_11_, ...), custom_call_target="tpu_custom_call" | custom-call | flops 2818572288 | bytes 10747904 | tf_op jit(solution)/shard_map/pallas_call | solution.py:81
  143.0 0.0 copy-start.2
  143.0 0.0 all-gather.2.cloned.1.call-done
  143.1 8.0 %fusion = f32[512,2560]{1,0:T(8,128)S(1)} fusion(bf16[512,1792]{1,0:T(8,128)(2,1)} %shard_map.65, bf16[2560,2560]{1,0:T(8,128)(2,1)} %all-gather.2.cloned.1.call-done), kind=kOutput, calls=%fused_computation.4 | convolution fusion | flops 4697620480 | bytes 16252928 | tf_op jit(solution)/shard_map/dot_general | solution.py:147
  151.1 0.0 copy-done.2
  151.1 4.5 %convolution_add_fusion = f32[512,2560]{1,0:T(8,128)} fusion(f32[512,2560]{1,0:T(8,128)S(1)} %fusion, bf16[512,256]{1,0:T(8,128)(2,1)S(1)} %copy-done.2, bf16[2560,2560]{1,0:T(8,128)(2,1)} %all-gather.2.cloned.1.call-done), kind=kOutput, calls=%fused_computation.7 | convolution fusion | flops 672399360 | bytes 12058624 | tf_op jit(solution)/shard_map/dot_general | solution.py:147
  155.6 0.0 all-to-all-done.2.refs_0_.refs_1_.refs_2_.refs_3_.refs_4_.refs_5_.refs_6_.refs_7_.refs_8_.refs_9_.refs_10_.refs_11_
  155.6 1.3 copy-done
  157.0 6.4 %shard_map.66 = bf16[512,512]{1,0:T(8,128)(2,1)} custom-call(s32[2]{0:T(128)} %slice_bitcast_fusion.slot_ref, f32[512,768]{1,0:T(8,128)} %bitcast.40, bf16[512,2560]{1,0:T(8,128)(2,1)} %bitcast.43, bf16[4,2,2,128,512]{4,3,2,1,0:T(8,128)(2,1)} %copy-done, bf16[4,2,2,128,512]{4,3,2,1,0:T(8,128)(2,1)} %copy-done, bf16[4,2,2,128,512]{4,3,2,1,0:T(8,128)(2,1)} %copy-done, ...), custom_call_target="tpu_custom_call" | custom-call | flops 805306368 | bytes 4194304 | tf_op jit(solution)/shard_map/pallas_call | solution.py:81
  163.4 6.5 %fusion.2 = bf16[1,512,2560]{2,1,0:T(8,128)(2,1)} fusion(f32[512,2560]{1,0:T(8,128)} %convolution_add_fusion, bf16[512,512]{1,0:T(8,128)(2,1)} %shard_map.66, bf16[2560,2560]{1,0:T(8,128)(2,1)} %all-gather.2.cloned.1.call-done, f32[2560]{0:T(1024)S(1)} %reduce), kind=kOutput, calls=%fused_computation.8 | convolution fusion | flops 1346109440 | bytes 11020288 | tf_op jit(solution)/shard_map/dot_general | solution.py:147
  (12 shorter events, 0.1 us)
Async XLA Ops:
  6.5 136.5 %all-gather.2.cloned.1.call-start = ((), (), s32[]{:S(2)}) async-start(), calls=%async_computation.3 | async-start | bytes 14745600 | tf_op jit(solution)/shard_map/all_gather | solution.py:117
  8.1 6.3 %collective-permute-start.2 = (s32[12]{0:T(128)S(1)}, s32[12]{0:T(128)S(1)}, u32[]{:S(2)}, u32[]{:S(2)}) collective-permute-start(s32[12]{0:T(128)S(1)} %reshape.186), channel_id=1, source_target_pairs={{0,24},{8,0},{16,8},{24,16},{1,25},{9,1},{17,9},{25,17},{2,26},{10... | collective-permute-start | bytes 152 | tf_op jit(solution)/shard_map/ppermute | solution.py:121
  12.0 4.5 %collective-permute-start = (s32[12]{0:T(128)S(1)}, s32[12]{0:T(128)S(1)}, u32[]{:S(2)}, u32[]{:S(2)}) collective-permute-start(s32[12]{0:T(128)S(1)} %reshape.186), channel_id=1, source_target_pairs={{0,8},{8,16},{16,24},{24,0},{1,9},{9,17},{17,25},{25,1},{2,10},{10... | collective-permute-start | bytes 152 | tf_op jit(solution)/shard_map/ppermute | solution.py:121
  12.0 4.5 %collective-permute-start.1 = (s32[12]{0:T(128)S(1)}, s32[12]{0:T(128)S(1)}, u32[]{:S(2)}, u32[]{:S(2)}) collective-permute-start(s32[12]{0:T(128)S(1)} %reshape.186), channel_id=1, source_target_pairs={{0,16},{8,24},{16,0},{24,8},{1,17},{9,25},{17,1},{25,9},{2,18},{10... | collective-permute-start | bytes 152 | tf_op jit(solution)/shard_map/ppermute | solution.py:121
  19.0 16.0 %all-to-all-start = ((bf16[4,2,2,128,256]{4,3,2,1,0:T(8,128)(2,1)}), bf16[4,2,2,128,256]{4,3,2,1,0:T(8,128)(2,1)S(1)}, u32[]{:S(2)}, u32[]{:S(2)}) async-start(bf16[4,2,2,128,256]{4,3,2,1,0:T(8,128)(2,1)} %bitcast.13), calls=%async_computation | async-start | bytes 2097152 | tf_op jit(solution)/shard_map/all_to_all | solution.py:142
  35.0 1.0 copy-start.1
  35.0 8.2 %copy-start.3 = (f32[1,2560]{1,0:T(1,128)S(1)}, f32[1,2560]{1,0:T(1,128)}, u32[]{:S(2)}) copy-start(f32[1,2560]{1,0:T(1,128)} %param.11) | copy-start | bytes 30724
  35.0 8.3 %copy-start.4 = (s32[1,4,5]{2,1,0:T(4,128)S(1)}, s32[1,4,5]{2,1,0:T(4,128)}, u32[]{:S(2)}) copy-start(s32[1,4,5]{2,1,0:T(4,128)} %param.8) | copy-start | bytes 244
  35.0 8.9 %copy-start.5 = (s32[1,4]{1,0:T(1,128)S(1)}, s32[1,4]{1,0:T(1,128)}, u32[]{:S(2)}) copy-start(s32[1,4]{1,0:T(1,128)} %param.9) | copy-start | bytes 52
  36.1 86.2 %all-to-all-start.1 = ((bf16[4,2,2,128,1792]{4,3,2,1,0:T(8,128)(2,1)}), bf16[4,2,2,128,1792]{4,3,2,1,0:T(8,128)(2,1)}, u32[]{:S(2)}, u32[]{:S(2)}) async-start(bf16[4,2,2,128,1792]{4,3,2,1,0:T(8,128)(2,1)} %bitcast.37), calls=%async_computation.1 | async-start | bytes 14680064 | tf_op jit(solution)/shard_map/all_to_all | solution.py:142
  122.3 33.4 %all-to-all-start.2 = ((bf16[4,2,2,128,512]{4,3,2,1,0:T(8,128)(2,1)}), bf16[4,2,2,128,512]{4,3,2,1,0:T(8,128)(2,1)S(1)}, u32[]{:S(2)}, u32[]{:S(2)}) async-start(bf16[4,2,2,128,512]{4,3,2,1,0:T(8,128)(2,1)} %bitcast.44), calls=%async_computation.2 | async-start | bytes 4194304 | tf_op jit(solution)/shard_map/all_to_all | solution.py:142
  143.0 8.1 %copy-start.2 = (bf16[512,256]{1,0:T(8,128)(2,1)S(1)}, bf16[512,256]{1,0:T(8,128)(2,1)}, u32[]{:S(2)}) copy-start(bf16[512,256]{1,0:T(8,128)(2,1)} %shard_map.64) | copy-start | bytes 786436
  155.6 1.3 copy-start
Sparse Core Ops, SparseCore 0:
  9.0 123.7 all-gather.1

commit v19 on v16

--- a/solution.py
+++ b/solution.py
@@ -27,7 +27,7 @@
         key_refs = refs[:pooled]
         value_refs = refs[pooled : 2 * pooled]
         out_ref = refs[2 * pooled]
-        mask = bias_ref[...]
+        mask = bias_ref[...].astype(jnp.float32)
         for h in range(group):
             cols = slice(h * HS, (h + 1) * HS)
             keys = jnp.concatenate([r[:, cols] for r in key_refs], axis=0)
@@ -76,7 +76,7 @@
     cost = pl.CostEstimate(
         flops=4 * rows * keys_total * width,
         transcendentals=heads * rows * keys_total,
-        bytes_accessed=2 * rows * width * 2 + 2 * keys_total * width * 2 + rows * keys_total * 4,
+        bytes_accessed=2 * rows * width * 2 + 2 * keys_total * width * 2 + rows * keys_total * 2,
     )
     return pl.pallas_call(
         kernel,
@@ -99,7 +99,7 @@
     )
     lane = jnp.arange(block_len, dtype=jnp.int32)
     seen = lane[None, None, :] < visible[:, :, None]
-    bias = jnp.where(seen, 0.0, -jnp.inf).astype(jnp.float32)
+    bias = jnp.where(seen, 0.0, -jnp.inf).astype(jnp.bfloat16)
     bias = bias.reshape(tiles, 1, -1)
     return jnp.broadcast_to(bias, (tiles, block_len, bias.shape[-1])).reshape(
         tiles * block_len, -1

time: 174 us -> 174 us (level)
  no operation moved by 1% of the time
where the time goes in v19:
time: 174 us; the launch traced here: 173 us
  waiting for transfers between devices  75.1 us (43%)
  Pallas kernels  25 us (14%)
  local copies, waits for them, and re-layouts  20.8 us (12%)
  matrix products  19.1 us (11%)
  starting transfers between devices  17.8 us (10%)
  between operations  13.5 us (8%)
    all_to_all x3, waiting for transfers between devices, shards(): lax.all_to_all(outgoing, 'seq', split_axis=0, concat_axis=0, tiled=True)  72.6 us
    pallas_call x3, Pallas kernels, attention(): pl.pallas_call(kernel, grid_spec=grid_spec, out_shape=jax.ShapeDtypeStruc...  25 us
    dot_general x3, matrix products, shards(): part = jnp.dot(mixed, weight[cols], preferred_element_type=jnp.float32)  19.1 us
    all_to_all x3, starting transfers between devices, shards(): lax.all_to_all(outgoing, 'seq', split_axis=0, concat_axis=0, tiled=True)  12.8 us
    gather x3, local copies, waits for them, and re-layouts, shards(): outgoing = jnp.take(blocks[..., cols], picks, axis=0, mode='clip')  9.81 us
    slice x2, local copies, waits for them, and re-layouts, shards(): outgoing = jnp.take(blocks[..., cols], picks, axis=0, mode='clip')  6.28 us
    ppermute x3, starting transfers between devices, shards(): lax.ppermute(window_ids, 'seq', [(s, (s + shift) % owners) for s in range...  5.02 us
  transfers between devices with their start and end apart: 7, of which 4 were waited for; matrix products, arithmetic and copies ran while one was open for 19% of the time, Pallas kernels for 11%

profile of v19, /device:TPU:0, one launch (start us, length us, event | category | flops | bytes accessed | tf_op | source)
XLA Modules:
  0.0 173.0 jit_solution(8230104392976348361)
XLA Ops:
  6.5 0.0 all-gather.2.cloned.1.call-start
  6.5 0.7 all-gather.2.cloned.1.call-update
  7.3 0.8 add_select_fusion.1
  8.0 0.1 reshape.187
  8.1 3.9 %collective-permute-start.2 = (s32[12]{0:T(128)S(1)}, s32[12]{0:T(128)S(1)}, u32[]{:S(2)}, u32[]{:S(2)}) collective-permute-start(s32[12]{0:T(128)S(1)} %reshape.187), channel_id=1, source_target_pairs={{0,24},{8,0},{16,8},{24,16},{1,25},{9,1},{17,9},{25,17},{2,26},{10... | collective-permute-start | bytes 152 | tf_op jit(solution)/shard_map/ppermute | solution.py:121
  12.0 0.5 collective-permute-start.1
  12.5 0.6 collective-permute-start
  13.1 0.1 stack_reshape.3
  13.2 2.0 %fusion.20 = (bf16[5,2,128,512]{3,2,1,0:T(8,128)(2,1)S(1)}, bf16[5,2,128,512]{3,2,1,0:T(8,128)(2,1)S(1)}) fusion(bf16[5,2,128,2560]{3,2,1,0:T(8,128)(2,1)} %bitcast.47), kind=kLoop, calls=%fused_computation.48 | loop fusion | bytes 5242880 | tf_op jit(solution)/shard_map/slice | solution.py:138
  15.2 0.0 collective-permute-done.2
  15.2 0.4 collective-permute-done.1
  15.6 1.4 collective-permute-done
  17.0 0.6 scatter_custom_fusion
  17.6 0.1 select_reduce_fusion.1
  17.7 0.1 copy.12
  17.8 0.1 reshape.193
  17.9 2.0 %gather_fusion = bf16[8,2,128,512]{3,2,1,0:T(8,128)(2,1)} fusion(bf16[5,2,128,512]{3,2,1,0:T(8,128)(2,1)S(1)} %get-tuple-element.14, s32[1024]{0:T(1024)S(1)} %pad_clamp_fusion), kind=kCustom, calls=%fused_computation | custom fusion | bytes 4194336 | tf_op jit(solution)/shard_map/jit(_take)/gather | solution.py:138
  19.9 3.8 %all-to-all-start = ((bf16[4,2,2,128,512]{4,3,2,1,0:T(8,128)(2,1)}), bf16[4,2,2,128,512]{4,3,2,1,0:T(8,128)(2,1)S(1)}, u32[]{:S(2)}, u32[]{:S(2)}) async-start(bf16[4,2,2,128,512]{4,3,2,1,0:T(8,128)(2,1)} %bitcast.46), calls=%async_computation | async-start | bytes 4194304 | tf_op jit(solution)/shard_map/all_to_all | solution.py:142
  23.7 4.3 %slice.47 = bf16[5,2,128,1536]{3,2,1,0:T(8,128)(2,1)} slice(bf16[5,2,128,2560]{3,2,1,0:T(8,128)(2,1)} %bitcast.48), slice={[0:5], [0:2], [0:128], [512:2048]} | slice | bytes 7864320 | tf_op jit(solution)/shard_map/slice | solution.py:138
  28.0 5.8 %gather_fusion.1 = bf16[8,2,128,1536]{3,2,1,0:T(8,128)(2,1)} fusion(bf16[5,2,128,1536]{3,2,1,0:T(8,128)(2,1)} %slice.47, s32[1024]{0:T(1024)S(1)} %pad_clamp_fusion), kind=kCustom, calls=%fused_computation.1 | custom fusion | bytes 12582944 | tf_op jit(solution)/shard_map/jit(_take)/gather | solution.py:138
  33.8 13.2 %all-to-all-done.refs_0_.refs_1_.refs_2_.refs_3_.refs_4_.refs_5_.refs_6_.refs_7_.refs_8_.refs_9_.refs_10_.refs_11_ = bf16[4,2,2,128,512]{4,3,2,1,0:T(8,128)(2,1)S(1)} async-done(((bf16[4,2,2,128,512]{4,3,2,1,0:T(8,128)(2,1)}), bf16[4,2,2,128,512]{4,3,2,1,0:T(8,128)(2,1)S(1)}, u32[]{:S(2)}, u32[]{:S(2)}) %all-to-all-start) | async-done | bytes 2097184 | tf_op jit(solution)/shard_map/all_to_all | solution.py:142
  47.0 0.0 copy-start
  47.0 1.3 copy-done
  48.4 5.2 %all-to-all-start.1 = ((bf16[4,2,2,128,1536]{4,3,2,1,0:T(8,128)(2,1)}), bf16[4,2,2,128,1536]{4,3,2,1,0:T(8,128)(2,1)}, u32[]{:S(2)}, u32[]{:S(2)}) async-start(bf16[4,2,2,128,1536]{4,3,2,1,0:T(8,128)(2,1)} %bitcast.38), calls=%async_computation.1 | async-start | bytes 12582912 | tf_op jit(solution)/shard_map/all_to_all | solution.py:142
  53.6 0.1 copy.10
  53.7 0.1 copy.9
  53.8 0.0 copy-done.3
  53.8 0.1 select_reduce_fusion
  53.9 0.0 copy-done.4
  53.9 0.5 slice_bitcast_fusion.slot_ref
  54.4 0.0 copy-done.5
  54.4 0.1 clamp_select_fusion
  54.5 0.1 broadcast_bitcast_fusion
  54.6 2.1 %gather_fusion.2 = bf16[8,2,128,512]{3,2,1,0:T(8,128)(2,1)} fusion(bf16[5,2,128,512]{3,2,1,0:T(8,128)(2,1)S(1)} %get-tuple-element.13, s32[1024]{0:T(1024)S(1)} %pad_clamp_fusion), kind=kCustom, calls=%fused_computation.2 | custom fusion | bytes 4194336 | tf_op jit(solution)/shard_map/jit(_take)/gather | solution.py:138
  56.6 0.9 broadcast_in_dim.54
  57.6 6.2 %shard_map.64 = bf16[512,512]{1,0:T(8,128)(2,1)} custom-call(s32[2]{0:T(128)} %slice_bitcast_fusion.slot_ref, bf16[512,768]{1,0:T(8,128)(2,1)} %bitcast.42, bf16[512,2560]{1,0:T(8,128)(2,1)} %bitcast.39, bf16[4,2,2,128,512]{4,3,2,1,0:T(8,128)(2,1)} %copy-done, bf16[4,2,2,128,512]{4,3,2,1,0:T(8,128)(2,1)} %copy-done, bf16[4,2,2,128,512]{4,3,2,1,0:T(8,128)(2,1)} %copy-done, ...), custom_call_target="tpu_custom_call" | custom-call | flops 805306368 | bytes 3407872 | tf_op jit(solution)/shard_map/pallas_call | solution.py:81
  63.8 59.3 %all-to-all-done.1.refs_0_.refs_1_.refs_2_.refs_3_.refs_4_.refs_5_.refs_6_.refs_7_.refs_8_.refs_9_.refs_10_.refs_11_ = bf16[4,2,2,128,1536]{4,3,2,1,0:T(8,128)(2,1)} async-done(((bf16[4,2,2,128,1536]{4,3,2,1,0:T(8,128)(2,1)}), bf16[4,2,2,128,1536]{4,3,2,1,0:T(8,128)(2,1)}, u32[]{:S(2)}, u32[]{:S(2)}) %all-to-all-start.1) | async-done | bytes 6291488 | tf_op jit(solution)/shard_map/all_to_all | solution.py:142
  123.1 3.8 %all-to-all-start.2 = ((bf16[4,2,2,128,512]{4,3,2,1,0:T(8,128)(2,1)}), bf16[4,2,2,128,512]{4,3,2,1,0:T(8,128)(2,1)S(1)}, u32[]{:S(2)}, u32[]{:S(2)}) async-start(bf16[4,2,2,128,512]{4,3,2,1,0:T(8,128)(2,1)} %bitcast.45), calls=%async_computation.2 | async-start | bytes 4194304 | tf_op jit(solution)/shard_map/all_to_all | solution.py:142
  126.9 12.6 %shard_map.65 = bf16[512,1536]{1,0:T(8,128)(2,1)} custom-call(s32[2]{0:T(128)} %slice_bitcast_fusion.slot_ref, bf16[512,768]{1,0:T(8,128)(2,1)} %bitcast.43, bf16[512,2560]{1,0:T(8,128)(2,1)} %bitcast.40, bf16[4,2,2,128,1536]{4,3,2,1,0:T(8,128)(2,1)} %all-to-all-done.1.refs_0_.refs_1_.refs_2_.refs_3_.refs_4_.refs_5_.refs_6_.refs_7_.refs_8_.refs_9_.refs_10_.refs_11_, ...), custom_call_target="tpu_custom_call" | custom-call | flops 2415919104 | bytes 8650752 | tf_op jit(solution)/shard_map/pallas_call | solution.py:81
  139.5 0.0 copy-start.2
  139.6 0.0 all-gather.2.cloned.1.call-done
  139.6 7.1 %fusion = f32[512,2560]{1,0:T(8,128)S(1)} fusion(bf16[512,1536]{1,0:T(8,128)(2,1)} %shard_map.65, bf16[2560,2560]{1,0:T(8,128)(2,1)} %all-gather.2.cloned.1.call-done), kind=kOutput, calls=%fused_computation.4 | convolution fusion | flops 4026531840 | bytes 14680064 | tf_op jit(solution)/shard_map/dot_general | solution.py:147
  146.7 0.0 copy-done.2
  146.7 5.5 %convolution_add_fusion = f32[512,2560]{1,0:T(8,128)} fusion(f32[512,2560]{1,0:T(8,128)S(1)} %fusion, bf16[512,512]{1,0:T(8,128)(2,1)S(1)} %copy-done.2, bf16[2560,2560]{1,0:T(8,128)(2,1)} %all-gather.2.cloned.1.call-done), kind=kOutput, calls=%fused_computation.7 | convolution fusion | flops 1343488000 | bytes 13631488 | tf_op jit(solution)/shard_map/dot_general | solution.py:147
  152.2 0.0 all-to-all-done.2.refs_0_.refs_1_.refs_2_.refs_3_.refs_4_.refs_5_.refs_6_.refs_7_.refs_8_.refs_9_.refs_10_.refs_11_
  152.2 1.3 copy-done.1
  153.5 6.2 %shard_map.66 = bf16[512,512]{1,0:T(8,128)(2,1)} custom-call(s32[2]{0:T(128)} %slice_bitcast_fusion.slot_ref, bf16[512,768]{1,0:T(8,128)(2,1)} %bitcast.44, bf16[512,2560]{1,0:T(8,128)(2,1)} %bitcast.41, bf16[4,2,2,128,512]{4,3,2,1,0:T(8,128)(2,1)} %copy-done.1, bf16[4,2,2,128,512]{4,3,2,1,0:T(8,128)(2,1)} %copy-done.1, ...), custom_call_target="tpu_custom_call" | custom-call | flops 805306368 | bytes 3407872 | tf_op jit(solution)/shard_map/pallas_call | solution.py:81
  159.7 6.5 %fusion.2 = bf16[1,512,2560]{2,1,0:T(8,128)(2,1)} fusion(f32[512,2560]{1,0:T(8,128)} %convolution_add_fusion, bf16[512,512]{1,0:T(8,128)(2,1)} %shard_map.66, bf16[2560,2560]{1,0:T(8,128)(2,1)} %all-gather.2.cloned.1.call-done, f32[2560]{0:T(1024)S(1)} %reduce), kind=kOutput, calls=%fused_computation.8 | convolution fusion | flops 1346109440 | bytes 11020288 | tf_op jit(solution)/shard_map/dot_general | solution.py:147
  (11 shorter events, 0.1 us)
Async XLA Ops:
  6.5 133.0 %all-gather.2.cloned.1.call-start = ((), (), s32[]{:S(2)}) async-start(), calls=%async_computation.3 | async-start | bytes 14745600 | tf_op jit(solution)/shard_map/all_gather | solution.py:117
  8.1 7.1 %collective-permute-start.2 = (s32[12]{0:T(128)S(1)}, s32[12]{0:T(128)S(1)}, u32[]{:S(2)}, u32[]{:S(2)}) collective-permute-start(s32[12]{0:T(128)S(1)} %reshape.187), channel_id=1, source_target_pairs={{0,24},{8,0},{16,8},{24,16},{1,25},{9,1},{17,9},{25,17},{2,26},{10... | collective-permute-start | bytes 152 | tf_op jit(solution)/shard_map/ppermute | solution.py:121
  12.0 3.6 %collective-permute-start.1 = (s32[12]{0:T(128)S(1)}, s32[12]{0:T(128)S(1)}, u32[]{:S(2)}, u32[]{:S(2)}) collective-permute-start(s32[12]{0:T(128)S(1)} %reshape.187), channel_id=1, source_target_pairs={{0,16},{8,24},{16,0},{24,8},{1,17},{9,25},{17,1},{25,9},{2,18},{10... | collective-permute-start | bytes 152 | tf_op jit(solution)/shard_map/ppermute | solution.py:121
  12.5 4.5 %collective-permute-start = (s32[12]{0:T(128)S(1)}, s32[12]{0:T(128)S(1)}, u32[]{:S(2)}, u32[]{:S(2)}) collective-permute-start(s32[12]{0:T(128)S(1)} %reshape.187), channel_id=1, source_target_pairs={{0,8},{8,16},{16,24},{24,0},{1,9},{9,17},{17,25},{25,1},{2,10},{10... | collective-permute-start | bytes 152 | tf_op jit(solution)/shard_map/ppermute | solution.py:121
  19.9 27.1 %all-to-all-start = ((bf16[4,2,2,128,512]{4,3,2,1,0:T(8,128)(2,1)}), bf16[4,2,2,128,512]{4,3,2,1,0:T(8,128)(2,1)S(1)}, u32[]{:S(2)}, u32[]{:S(2)}) async-start(bf16[4,2,2,128,512]{4,3,2,1,0:T(8,128)(2,1)} %bitcast.46), calls=%async_computation | async-start | bytes 4194304 | tf_op jit(solution)/shard_map/all_to_all | solution.py:142
  47.0 1.3 copy-start
  47.0 6.8 %copy-start.3 = (f32[1,2560]{1,0:T(1,128)S(1)}, f32[1,2560]{1,0:T(1,128)}, u32[]{:S(2)}) copy-start(f32[1,2560]{1,0:T(1,128)} %param.11) | copy-start | bytes 30724
  47.0 6.9 %copy-start.4 = (s32[1,4,5]{2,1,0:T(4,128)S(1)}, s32[1,4,5]{2,1,0:T(4,128)}, u32[]{:S(2)}) copy-start(s32[1,4,5]{2,1,0:T(4,128)} %param.8) | copy-start | bytes 244
  47.0 7.4 %copy-start.5 = (s32[1,4]{1,0:T(1,128)S(1)}, s32[1,4]{1,0:T(1,128)}, u32[]{:S(2)}) copy-start(s32[1,4]{1,0:T(1,128)} %param.9) | copy-start | bytes 52
  48.4 74.7 %all-to-all-start.1 = ((bf16[4,2,2,128,1536]{4,3,2,1,0:T(8,128)(2,1)}), bf16[4,2,2,128,1536]{4,3,2,1,0:T(8,128)(2,1)}, u32[]{:S(2)}, u32[]{:S(2)}) async-start(bf16[4,2,2,128,1536]{4,3,2,1,0:T(8,128)(2,1)} %bitcast.38), calls=%async_computation.1 | async-start | bytes 12582912 | tf_op jit(solution)/shard_map/all_to_all | solution.py:142
  123.1 29.1 %all-to-all-start.2 = ((bf16[4,2,2,128,512]{4,3,2,1,0:T(8,128)(2,1)}), bf16[4,2,2,128,512]{4,3,2,1,0:T(8,128)(2,1)S(1)}, u32[]{:S(2)}, u32[]{:S(2)}) async-start(bf16[4,2,2,128,512]{4,3,2,1,0:T(8,128)(2,1)} %bitcast.45), calls=%async_computation.2 | async-start | bytes 4194304 | tf_op jit(solution)/shard_map/all_to_all | solution.py:142
  139.5 7.1 %copy-start.2 = (bf16[512,512]{1,0:T(8,128)(2,1)S(1)}, bf16[512,512]{1,0:T(8,128)(2,1)}, u32[]{:S(2)}) copy-start(bf16[512,512]{1,0:T(8,128)(2,1)} %shard_map.64) | copy-start | bytes 1572868
  152.2 1.3 copy-start.1
Sparse Core Ops, SparseCore 0:
  9.0 123.7 all-gather.1
